TPU v7x, 512 devices: a whole 4x8x8 slice. The times are simulated.
512 devices in a mesh: dp: 16 (over y, core), expert: 32 (over x, z).
Axes of the slice: x: 4, y: 8, z: 8, core: 2. Of those that a mesh axis runs over, the one named last changes fastest.
Arguments:
- tokens: bfloat16 [65536, 1024], P(('dp', 'expert')), may hold values from -6 to 6
- routes: int32 [65536, 4], P(('dp', 'expert')), may hold values from 0 to 31, all different within a row; in each aligned block of 128 rows (0 to 127, 128 to 255, ...) at most 32 rows name the same one
- gates: float32 [65536, 4], P(('dp', 'expert')), may hold values from 0.05 to 0.5
- w_in: bfloat16 [32, 1024, 768], P('expert', 'dp'), may hold values from -6 to 6
- w_down: bfloat16 [32, 384, 1024], P('expert', 'dp'), may hold values from -6 to 6
- out_grad: bfloat16 [65536, 1024], P(('dp', 'expert')), may hold values from -6 to 6
Outputs:
- moe_out: bfloat16 [65536, 1024], P(('dp', 'expert'))
- token_grad: bfloat16 [65536, 1024], P(('dp', 'expert'))
- new_w_in: bfloat16 [32, 1024, 768], P('expert', 'dp')
- new_w_down: bfloat16 [32, 384, 1024], P('expert', 'dp')
Inputs may be any that keep to these rules, and one draw needn't show every extreme that they name: `routes`: within one device's 128 tokens no expert is named more than 32 times, a bound that some block reaches; a token names 4 different experts.
All inputs are finite; a program needn't handle non-finite values.
Results may differ from a plain program's by a relative error of at most 0.014.
Values may be sent and summed in bfloat16 or wider, within the bound.
No kernel may reach another device: no remote copies, remote signals or barrier semaphores. Data moves between devices by JAX's collectives and lax.ppermute only.
A program may use at most 64 MiB of HBM per device.

v0:
```python
import jax
import jax.numpy as jnp
from jax import lax
from jax.sharding import PartitionSpec as P

step_rate = 0.5


def slot_numbers(route_rows, experts, capacity):
    flat_routes = route_rows.reshape(-1)
    one_hot = (flat_routes[:, None] == jnp.arange(experts, dtype=jnp.int32)[None, :]).astype(
        jnp.int32
    )
    running = jnp.cumsum(one_hot, axis=0)
    position = jnp.sum(one_hot * running, axis=1) - 1
    return flat_routes * capacity + position


def expert_forward(inputs, full_in, full_down):
    model_width = full_in.shape[1]
    hidden_units = full_down.shape[1]
    projected = jnp.einsum(
        "sxcd,xdj->sxcj", inputs, full_in, preferred_element_type=jnp.float32
    ) * model_width ** (-0.5)
    gate_part = projected[..., :hidden_units]
    up_part = projected[..., hidden_units:]
    activation = (jax.nn.silu(gate_part) * up_part).astype(jnp.bfloat16)
    results = (
        jnp.einsum("sxcf,xfd->sxcd", activation, full_down, preferred_element_type=jnp.float32)
        * hidden_units ** (-0.5)
    ).astype(jnp.bfloat16)
    return (projected, activation, results)


def expert_backward(projected, grad_rows, full_in, full_down):
    model_width = full_in.shape[1]
    hidden_units = full_down.shape[1]
    grad_act = jnp.einsum(
        "sxcd,xfd->sxcf", grad_rows, full_down, preferred_element_type=jnp.float32
    ) * hidden_units ** (-0.5)
    gate_part = projected[..., :hidden_units]
    up_part = projected[..., hidden_units:]
    sigmoid_gate = jax.nn.sigmoid(gate_part)
    grad_gate = grad_act * up_part * sigmoid_gate * (1.0 + gate_part * (1.0 - sigmoid_gate))
    grad_up = grad_act * jax.nn.silu(gate_part)
    grad_hidden = jnp.concatenate([grad_gate, grad_up], axis=-1).astype(jnp.bfloat16)
    grad_inputs = (
        jnp.einsum("sxcj,xdj->sxcd", grad_hidden, full_in, preferred_element_type=jnp.float32)
        * model_width ** (-0.5)
    ).astype(jnp.bfloat16)
    return (grad_hidden, grad_inputs)


def body(tokens, routes, gates, w_in, w_down, out_grad):
    tok_rows, model_width = tokens.shape
    top_count = routes.shape[1]
    per_device = w_in.shape[0]
    hidden_units = w_down.shape[2] and w_in.shape[2] // 2
    sources = lax.axis_size("expert")
    experts = per_device * sources
    capacity = min(tok_rows, 2 * tok_rows * top_count // experts)
    slot_index = slot_numbers(routes, experts, capacity)
    token_of = jnp.arange(tok_rows * top_count, dtype=jnp.int32) // top_count
    layout = (sources, per_device, capacity, model_width)
    send_inputs = (
        jnp.zeros((experts * capacity, model_width), jnp.bfloat16)
        .at[slot_index]
        .set(tokens[token_of])
        .reshape(layout)
    )
    scaled = (gates.reshape(-1)[:, None] * out_grad[token_of].astype(jnp.float32)).astype(
        jnp.bfloat16
    )
    send_grads = (
        jnp.zeros((experts * capacity, model_width), jnp.bfloat16)
        .at[slot_index]
        .set(scaled)
        .reshape(layout)
    )
    full_in, full_down = (
        lax.all_gather(w_in, "dp", axis=1, tiled=True),
        lax.all_gather(w_down, "dp", axis=1, tiled=True),
    )
    inputs_here = lax.all_to_all(send_inputs, "expert", split_axis=0, concat_axis=0, tiled=True)
    projected_here, activation_here, results_here = expert_forward(inputs_here, full_in, full_down)
    results_home = lax.all_to_all(results_here, "expert", split_axis=0, concat_axis=0, tiled=True)
    grad_rows = lax.all_to_all(send_grads, "expert", split_axis=0, concat_axis=0, tiled=True)
    grad_hidden, grad_inputs = expert_backward(projected_here, grad_rows, full_in, full_down)
    inputs_back = lax.all_to_all(grad_inputs, "expert", split_axis=0, concat_axis=0, tiled=True)
    picked = results_home.reshape(experts * capacity, model_width)[slot_index].astype(jnp.float32)
    picked = picked.reshape(tok_rows, top_count, model_width)
    moe_out = jnp.sum(picked * gates[:, :, None], axis=1).astype(jnp.bfloat16)
    back_rows = inputs_back.reshape(experts * capacity, model_width)[slot_index].astype(jnp.float32)
    token_grad = jnp.sum(back_rows.reshape(tok_rows, top_count, model_width), axis=1).astype(
        jnp.bfloat16
    )
    column_part = inputs_here
    summed_in = lax.psum_scatter(
        (
            jnp.einsum(
                "sxcd,sxcj->dxj", column_part, grad_hidden, preferred_element_type=jnp.float32
            )
            * model_width ** (-0.5)
        ).astype(jnp.bfloat16),
        "dp",
        scatter_dimension=0,
        tiled=True,
    ).astype(jnp.float32)
    column_part = activation_here
    summed_down = lax.psum_scatter(
        (
            jnp.einsum("sxcf,sxcd->fxd", column_part, grad_rows, preferred_element_type=jnp.float32)
            * hidden_units ** (-0.5)
        ).astype(jnp.bfloat16),
        "dp",
        scatter_dimension=0,
        tiled=True,
    ).astype(jnp.float32)
    new_w_in = (w_in.astype(jnp.float32) - step_rate * jnp.transpose(summed_in, (1, 0, 2))).astype(
        jnp.bfloat16
    )
    new_w_down = (
        w_down.astype(jnp.float32) - step_rate * jnp.transpose(summed_down, (1, 0, 2))
    ).astype(jnp.bfloat16)
    return (moe_out, token_grad, new_w_in, new_w_down)


def solution(mesh):
    return jax.shard_map(
        body,
        mesh=mesh,
        in_specs=(
            P(("dp", "expert"), None),
            P(("dp", "expert"), None),
            P(("dp", "expert"), None),
            P("expert", "dp", None),
            P("expert", "dp", None),
            P(("dp", "expert"), None),
        ),
        out_specs=(
            P(("dp", "expert"), None),
            P(("dp", "expert"), None),
            P("expert", "dp", None),
            P("expert", "dp", None),
        ),
        check_vma=False,
    )
```

profile of v0, /device:TPU:56, one launch (start us, length us, event | category | flops | bytes accessed | tf_op | source)
XLA Modules:
  0.0 367.4 jit_solution(6107741425047522396)
XLA Ops:
  10.8 7.7 %scatter_custom_fusion = bf16[1024,1024]{1,0:T(8,128)(2,1)} fusion(s32[512]{0:T(512)S(1)} %bitcast.146, bf16[128,1024]{1,0:T(8,128)(2,1)S(1)} %copy-done, s32[1024]{0:T(1024)S(1)} %pad_clamp_fusion.1, bf16[]{:T(256)} %constant.17.clone.1), kind=kCustom, calls=%fused_computation.41 | custom fusion | bytes 2097154 | tf_op jit(solution)/shard_map/scatter | solution.py:68
  18.5 13.5 %all-to-all-start = ((bf16[32,1,32,1024]{3,2,1,0:T(8,128)(2,1)}), bf16[32,1,32,1024]{3,2,1,0:T(8,128)(2,1)S(1)}, u32[]{:S(2)}, u32[]{:S(2)}) async-start(bf16[32,1,32,1024]{3,2,1,0:T(8,128)(2,1)} %bitcast.4), calls=%async_computation | async-start | bytes 4194304 | tf_op jit(solution)/shard_map/all_to_all | solution.py:84
  32.2 7.8 %scatter_custom_fusion.1 = bf16[1024,1024]{1,0:T(8,128)(2,1)} fusion(s32[512]{0:T(512)S(1)} %bitcast.147, f32[512]{0:T(512)S(1)} %mul.173, bf16[]{:T(256)} %constant.17.clone.1, bf16[128,1024]{1,0:T(8,128)(2,1)S(1)} %copy-done.3, s32[1024]{0:T(1024)S(1)} %pad_clamp_fusion.1), kind=kCustom, calls=%fused_computation.40 | custom fusion | flops 1572864 | bytes 2365442 | tf_op jit(solution)/shard_map/scatter | solution.py:77
  40.1 41.8 %all-to-all-done = bf16[32,1,32,1024]{3,2,1,0:T(8,128)(2,1)S(1)} async-done(((bf16[32,1,32,1024]{3,2,1,0:T(8,128)(2,1)}), bf16[32,1,32,1024]{3,2,1,0:T(8,128)(2,1)S(1)}, u32[]{:S(2)}, u32[]{:S(2)}) %all-to-all-start) | async-done | bytes 2097184 | tf_op jit(solution)/shard_map/all_to_all | solution.py:84
  81.9 6.4 %all-to-all-start.2 = ((bf16[32,1,32,1024]{3,2,1,0:T(8,128)(2,1)}), bf16[32,1,32,1024]{3,2,1,0:T(8,128)(2,1)}, u32[]{:S(2)}, u32[]{:S(2)}) async-start(bf16[32,1,32,1024]{3,2,1,0:T(8,128)(2,1)} %bitcast.21), calls=%async_computation.2 | async-start | bytes 4194304 | tf_op jit(solution)/shard_map/all_to_all | solution.py:87
  89.0 17.1 %all_gather.7 = bf16[1,384,1024]{2,1,0:T(8,128)(2,1)S(1)} all-gather(bf16[1,24,1024]{2,1,0:T(8,128)(2,1)S(1)} %copy-done.4), channel_id=1, replica_groups=mesh['dp'=16,'expert'=32] {'dp'}, dimensions={1}, use_global_device_ids=true | all-gather | bytes 835584 | tf_op jit(solution)/shard_map/all_gather | solution.py:82
  106.1 25.9 %all-gather.2.cloned.1.call-done = bf16[1,1024,768]{2,1,0:T(8,128)(2,1)} async-done(((bf16[1,64,768]{2,1,0:T(8,128)(2,1)}), bf16[1,1024,768]{2,1,0:T(8,128)(2,1)}) %all-gather.2.cloned.1.call-update) | async-done | bytes 1572880 | tf_op jit(solution)/shard_map/all_gather | solution.py:81
  132.0 4.9 %multiply_bitcast_fusion = f32[32,1,32,768]{3,2,0,1:T(8,128)} fusion(bf16[32,1,32,1024]{3,2,1,0:T(8,128)(2,1)S(1)} %all-to-all-done, bf16[1,1024,768]{2,1,0:T(8,128)(2,1)} %all-gather.2.cloned.1.call-done), kind=kOutput, calls=%fused_computation.10 | convolution fusion | flops 1611399168 | bytes 6815744 | tf_op jit(solution)/shard_map/sxcd,xdj->sxcj/dot_general | solution.py:22
  138.0 5.2 %fusion.44 = (bf16[32,32,384]{2,1,0:T(8,128)(2,1)S(1)}, bf16[32,32,384]{2,1,0:T(8,128)(2,1)S(1)}, bf16[32,32,384]{2,1,0:T(8,128)(2,1)}) fusion(f32[32,1,32,768]{3,2,0,1:T(8,128)} %multiply_bitcast_fusion, bf16[1,384,1024]{2,1,0:T(8,128)(2,1)S(1)} %all_gather.7, bf16[32,1,32,1024]{3,2,1,0:T(8,128)(2,1)} %all-to-all-done.2), kind=kOutput, calls=%fused_computation.50 | convolution fusion | flops 811597824 | bytes 8388608 | tf_op jit(solution)/shard_map/sxcd,xfd->sxcf/dot_general | solution.py:38
  144.4 3.2 fusion.14
  147.6 9.2 %all-to-all-start.3 = ((bf16[32,1,32,1024]{3,2,1,0:T(8,128)(2,1)}), bf16[32,1,32,1024]{3,2,1,0:T(8,128)(2,1)S(1)}, u32[]{:S(2)}, u32[]{:S(2)}) async-start(bf16[32,1,32,1024]{3,2,1,0:T(8,128)(2,1)} %fusion.14), calls=%async_computation.3 | async-start | bytes 4194304 | tf_op jit(solution)/shard_map/all_to_all | solution.py:89
  156.9 3.9 %fusion.31 = bf16[384,1,1024]{0,2,1:T(8,128)(2,1)} fusion(bf16[32,32,384]{2,1,0:T(8,128)(2,1)} %get-tuple-element.18, bf16[32,1,32,1024]{3,2,1,0:T(8,128)(2,1)} %all-to-all-done.2), kind=kOutput, calls=%fused_computation.39 | convolution fusion | flops 806092800 | bytes 3670016 | tf_op jit(solution)/shard_map/sxcf,sxcd->fxd/dot_general | solution.py:112
  160.8 4.8 %copy.43 = bf16[384,1,1024]{2,1,0:T(2,128)(2,1)} copy(bf16[384,1,1024]{0,2,1:T(8,128)(2,1)} %fusion.31) | data formatting | bytes 1572864 | tf_op jit(solution)/shard_map/convert_element_type | solution.py:114
  165.6 3.7 %fusion.13 = bf16[32,1,32,1024]{3,2,1,0:T(8,128)(2,1)} fusion(bf16[32,32,384]{2,1,0:T(8,128)(2,1)} %get-tuple-element.18, bf16[1,384,1024]{2,1,0:T(8,128)(2,1)S(1)} %all_gather.7), kind=kOutput, calls=%fused_computation.21 | convolution fusion | flops 807403520 | bytes 3670016 | tf_op jit(solution)/shard_map/sxcf,xfd->sxcd/dot_general | solution.py:29
  169.3 37.8 %all-to-all-done.3 = bf16[32,1,32,1024]{3,2,1,0:T(8,128)(2,1)S(1)} async-done(((bf16[32,1,32,1024]{3,2,1,0:T(8,128)(2,1)}), bf16[32,1,32,1024]{3,2,1,0:T(8,128)(2,1)S(1)}, u32[]{:S(2)}, u32[]{:S(2)}) %all-to-all-start.3) | async-done | bytes 2097184 | tf_op jit(solution)/shard_map/all_to_all | solution.py:89
  207.2 6.5 %all-to-all-start.1 = ((bf16[32,1,32,1024]{3,2,1,0:T(8,128)(2,1)}), bf16[32,1,32,1024]{3,2,1,0:T(8,128)(2,1)}, u32[]{:S(2)}, u32[]{:S(2)}) async-start(bf16[32,1,32,1024]{3,2,1,0:T(8,128)(2,1)} %fusion.13), calls=%async_computation.1 | async-start | bytes 4194304 | tf_op jit(solution)/shard_map/all_to_all | solution.py:86
  213.8 4.8 %fusion.23 = bf16[1024,768]{0,1:T(8,128)(2,1)} fusion(bf16[32,1,32,1024]{3,2,1,0:T(8,128)(2,1)} %copy-done.1, bf16[32,32,384]{2,1,0:T(8,128)(2,1)} %copy-done.9, bf16[32,32,384]{2,1,0:T(8,128)(2,1)S(1)} %copy-done.8), kind=kOutput, calls=%fused_computation.37 | convolution fusion | flops 1615331328 | bytes 5242880 | tf_op jit(solution)/shard_map/sxcd,sxcj->dxj/dot_general | solution.py:100
  218.6 2.6 copy.48
  223.4 60.3 %all-reduce.3.cloned.1.call-done = bf16[384,1,1024]{2,1,0:T(2,128)(2,1)} async-done(((bf16[384,1,1024]{2,1,0:T(2,128)(2,1)}), bf16[384,1,1024]{2,1,0:T(2,128)(2,1)}) %all-reduce.3.cloned.1.call-update) | async-done | bytes 786448
  285.4 61.6 %reduce-scatter.4.cloned.1.call-done = bf16[64,768]{1,0:T(8,128)(2,1)} async-done(((bf16[1024,768]{1,0:T(8,128)(2,1)}), bf16[64,768]{1,0:T(8,128)(2,1)}) %reduce-scatter.4.cloned.1.call-update) | async-done | bytes 98320
  348.9 2.0 gather_fusion.1
  351.4 2.1 reduce_sum.32
  353.5 4.6 %gather_fusion = bf16[512,1024]{1,0:T(8,128)(2,1)S(1)} fusion(bf16[1024,1024]{1,0:T(8,128)(2,1)} %bitcast.20, s32[1024]{0:T(1024)S(1)} %pad_clamp_fusion), kind=kCustom, calls=%fused_computation.1 | custom fusion | bytes 2099200 | tf_op jit(solution)/shard_map/gather | solution.py:90
  358.8 2.1 multiply_reduce_fusion
  (56 shorter events, 13.0 us)
Async XLA Ops:
  7.2 3.6 copy-start
  18.5 13.5 %copy-start.5 = (f32[128,4]{0,1:T(4,128)S(1)}, f32[128,4]{0,1:T(4,128)}, u32[]{:S(2)}) copy-start(f32[128,4]{0,1:T(4,128)} %param.8) | copy-start | bytes 6148
  18.5 13.7 %copy-start.3 = (bf16[128,1024]{1,0:T(8,128)(2,1)S(1)}, bf16[128,1024]{1,0:T(8,128)(2,1)}, u32[]{:S(2)}) copy-start(bf16[128,1024]{1,0:T(8,128)(2,1)} %param.11) | copy-start | bytes 786436
  18.5 63.3 %all-to-all-start = ((bf16[32,1,32,1024]{3,2,1,0:T(8,128)(2,1)}), bf16[32,1,32,1024]{3,2,1,0:T(8,128)(2,1)S(1)}, u32[]{:S(2)}, u32[]{:S(2)}) async-start(bf16[32,1,32,1024]{3,2,1,0:T(8,128)(2,1)} %bitcast.4), calls=%async_computation | async-start | bytes 4194304 | tf_op jit(solution)/shard_map/all_to_all | solution.py:84
  81.9 50.1 %copy-start.1 = (bf16[32,1,32,1024]{3,2,1,0:T(8,128)(2,1)}, bf16[32,1,32,1024]{3,2,1,0:T(8,128)(2,1)S(1)}, u32[]{:S(2)}) copy-start(bf16[32,1,32,1024]{3,2,1,0:T(8,128)(2,1)S(1)} %all-to-all-done) | copy-start | bytes 6291460
  81.9 7.1 %copy-start.4 = (bf16[1,24,1024]{2,1,0:T(8,128)(2,1)S(1)}, bf16[1,24,1024]{2,1,0:T(8,128)(2,1)}, u32[]{:S(2)}) copy-start(bf16[1,24,1024]{2,1,0:T(8,128)(2,1)} %param.10) | copy-start | bytes 147460
  81.9 56.1 %all-to-all-start.2 = ((bf16[32,1,32,1024]{3,2,1,0:T(8,128)(2,1)}), bf16[32,1,32,1024]{3,2,1,0:T(8,128)(2,1)}, u32[]{:S(2)}, u32[]{:S(2)}) async-start(bf16[32,1,32,1024]{3,2,1,0:T(8,128)(2,1)} %bitcast.21), calls=%async_computation.2 | async-start | bytes 4194304 | tf_op jit(solution)/shard_map/all_to_all | solution.py:87
  88.3 43.7 %all-gather.2.cloned.1.call-start = ((), (), s32[]{:S(2)}) async-start(), calls=%async_computation.5 | async-start | bytes 1671168 | tf_op jit(solution)/shard_map/all_gather | solution.py:81
  136.9 7.5 %copy-start.6 = (bf16[1,1024,768]{2,1,0:T(8,128)(2,1)S(1)}, bf16[1,1024,768]{2,1,0:T(8,128)(2,1)}, u32[]{:S(2)}) copy-start(bf16[1,1024,768]{2,1,0:T(8,128)(2,1)} %all-gather.2.cloned.1.call-done) | copy-start | bytes 4718596
  143.2 0.9 copy-start.7
  143.2 1.2 copy-start.9
  147.6 59.6 %all-to-all-start.3 = ((bf16[32,1,32,1024]{3,2,1,0:T(8,128)(2,1)}), bf16[32,1,32,1024]{3,2,1,0:T(8,128)(2,1)S(1)}, u32[]{:S(2)}, u32[]{:S(2)}) async-start(bf16[32,1,32,1024]{3,2,1,0:T(8,128)(2,1)} %fusion.14), calls=%async_computation.3 | async-start | bytes 4194304 | tf_op jit(solution)/shard_map/all_to_all | solution.py:89
  156.8 126.9 %all-reduce.3.cloned.1.call-start = ((), (), s32[]{:S(2)}) async-start(), calls=%async_computation.7 | async-start | bytes 3145728
  169.3 44.4 %copy-start.8 = (bf16[32,32,384]{2,1,0:T(8,128)(2,1)S(1)}, bf16[32,32,384]{2,1,0:T(8,128)(2,1)}, u32[]{:S(2)}) copy-start(bf16[32,32,384]{2,1,0:T(8,128)(2,1)} %copy-done.7) | copy-start | bytes 2359300
  207.2 146.3 %all-to-all-start.1 = ((bf16[32,1,32,1024]{3,2,1,0:T(8,128)(2,1)}), bf16[32,1,32,1024]{3,2,1,0:T(8,128)(2,1)}, u32[]{:S(2)}, u32[]{:S(2)}) async-start(bf16[32,1,32,1024]{3,2,1,0:T(8,128)(2,1)} %fusion.13), calls=%async_computation.1 | async-start | bytes 4194304 | tf_op jit(solution)/shard_map/all_to_all | solution.py:86
  213.7 133.3 %reduce-scatter.4.cloned.1.call-start = ((), (), s32[]{:S(2)}) async-start(), calls=%async_computation.6 | async-start | bytes 1671168
  218.6 2.7 copy-start.2
Sparse Core Ops, SparseCore 0:
  91.2 40.7 all-gather.1
  165.8 117.9 all-reduce.2
  286.8 60.1 reduce-scatter.3
where the time goes:
time: 372 us; the launch traced here: 367 us
  waiting for transfers between devices  229 us (62%)
  starting transfers between devices  35.7 us (10%)
  local copies, waits for them, and re-layouts  29.8 us (8%)
  matrix products  25.8 us (7%)
  blocking collectives  17.1 us (5%)
  other arithmetic  15.1 us (4%)
  between operations  14.6 us (4%)
    unnamed x5, waiting for transfers between devices  123 us
    all_to_all x1, waiting for transfers between devices, body(): lax.all_to_all(send_inputs, 'expert', split_axis=0, concat_axis=0, tiled=...  41.8 us
    all_to_all x1, waiting for transfers between devices, body(): lax.all_to_all(grad_inputs, 'expert', split_axis=0, concat_axis=0, tiled=...  37.8 us
    all_gather x1, waiting for transfers between devices, body(): lax.all_gather(w_in, 'dp', axis=1, tiled=True)  25.9 us
    all_gather x1, blocking collectives, body(): lax.all_gather(w_down, 'dp', axis=1, tiled=True)  17.1 us
    all_to_all x1, starting transfers between devices, body(): lax.all_to_all(send_inputs, 'expert', split_axis=0, concat_axis=0, tiled=...  13.5 us
    all_to_all x1, starting transfers between devices, body(): lax.all_to_all(grad_inputs, 'expert', split_axis=0, concat_axis=0, tiled=...  9.21 us
    unnamed x28, local copies, waits for them, and re-layouts  8.67 us
  transfers between devices with their start and end apart: 7, of which 6 were waited for; matrix products, arithmetic and copies ran while one was open for 12% of the time, Pallas kernels for 0%

commit v1 on v0

v1 whole, which is shorter than its diff:
```python
import jax
import jax.numpy as jnp
from jax import lax
from jax.sharding import PartitionSpec as P

step_rate = 0.5


def slot_numbers(route_rows, experts, capacity):
    flat_routes = route_rows.reshape(-1)
    one_hot = (flat_routes[:, None] == jnp.arange(experts, dtype=jnp.int32)[None, :]).astype(
        jnp.int32
    )
    running = jnp.cumsum(one_hot, axis=0)
    position = jnp.sum(one_hot * running, axis=1) - 1
    return flat_routes * capacity + position


def expert_forward(inputs, full_in, full_down):
    model_width = full_in.shape[1]
    hidden_units = full_down.shape[1]
    projected = jnp.einsum(
        "sxcd,xdj->sxcj", inputs, full_in, preferred_element_type=jnp.float32
    ) * model_width ** (-0.5)
    gate_part = projected[..., :hidden_units]
    up_part = projected[..., hidden_units:]
    activation = (jax.nn.silu(gate_part) * up_part).astype(jnp.bfloat16)
    results = (
        jnp.einsum("sxcf,xfd->sxcd", activation, full_down, preferred_element_type=jnp.float32)
        * hidden_units ** (-0.5)
    ).astype(jnp.bfloat16)
    return (projected, activation, results)


def expert_backward(projected, grad_rows, full_in, full_down):
    model_width = full_in.shape[1]
    hidden_units = full_down.shape[1]
    grad_act = jnp.einsum(
        "sxcd,xfd->sxcf", grad_rows, full_down, preferred_element_type=jnp.float32
    ) * hidden_units ** (-0.5)
    gate_part = projected[..., :hidden_units]
    up_part = projected[..., hidden_units:]
    sigmoid_gate = jax.nn.sigmoid(gate_part)
    grad_gate = grad_act * up_part * sigmoid_gate * (1.0 + gate_part * (1.0 - sigmoid_gate))
    grad_up = grad_act * jax.nn.silu(gate_part)
    grad_hidden = jnp.concatenate([grad_gate, grad_up], axis=-1).astype(jnp.bfloat16)
    grad_inputs = (
        jnp.einsum("sxcj,xdj->sxcd", grad_hidden, full_in, preferred_element_type=jnp.float32)
        * model_width ** (-0.5)
    ).astype(jnp.bfloat16)
    return (grad_hidden, grad_inputs)


def to_owner_rows(grad, owners):
    per_device, rows, cols = grad.shape
    part = rows // owners
    return (
        grad.reshape(per_device, owners, part, cols)
        .transpose(1, 0, 2, 3)
        .reshape(owners, per_device * part * cols)
    )


def from_owner_rows(flat, owners, per_device, part, cols):
    return (
        flat.reshape(owners, per_device, part, cols)
        .transpose(1, 0, 2, 3)
        .reshape(per_device, owners * part, cols)
    )


def body(tokens, routes, gates, w_in, w_down, out_grad):
    tok_rows, model_width = tokens.shape
    top_count = routes.shape[1]
    per_device, in_rows, in_cols = w_in.shape
    _, down_rows, down_cols = w_down.shape
    hidden_units = in_cols // 2
    sources = lax.axis_size("expert")
    owners = lax.axis_size("dp")
    experts = per_device * sources
    capacity = min(tok_rows, 2 * tok_rows * top_count // experts)
    total = experts * capacity

    in_size = in_rows * in_cols
    packed_w = jnp.concatenate(
        [w_in.reshape(1, per_device * in_size), w_down.reshape(1, per_device * down_rows * down_cols)],
        axis=1,
    )
    gathered = lax.all_gather(packed_w, "dp", axis=0, tiled=True)
    full_in = from_owner_rows(gathered[:, : per_device * in_size], owners, per_device, in_rows, in_cols)
    full_down = from_owner_rows(
        gathered[:, per_device * in_size :], owners, per_device, down_rows, down_cols
    )

    slot_index = slot_numbers(routes, experts, capacity).reshape(tok_rows, top_count)
    match = slot_index[None, :, :] == jnp.arange(total, dtype=jnp.int32)[:, None, None]
    pick = jnp.any(match, axis=2).astype(jnp.bfloat16)
    gate_of_slot = jnp.sum(jnp.where(match, gates[None, :, :], 0.0), axis=(1, 2))
    layout = (sources, per_device, capacity, model_width)
    send_inputs = jnp.dot(pick, tokens, preferred_element_type=jnp.float32).astype(jnp.bfloat16)
    grad_of_slot = jnp.dot(pick, out_grad, preferred_element_type=jnp.float32)
    send_grads = (gate_of_slot[:, None] * grad_of_slot).astype(jnp.bfloat16)

    inputs_here = lax.all_to_all(
        send_inputs.reshape(layout), "expert", split_axis=0, concat_axis=0, tiled=True
    )
    grad_rows = lax.all_to_all(
        send_grads.reshape(layout), "expert", split_axis=0, concat_axis=0, tiled=True
    )
    projected_here, activation_here, results_here = expert_forward(inputs_here, full_in, full_down)
    results_home = lax.all_to_all(results_here, "expert", split_axis=0, concat_axis=0, tiled=True)
    grad_hidden, grad_inputs = expert_backward(projected_here, grad_rows, full_in, full_down)

    grad_in = (
        jnp.einsum("sxcd,sxcj->xdj", inputs_here, grad_hidden, preferred_element_type=jnp.float32)
        * model_width ** (-0.5)
    ).astype(jnp.bfloat16)
    grad_down = (
        jnp.einsum("sxcf,sxcd->xfd", activation_here, grad_rows, preferred_element_type=jnp.float32)
        * hidden_units ** (-0.5)
    ).astype(jnp.bfloat16)
    packed_g = jnp.concatenate([to_owner_rows(grad_in, owners), to_owner_rows(grad_down, owners)], axis=1)
    packed_g = packed_g.reshape(owners * 8, -1)
    summed = lax.psum_scatter(packed_g, "dp", scatter_dimension=0, tiled=True)
    summed = summed.reshape(1, -1).astype(jnp.float32)
    summed_in = from_owner_rows(summed[:, : per_device * in_size], 1, per_device, in_rows, in_cols)
    summed_down = from_owner_rows(
        summed[:, per_device * in_size :], 1, per_device, down_rows, down_cols
    )

    inputs_back = lax.all_to_all(grad_inputs, "expert", split_axis=0, concat_axis=0, tiled=True)

    combine = jnp.sum(jnp.where(match, gates[None, :, :], 0.0), axis=2)
    moe_out = jnp.einsum(
        "st,sd->td",
        combine,
        results_home.reshape(total, model_width).astype(jnp.float32),
        precision=lax.Precision.HIGHEST,
        preferred_element_type=jnp.float32,
    ).astype(jnp.bfloat16)
    token_grad = jnp.einsum(
        "st,sd->td",
        pick,
        inputs_back.reshape(total, model_width),
        preferred_element_type=jnp.float32,
    ).astype(jnp.bfloat16)

    new_w_in = (w_in.astype(jnp.float32) - step_rate * summed_in).astype(jnp.bfloat16)
    new_w_down = (w_down.astype(jnp.float32) - step_rate * summed_down).astype(jnp.bfloat16)
    return (moe_out, token_grad, new_w_in, new_w_down)


def solution(mesh):
    return jax.shard_map(
        body,
        mesh=mesh,
        in_specs=(
            P(("dp", "expert"), None),
            P(("dp", "expert"), None),
            P(("dp", "expert"), None),
            P("expert", "dp", None),
            P("expert", "dp", None),
            P(("dp", "expert"), None),
        ),
        out_specs=(
            P(("dp", "expert"), None),
            P(("dp", "expert"), None),
            P("expert", "dp", None),
            P("expert", "dp", None),
        ),
        check_vma=False,
    )
```

time: 372 us -> 275 us (0.74); the launches traced: 367 us -> 274 us
  waiting for transfers between devices: 229 us -> 168 us
  blocking collectives: 17.1 us -> 0 us
  local copies, waits for them, and re-layouts: 29.8 us -> 21.5 us
  other arithmetic: 15.1 us -> 9.08 us
    unnamed x5 -> x2, waiting for transfers between devices: 123 us -> 0.03 us
    all_to_all x1, waiting for transfers between devices: 0.01 us -> 46.9 us  [body(): lax.all_to_all(results_here, 'expert', split_axis=0, concat_axis=0, tiled...]
    all_to_all x2, waiting for transfers between devices: 42.9 us -> 79.2 us  [the longest x1 45.5 us: body(): lax.all_to_all(send_inputs.reshape(layout), 'expert', split_axis=0, conca...]
    all_gather x1, waiting for transfers between devices: 25.9 us -> 0.02 us  [body(): gathered = lax.all_gather(packed_w, 'dp', axis=0, tiled=True)]
    all_gather x1 -> x0, blocking collectives: 17.1 us -> none  [body(): lax.all_gather(w_down, 'dp', axis=1, tiled=True)]
    another operation x1 -> x5, local copies, waits for them, and re-layouts: 0.01 us -> 8.32 us  [the longest x2 4.25 us: to_owner_rows(): return grad.reshape(per_device, owners, part, cols).transpose(1, 0, 2, 3)...]
    scatter x1 -> x0, other arithmetic: 7.82 us -> none  [body(): send_grads = jnp.zeros((experts * capacity, model_width), jnp.bfloat16).a...]
    scatter x1 -> x0, local copies, waits for them, and re-layouts: 7.75 us -> none  [body(): send_inputs = jnp.zeros((experts * capacity, model_width), jnp.bfloat16)....]
  transfers between devices with their start and end apart: 7 -> 6, of which waited for: 6 -> 4; matrix products, arithmetic and copies ran while one was open for 12% -> 11% of each run, Pallas kernels for 0% -> 0%
where the time goes in v1:
time: 275 us; the launch traced here: 274 us
  waiting for transfers between devices  168 us (61%)
  starting transfers between devices  32 us (12%)
  matrix products  29.1 us (11%)
  local copies, waits for them, and re-layouts  21.5 us (8%)
  between operations  14.3 us (5%)
  other arithmetic  9.08 us (3%)
    all_to_all x1, waiting for transfers between devices, body(): lax.all_to_all(results_here, 'expert', split_axis=0, concat_axis=0, tiled...  46.9 us
    all_to_all x1, waiting for transfers between devices, body(): lax.all_to_all(send_inputs.reshape(layout), 'expert', split_axis=0, conca...  45.5 us
    all_to_all x1, waiting for transfers between devices, body(): lax.all_to_all(grad_inputs, 'expert', split_axis=0, concat_axis=0, tiled=...  42 us
    all_to_all x1, waiting for transfers between devices, body(): lax.all_to_all(send_grads.reshape(layout), 'expert', split_axis=0, concat...  33.7 us
    all_to_all x1, starting transfers between devices, body(): lax.all_to_all(send_inputs.reshape(layout), 'expert', split_axis=0, conca...  13.3 us
    unnamed x33, local copies, waits for them, and re-layouts  9.05 us
    all_to_all x1, starting transfers between devices, body(): lax.all_to_all(send_grads.reshape(layout), 'expert', split_axis=0, concat...  6.31 us
    all_to_all x1, starting transfers between devices, body(): lax.all_to_all(grad_inputs, 'expert', split_axis=0, concat_axis=0, tiled=...  6.27 us
  transfers between devices with their start and end apart: 6, of which 4 were waited for; matrix products, arithmetic and copies ran while one was open for 11% of the time, Pallas kernels for 0%

profile of v1, /device:TPU:56, one launch (start us, length us, event | category | flops | bytes accessed | tf_op | source)
XLA Modules:
  0.0 274.1 jit_solution(2985038796484547932)
XLA Ops:
  11.0 2.1 convolution_convert_fusion
  13.1 13.3 %all-to-all-start = ((bf16[32,1,32,1024]{3,2,1,0:T(8,128)(2,1)}), bf16[32,1,32,1024]{3,2,1,0:T(8,128)(2,1)S(1)}, u32[]{:S(2)}, u32[]{:S(2)}) async-start(bf16[32,1,32,1024]{3,2,1,0:T(8,128)(2,1)} %bitcast.3), calls=%async_computation | async-start | bytes 4194304 | tf_op jit(solution)/shard_map/all_to_all | solution.py:104
  28.9 2.1 multiply_convert_fusion.1
  31.0 45.5 %all-to-all-done = bf16[32,1,32,1024]{3,2,1,0:T(8,128)(2,1)S(1)} async-done(((bf16[32,1,32,1024]{3,2,1,0:T(8,128)(2,1)}), bf16[32,1,32,1024]{3,2,1,0:T(8,128)(2,1)S(1)}, u32[]{:S(2)}, u32[]{:S(2)}) %all-to-all-start) | async-done | bytes 2097184 | tf_op jit(solution)/shard_map/all_to_all | solution.py:104
  77.9 6.3 %all-to-all-start.2 = ((bf16[32,1,32,1024]{3,2,1,0:T(8,128)(2,1)}), bf16[32,1,32,1024]{3,2,1,0:T(8,128)(2,1)S(1)}, u32[]{:S(2)}, u32[]{:S(2)}) async-start(bf16[32,1,32,1024]{3,2,1,0:T(8,128)(2,1)} %bitcast.117), calls=%async_computation.2 | async-start | bytes 4194304 | tf_op jit(solution)/shard_map/all_to_all | solution.py:107
  84.2 4.9 %copy.71 = bf16[16,1,73728]{2,0,1:T(8,128)(2,1)S(1)} copy(bf16[16,1,73728]{2,1,0:T(2,128)(2,1)} %all-gather.3.cloned.1.call-done) | data formatting | bytes 4718592
  90.4 2.7 %reshape.180 = bf16[1024,768,1]{1,0,2:T(8,128)(2,1)} reshape(bf16[16,49152]{1,0:T(8,128)(2,1)} %slice.36) | data formatting | bytes 3145728 | tf_op jit(solution)/shard_map/reshape.3
  94.5 5.5 %multiply_bitcast_fusion = f32[32,1,32,768]{3,2,0,1:T(8,128)} fusion(bf16[1024,768,1]{1,0,2:T(8,128)(2,1)} %reshape.180, bf16[32,1,32,1024]{3,2,1,0:T(8,128)(2,1)} %copy-done.1), kind=kOutput, calls=%fused_computation.5 | convolution fusion | flops 1611399168 | bytes 6815744 | tf_op jit(solution)/shard_map/sxcd,xdj->sxcj/dot_general | solution.py:22
  100.0 33.7 %all-to-all-done.2 = bf16[32,1,32,1024]{3,2,1,0:T(8,128)(2,1)S(1)} async-done(((bf16[32,1,32,1024]{3,2,1,0:T(8,128)(2,1)}), bf16[32,1,32,1024]{3,2,1,0:T(8,128)(2,1)S(1)}, u32[]{:S(2)}, u32[]{:S(2)}) %all-to-all-start.2) | async-done | bytes 2097184 | tf_op jit(solution)/shard_map/all_to_all | solution.py:107
  133.8 4.0 %fusion.26 = (bf16[32,32,384]{2,1,0:T(8,128)(2,1)S(1)}, bf16[32,32,384]{2,1,0:T(8,128)(2,1)S(1)}, bf16[32,32,384]{2,1,0:T(8,128)(2,1)S(1)}) fusion(f32[32,1,32,768]{3,2,0,1:T(8,128)} %multiply_bitcast_fusion, bf16[384,1024,1]{1,0,2:T(8,128)(2,1)} %reshape.181, bf16[32,1,32,1024]{3,2,1,0:T(8,128)(2,1)S(1)} %all-to-all-done.2), kind=kOutput, calls=%fused_computation.39 | convolution fusion | flops 811597824 | bytes 8388608 | tf_op jit(solution)/shard_map/sxcd,xfd->sxcf/dot_general | solution.py:38
  137.8 3.2 %fusion.2 = bf16[32,1,32,1024]{3,2,1,0:T(8,128)(2,1)} fusion(bf16[1024,768,1]{1,0,2:T(8,128)(2,1)S(1)} %copy-done.4, bf16[32,32,384]{2,1,0:T(8,128)(2,1)S(1)} %get-tuple-element.7, bf16[32,32,384]{2,1,0:T(8,128)(2,1)S(1)} %get-tuple-element.6), kind=kOutput, calls=%fused_computation.11 | convolution fusion | flops 1615855616 | bytes 5242880 | tf_op jit(solution)/shard_map/sxcj,xdj->sxcd/dot_general | solution.py:48
  141.0 3.1 %fusion = bf16[1024,768]{1,0:T(8,128)(2,1)} fusion(bf16[32,1,32,1024]{3,2,1,0:T(8,128)(2,1)S(1)} %copy-done.2, bf16[32,32,384]{2,1,0:T(8,128)(2,1)S(1)} %get-tuple-element.7, bf16[32,32,384]{2,1,0:T(8,128)(2,1)S(1)} %get-tuple-element.6), kind=kOutput, calls=%fused_computation.4 | convolution fusion | flops 1615331328 | bytes 5242880 | tf_op jit(solution)/shard_map/sxcd,sxcj->xdj/dot_general | solution.py:115
  144.1 2.8 %reshape_transpose_reshape.4 = bf16[16,49152]{1,0:T(8,128)(2,1)} reshape(bf16[1024,768]{1,0:T(8,128)(2,1)} %fusion) | data formatting | bytes 3145728 | tf_op jit(solution)/shard_map/reshape;transpose;reshape | solution.py:60
  146.9 1.9 fusion.16
  148.8 1.5 reshape_transpose_reshape.5
  150.3 6.3 %all-to-all-start.3 = ((bf16[32,1,32,1024]{3,2,1,0:T(8,128)(2,1)}), bf16[32,1,32,1024]{3,2,1,0:T(8,128)(2,1)}, u32[]{:S(2)}, u32[]{:S(2)}) async-start(bf16[32,1,32,1024]{3,2,1,0:T(8,128)(2,1)} %fusion.2), calls=%async_computation.3 | async-start | bytes 4194304 | tf_op jit(solution)/shard_map/all_to_all | solution.py:131
  156.6 1.6 pad_maximum_fusion
  158.1 2.2 reshape.176
  161.7 2.6 fusion.1
  164.3 42.0 %all-to-all-done.3 = bf16[32,1,32,1024]{3,2,1,0:T(8,128)(2,1)} async-done(((bf16[32,1,32,1024]{3,2,1,0:T(8,128)(2,1)}), bf16[32,1,32,1024]{3,2,1,0:T(8,128)(2,1)}, u32[]{:S(2)}, u32[]{:S(2)}) %all-to-all-start.3) | async-done | bytes 2097184 | tf_op jit(solution)/shard_map/all_to_all | solution.py:131
  206.2 6.0 %all-to-all-start.1 = ((bf16[32,1,32,1024]{3,2,1,0:T(8,128)(2,1)}), bf16[32,1,32,1024]{3,2,1,0:T(8,128)(2,1)S(1)}, u32[]{:S(2)}, u32[]{:S(2)}) async-start(bf16[32,1,32,1024]{3,2,1,0:T(8,128)(2,1)} %fusion.1), calls=%async_computation.1 | async-start | bytes 4194304 | tf_op jit(solution)/shard_map/all_to_all | solution.py:111
  212.3 2.8 %convolution_convert_fusion.1 = bf16[128,1024]{1,0:T(8,128)(2,1)} fusion(pred[1024,128]{1,0:T(8,128)(4,1)S(1)} %fusion.11, bf16[1024,1024]{1,0:T(8,128)(2,1)} %bitcast.24), kind=kOutput, calls=%fused_computation.35 | convolution fusion | flops 268566528 | bytes 2490368 | tf_op jit(solution)/shard_map/st,sd->td/dot_general | solution.py:141
  215.1 46.9 %all-to-all-done.1 = bf16[32,1,32,1024]{3,2,1,0:T(8,128)(2,1)S(1)} async-done(((bf16[32,1,32,1024]{3,2,1,0:T(8,128)(2,1)}), bf16[32,1,32,1024]{3,2,1,0:T(8,128)(2,1)S(1)}, u32[]{:S(2)}, u32[]{:S(2)}) %all-to-all-start.1) | async-done | bytes 2097184 | tf_op jit(solution)/shard_map/all_to_all | solution.py:111
  262.0 1.8 convolution_convert_fusion.2
  (63 shorter events, 15.1 us)
Async XLA Ops:
  7.2 3.9 %copy-start = (bf16[128,1024]{1,0:T(8,128)(2,1)S(1)}, bf16[128,1024]{1,0:T(8,128)(2,1)}, u32[]{:S(2)}) copy-start(bf16[128,1024]{1,0:T(8,128)(2,1)} %param.6) | copy-start | bytes 786436
  13.1 13.4 %copy-start.11 = (bf16[1,24,1024]{2,1,0:T(8,128)(2,1)S(1)}, bf16[1,24,1024]{2,1,0:T(8,128)(2,1)}, u32[]{:S(2)}) copy-start(bf16[1,24,1024]{2,1,0:T(8,128)(2,1)} %param.10) | copy-start | bytes 147460
  13.1 13.5 %copy-start.8 = (bf16[1,64,768]{2,1,0:T(8,128)(2,1)S(1)}, bf16[1,64,768]{2,1,0:T(8,128)(2,1)}, u32[]{:S(2)}) copy-start(bf16[1,64,768]{2,1,0:T(8,128)(2,1)} %param.9) | copy-start | bytes 294916
  13.1 14.7 %copy-start.13 = (f32[128,4]{0,1:T(4,128)S(1)}, f32[128,4]{0,1:T(4,128)}, u32[]{:S(2)}) copy-start(f32[128,4]{0,1:T(4,128)} %param.8) | copy-start | bytes 6148
  13.1 15.8 %copy-start.10 = (bf16[128,1024]{1,0:T(8,128)(2,1)S(1)}, bf16[128,1024]{1,0:T(8,128)(2,1)}, u32[]{:S(2)}) copy-start(bf16[128,1024]{1,0:T(8,128)(2,1)} %param.11) | copy-start | bytes 786436
  13.1 63.4 %all-to-all-start = ((bf16[32,1,32,1024]{3,2,1,0:T(8,128)(2,1)}), bf16[32,1,32,1024]{3,2,1,0:T(8,128)(2,1)S(1)}, u32[]{:S(2)}, u32[]{:S(2)}) async-start(bf16[32,1,32,1024]{3,2,1,0:T(8,128)(2,1)} %bitcast.3), calls=%async_computation | async-start | bytes 4194304 | tf_op jit(solution)/shard_map/all_to_all | solution.py:104
  26.4 57.8 %all-gather.3.cloned.1.call-start = ((), (), s32[]{:S(2)}) async-start(), calls=%async_computation.6 | async-start | bytes 5013504 | tf_op jit(solution)/shard_map/all_gather | solution.py:89
  76.5 1.4 copy-start.1
  77.9 55.9 %all-to-all-start.2 = ((bf16[32,1,32,1024]{3,2,1,0:T(8,128)(2,1)}), bf16[32,1,32,1024]{3,2,1,0:T(8,128)(2,1)S(1)}, u32[]{:S(2)}, u32[]{:S(2)}) async-start(bf16[32,1,32,1024]{3,2,1,0:T(8,128)(2,1)} %bitcast.117), calls=%async_computation.2 | async-start | bytes 4194304 | tf_op jit(solution)/shard_map/all_to_all | solution.py:107
  133.8 4.1 %copy-start.4 = (bf16[1024,768,1]{1,0,2:T(8,128)(2,1)S(1)}, bf16[1024,768,1]{1,0,2:T(8,128)(2,1)}, u32[]{:S(2)}) copy-start(bf16[1024,768,1]{1,0,2:T(8,128)(2,1)} %reshape.180) | copy-start | bytes 4718596
  137.8 9.1 %copy-start.5 = (bf16[32,32,384]{2,1,0:T(8,128)(2,1)}, bf16[32,32,384]{2,1,0:T(8,128)(2,1)S(1)}, u32[]{:S(2)}) copy-start(bf16[32,32,384]{2,1,0:T(8,128)(2,1)S(1)} %get-tuple-element.8) | copy-start | bytes 2359300
  137.8 3.2 %copy-start.2 = (bf16[32,1,32,1024]{3,2,1,0:T(8,128)(2,1)S(1)}, bf16[32,1,32,1024]{3,2,1,0:T(8,128)(2,1)}, u32[]{:S(2)}) copy-start(bf16[32,1,32,1024]{3,2,1,0:T(8,128)(2,1)} %copy-done.1) | copy-start | bytes 6291460
  150.3 56.0 %all-to-all-start.3 = ((bf16[32,1,32,1024]{3,2,1,0:T(8,128)(2,1)}), bf16[32,1,32,1024]{3,2,1,0:T(8,128)(2,1)}, u32[]{:S(2)}, u32[]{:S(2)}) async-start(bf16[32,1,32,1024]{3,2,1,0:T(8,128)(2,1)} %fusion.2), calls=%async_computation.3 | async-start | bytes 4194304 | tf_op jit(solution)/shard_map/all_to_all | solution.py:131
  156.5 107.3 %reduce-scatter.2.cloned.1.call-start = ((), (), s32[]{:S(2)}) async-start(), calls=%async_computation.5 | async-start | bytes 2506752 | tf_op jit(solution)/shard_map/reduce_scatter | solution.py:124
  160.3 1.1 copy-start.6
  160.3 1.4 copy-start.7
  206.2 55.7 %all-to-all-start.1 = ((bf16[32,1,32,1024]{3,2,1,0:T(8,128)(2,1)}), bf16[32,1,32,1024]{3,2,1,0:T(8,128)(2,1)S(1)}, u32[]{:S(2)}, u32[]{:S(2)}) async-start(bf16[32,1,32,1024]{3,2,1,0:T(8,128)(2,1)} %fusion.1), calls=%async_computation.1 | async-start | bytes 4194304 | tf_op jit(solution)/shard_map/all_to_all | solution.py:111
  212.3 49.7 %copy-start.3 = (f32[1024,128]{1,0:T(8,128)S(1)}, f32[1024,128]{1,0:T(8,128)}, u32[]{:S(2)}) copy-start(f32[1024,128]{1,0:T(8,128)} %get-tuple-element.5) | copy-start | bytes 1572868
  262.0 4.0 %copy-start.9 = (bf16[1,64,768]{2,1,0:T(8,128)(2,1)S(1)}, bf16[1,64,768]{2,1,0:T(8,128)(2,1)}, u32[]{:S(2)}) copy-start(bf16[1,64,768]{2,1,0:T(8,128)(2,1)} %param.9) | copy-start | bytes 294916
  262.0 4.7 %copy-start.12 = (bf16[1,24,1024]{2,1,0:T(8,128)(2,1)S(1)}, bf16[1,24,1024]{2,1,0:T(8,128)(2,1)}, u32[]{:S(2)}) copy-start(bf16[1,24,1024]{2,1,0:T(8,128)(2,1)} %param.10) | copy-start | bytes 147460
Sparse Core Ops, SparseCore 0:
  29.4 45.2 all-gather.2
  160.4 60.7 reduce-scatter.1

commit v2 on v1

--- a/solution.py
+++ b/solution.py
@@ -107,7 +107,9 @@
     grad_rows = lax.all_to_all(
         send_grads.reshape(layout), "expert", split_axis=0, concat_axis=0, tiled=True
     )
-    projected_here, activation_here, results_here = expert_forward(inputs_here, full_in, full_down)
+    projected_here, activation_here, results_here = lax.optimization_barrier(
+        expert_forward(inputs_here, full_in, full_down)
+    )
     results_home = lax.all_to_all(results_here, "expert", split_axis=0, concat_axis=0, tiled=True)
     grad_hidden, grad_inputs = expert_backward(projected_here, grad_rows, full_in, full_down)
 

time: 275 us -> 267 us (0.971)
  waiting for transfers between devices: 168 us -> 160 us
    all_to_all x1, waiting for transfers between devices: 42 us -> 36.8 us  [body(): lax.all_to_all(grad_inputs, 'expert', split_axis=0, concat_axis=0, tiled=...]
    all_to_all x1, waiting for transfers between devices: 33.7 us -> 31 us  [body(): lax.all_to_all(send_grads.reshape(layout), 'expert', split_axis=0, concat...]
  transfers between devices with their start and end apart: 6 -> 6, of which waited for: 4 -> 4; matrix products, arithmetic and copies ran while one was open for 11% -> 15% of each run, Pallas kernels for 0% -> 0%
where the time goes in v2:
time: 267 us; the launch traced here: 266 us
  waiting for transfers between devices  160 us (60%)
  starting transfers between devices  32.2 us (12%)
  matrix products  28.4 us (11%)
  local copies, waits for them, and re-layouts  21.4 us (8%)
  between operations  14.3 us (5%)
  other arithmetic  9.52 us (4%)
    all_to_all x1, waiting for transfers between devices, body(): lax.all_to_all(results_here, 'expert', split_axis=0, concat_axis=0, tiled...  46.9 us
    all_to_all x1, waiting for transfers between devices, body(): lax.all_to_all(send_inputs.reshape(layout), 'expert', split_axis=0, conca...  45.6 us
    all_to_all x1, waiting for transfers between devices, body(): lax.all_to_all(grad_inputs, 'expert', split_axis=0, concat_axis=0, tiled=...  36.8 us
    all_to_all x1, waiting for transfers between devices, body(): lax.all_to_all(send_grads.reshape(layout), 'expert', split_axis=0, concat...  31 us
    all_to_all x1, starting transfers between devices, body(): lax.all_to_all(send_inputs.reshape(layout), 'expert', split_axis=0, conca...  13.3 us
    unnamed x33, local copies, waits for them, and re-layouts  10.1 us
    all_to_all x1, starting transfers between devices, body(): lax.all_to_all(send_grads.reshape(layout), 'expert', split_axis=0, concat...  6.31 us
    all_to_all x1, starting transfers between devices, body(): lax.all_to_all(grad_inputs, 'expert', split_axis=0, concat_axis=0, tiled=...  6.26 us
  transfers between devices with their start and end apart: 6, of which 4 were waited for; matrix products, arithmetic and copies ran while one was open for 15% of the time, Pallas kernels for 0%

profile of v2, /device:TPU:56, one launch (start us, length us, event | category | flops | bytes accessed | tf_op | source)
XLA Modules:
  0.0 266.0 jit_solution(4464704520859162257)
XLA Ops:
  11.0 2.1 convolution_convert_fusion
  13.1 13.3 %all-to-all-start = ((bf16[32,1,32,1024]{3,2,1,0:T(8,128)(2,1)}), bf16[32,1,32,1024]{3,2,1,0:T(8,128)(2,1)S(1)}, u32[]{:S(2)}, u32[]{:S(2)}) async-start(bf16[32,1,32,1024]{3,2,1,0:T(8,128)(2,1)} %bitcast.3), calls=%async_computation | async-start | bytes 4194304 | tf_op jit(solution)/shard_map/all_to_all | solution.py:104
  28.9 2.1 multiply_convert_fusion.1
  30.9 45.6 %all-to-all-done = bf16[32,1,32,1024]{3,2,1,0:T(8,128)(2,1)S(1)} async-done(((bf16[32,1,32,1024]{3,2,1,0:T(8,128)(2,1)}), bf16[32,1,32,1024]{3,2,1,0:T(8,128)(2,1)S(1)}, u32[]{:S(2)}, u32[]{:S(2)}) %all-to-all-start) | async-done | bytes 2097184 | tf_op jit(solution)/shard_map/all_to_all | solution.py:104
  77.8 6.3 %all-to-all-start.2 = ((bf16[32,1,32,1024]{3,2,1,0:T(8,128)(2,1)}), bf16[32,1,32,1024]{3,2,1,0:T(8,128)(2,1)S(1)}, u32[]{:S(2)}, u32[]{:S(2)}) async-start(bf16[32,1,32,1024]{3,2,1,0:T(8,128)(2,1)} %bitcast.118), calls=%async_computation.2 | async-start | bytes 4194304 | tf_op jit(solution)/shard_map/all_to_all | solution.py:107
  84.2 4.9 %copy.71 = bf16[16,1,73728]{2,0,1:T(8,128)(2,1)S(1)} copy(bf16[16,1,73728]{2,1,0:T(2,128)(2,1)} %all-gather.3.cloned.1.call-done) | data formatting | bytes 4718592
  90.4 2.8 %reshape.183 = bf16[1024,768,1]{1,0,2:T(8,128)(2,1)} reshape(bf16[16,49152]{1,0:T(8,128)(2,1)} %slice.41) | data formatting | bytes 3145728 | tf_op jit(solution)/shard_map/reshape.3
  94.5 4.0 %multiply_bitcast_fusion = f32[32,1,32,768]{3,2,0,1:T(8,128)S(1)} fusion(bf16[1024,768,1]{1,0,2:T(8,128)(2,1)} %reshape.183, bf16[32,1,32,1024]{3,2,1,0:T(8,128)(2,1)} %copy-done.2), kind=kOutput, calls=%fused_computation.5 | convolution fusion | flops 1611399168 | bytes 6815744 | tf_op jit(solution)/shard_map/sxcd,xdj->sxcj/dot_general | solution.py:22
  100.2 2.6 fusion.1
  102.8 31.0 %all-to-all-done.2 = bf16[32,1,32,1024]{3,2,1,0:T(8,128)(2,1)S(1)} async-done(((bf16[32,1,32,1024]{3,2,1,0:T(8,128)(2,1)}), bf16[32,1,32,1024]{3,2,1,0:T(8,128)(2,1)S(1)}, u32[]{:S(2)}, u32[]{:S(2)}) %all-to-all-start.2) | async-done | bytes 2097184 | tf_op jit(solution)/shard_map/all_to_all | solution.py:107
  133.8 4.0 %fusion.27 = (bf16[32,32,384]{2,1,0:T(8,128)(2,1)S(1)}, bf16[32,32,384]{2,1,0:T(8,128)(2,1)S(1)}) fusion(f32[32,1,32,768]{3,2,0,1:T(8,128)} %copy-done.1, bf16[384,1024,1]{1,0,2:T(8,128)(2,1)} %reshape.184, bf16[32,1,32,1024]{3,2,1,0:T(8,128)(2,1)S(1)} %all-to-all-done.2), kind=kOutput, calls=%fused_computation.40 | convolution fusion | flops 810811392 | bytes 7602176 | tf_op jit(solution)/shard_map/sxcd,xfd->sxcf/dot_general | solution.py:38
  139.0 3.2 %fusion.2 = bf16[32,1,32,1024]{3,2,1,0:T(8,128)(2,1)} fusion(bf16[1024,768,1]{1,0,2:T(8,128)(2,1)S(1)} %copy-done.4, bf16[32,32,384]{2,1,0:T(8,128)(2,1)S(1)} %get-tuple-element.13, bf16[32,32,384]{2,1,0:T(8,128)(2,1)S(1)} %get-tuple-element.12), kind=kOutput, calls=%fused_computation.11 | convolution fusion | flops 1615855616 | bytes 5242880 | tf_op jit(solution)/shard_map/sxcj,xdj->sxcd/dot_general | solution.py:48
  142.1 6.3 %all-to-all-start.3 = ((bf16[32,1,32,1024]{3,2,1,0:T(8,128)(2,1)}), bf16[32,1,32,1024]{3,2,1,0:T(8,128)(2,1)}, u32[]{:S(2)}, u32[]{:S(2)}) async-start(bf16[32,1,32,1024]{3,2,1,0:T(8,128)(2,1)} %fusion.2), calls=%async_computation.3 | async-start | bytes 4194304 | tf_op jit(solution)/shard_map/all_to_all | solution.py:133
  148.6 1.9 fusion.17
  150.6 1.5 reshape_transpose_reshape.5
  152.0 3.9 %fusion = bf16[1024,768]{1,0:T(8,128)(2,1)S(1)} fusion(bf16[32,1,32,1024]{3,2,1,0:T(8,128)(2,1)} %copy-done.2, bf16[32,32,384]{2,1,0:T(8,128)(2,1)} %copy-done.13, bf16[32,32,384]{2,1,0:T(8,128)(2,1)} %copy-done.12), kind=kOutput, calls=%fused_computation.4 | convolution fusion | flops 1615331328 | bytes 5242880 | tf_op jit(solution)/shard_map/sxcd,sxcj->xdj/dot_general | solution.py:117
  155.9 1.6 reshape_transpose_reshape.4
  157.6 1.6 pad_maximum_fusion
  159.1 2.2 reshape.179
  161.3 36.8 %all-to-all-done.3 = bf16[32,1,32,1024]{3,2,1,0:T(8,128)(2,1)} async-done(((bf16[32,1,32,1024]{3,2,1,0:T(8,128)(2,1)}), bf16[32,1,32,1024]{3,2,1,0:T(8,128)(2,1)}, u32[]{:S(2)}, u32[]{:S(2)}) %all-to-all-start.3) | async-done | bytes 2097184 | tf_op jit(solution)/shard_map/all_to_all | solution.py:133
  198.1 6.0 %all-to-all-start.1 = ((bf16[32,1,32,1024]{3,2,1,0:T(8,128)(2,1)}), bf16[32,1,32,1024]{3,2,1,0:T(8,128)(2,1)S(1)}, u32[]{:S(2)}, u32[]{:S(2)}) async-start(bf16[32,1,32,1024]{3,2,1,0:T(8,128)(2,1)} %bitcast.120), calls=%async_computation.1 | async-start | bytes 4194304 | tf_op jit(solution)/shard_map/all_to_all | solution.py:113
  204.1 2.9 %convolution_convert_fusion.1 = bf16[128,1024]{1,0:T(8,128)(2,1)} fusion(pred[1024,128]{1,0:T(8,128)(4,1)S(1)} %fusion.11, bf16[1024,1024]{1,0:T(8,128)(2,1)} %bitcast.24), kind=kOutput, calls=%fused_computation.35 | convolution fusion | flops 268566528 | bytes 2490368 | tf_op jit(solution)/shard_map/st,sd->td/dot_general | solution.py:143
  207.0 46.9 %all-to-all-done.1 = bf16[32,1,32,1024]{3,2,1,0:T(8,128)(2,1)S(1)} async-done(((bf16[32,1,32,1024]{3,2,1,0:T(8,128)(2,1)}), bf16[32,1,32,1024]{3,2,1,0:T(8,128)(2,1)S(1)}, u32[]{:S(2)}, u32[]{:S(2)}) %all-to-all-start.1) | async-done | bytes 2097184 | tf_op jit(solution)/shard_map/all_to_all | solution.py:113
  253.9 1.8 convolution_convert_fusion.2
  (64 shorter events, 16.7 us)
Async XLA Ops:
  7.2 3.9 %copy-start = (bf16[128,1024]{1,0:T(8,128)(2,1)S(1)}, bf16[128,1024]{1,0:T(8,128)(2,1)}, u32[]{:S(2)}) copy-start(bf16[128,1024]{1,0:T(8,128)(2,1)} %param.6) | copy-start | bytes 786436
  13.1 13.4 %copy-start.9 = (bf16[1,24,1024]{2,1,0:T(8,128)(2,1)S(1)}, bf16[1,24,1024]{2,1,0:T(8,128)(2,1)}, u32[]{:S(2)}) copy-start(bf16[1,24,1024]{2,1,0:T(8,128)(2,1)} %param.10) | copy-start | bytes 147460
  13.1 13.5 %copy-start.6 = (bf16[1,64,768]{2,1,0:T(8,128)(2,1)S(1)}, bf16[1,64,768]{2,1,0:T(8,128)(2,1)}, u32[]{:S(2)}) copy-start(bf16[1,64,768]{2,1,0:T(8,128)(2,1)} %param.9) | copy-start | bytes 294916
  13.1 14.7 %copy-start.11 = (f32[128,4]{0,1:T(4,128)S(1)}, f32[128,4]{0,1:T(4,128)}, u32[]{:S(2)}) copy-start(f32[128,4]{0,1:T(4,128)} %param.8) | copy-start | bytes 6148
  13.1 15.7 %copy-start.8 = (bf16[128,1024]{1,0:T(8,128)(2,1)S(1)}, bf16[128,1024]{1,0:T(8,128)(2,1)}, u32[]{:S(2)}) copy-start(bf16[128,1024]{1,0:T(8,128)(2,1)} %param.11) | copy-start | bytes 786436
  13.1 63.4 %all-to-all-start = ((bf16[32,1,32,1024]{3,2,1,0:T(8,128)(2,1)}), bf16[32,1,32,1024]{3,2,1,0:T(8,128)(2,1)S(1)}, u32[]{:S(2)}, u32[]{:S(2)}) async-start(bf16[32,1,32,1024]{3,2,1,0:T(8,128)(2,1)} %bitcast.3), calls=%async_computation | async-start | bytes 4194304 | tf_op jit(solution)/shard_map/all_to_all | solution.py:104
  26.4 57.7 %all-gather.3.cloned.1.call-start = ((), (), s32[]{:S(2)}) async-start(), calls=%async_computation.6 | async-start | bytes 5013504 | tf_op jit(solution)/shard_map/all_gather | solution.py:89
  76.5 1.4 copy-start.2
  77.8 55.9 %all-to-all-start.2 = ((bf16[32,1,32,1024]{3,2,1,0:T(8,128)(2,1)}), bf16[32,1,32,1024]{3,2,1,0:T(8,128)(2,1)S(1)}, u32[]{:S(2)}, u32[]{:S(2)}) async-start(bf16[32,1,32,1024]{3,2,1,0:T(8,128)(2,1)} %bitcast.118), calls=%async_computation.2 | async-start | bytes 4194304 | tf_op jit(solution)/shard_map/all_to_all | solution.py:107
  98.4 1.7 copy-start.1
  98.5 1.7 copy-start.5
  133.8 5.2 %copy-start.4 = (bf16[1024,768,1]{1,0,2:T(8,128)(2,1)S(1)}, bf16[1024,768,1]{1,0,2:T(8,128)(2,1)}, u32[]{:S(2)}) copy-start(bf16[1024,768,1]{1,0,2:T(8,128)(2,1)} %reshape.183) | copy-start | bytes 4718596
  137.8 0.9 copy-start.12
  137.8 1.2 copy-start.13
  142.1 56.0 %all-to-all-start.3 = ((bf16[32,1,32,1024]{3,2,1,0:T(8,128)(2,1)}), bf16[32,1,32,1024]{3,2,1,0:T(8,128)(2,1)}, u32[]{:S(2)}, u32[]{:S(2)}) async-start(bf16[32,1,32,1024]{3,2,1,0:T(8,128)(2,1)} %fusion.2), calls=%async_computation.3 | async-start | bytes 4194304 | tf_op jit(solution)/shard_map/all_to_all | solution.py:133
  148.4 107.3 %reduce-scatter.2.cloned.1.call-start = ((), (), s32[]{:S(2)}) async-start(), calls=%async_computation.5 | async-start | bytes 2506752 | tf_op jit(solution)/shard_map/reduce_scatter | solution.py:126
  198.1 55.7 %all-to-all-start.1 = ((bf16[32,1,32,1024]{3,2,1,0:T(8,128)(2,1)}), bf16[32,1,32,1024]{3,2,1,0:T(8,128)(2,1)S(1)}, u32[]{:S(2)}, u32[]{:S(2)}) async-start(bf16[32,1,32,1024]{3,2,1,0:T(8,128)(2,1)} %bitcast.120), calls=%async_computation.1 | async-start | bytes 4194304 | tf_op jit(solution)/shard_map/all_to_all | solution.py:113
  204.1 49.7 %copy-start.3 = (f32[1024,128]{1,0:T(8,128)S(1)}, f32[1024,128]{1,0:T(8,128)}, u32[]{:S(2)}) copy-start(f32[1024,128]{1,0:T(8,128)} %get-tuple-element.11) | copy-start | bytes 1572868
  253.8 4.0 %copy-start.7 = (bf16[1,64,768]{2,1,0:T(8,128)(2,1)S(1)}, bf16[1,64,768]{2,1,0:T(8,128)(2,1)}, u32[]{:S(2)}) copy-start(bf16[1,64,768]{2,1,0:T(8,128)(2,1)} %param.9) | copy-start | bytes 294916
  253.8 4.7 %copy-start.10 = (bf16[1,24,1024]{2,1,0:T(8,128)(2,1)S(1)}, bf16[1,24,1024]{2,1,0:T(8,128)(2,1)}, u32[]{:S(2)}) copy-start(bf16[1,24,1024]{2,1,0:T(8,128)(2,1)} %param.10) | copy-start | bytes 147460
Sparse Core Ops, SparseCore 0:
  29.4 45.2 all-gather.2
  161.4 60.3 reduce-scatter.1

commit v3 on v2

--- a/solution.py
+++ b/solution.py
@@ -132,6 +132,10 @@
 
     inputs_back = lax.all_to_all(grad_inputs, "expert", split_axis=0, concat_axis=0, tiled=True)
 
+    new_w_in = (w_in.astype(jnp.float32) - step_rate * summed_in).astype(jnp.bfloat16)
+    new_w_down = (w_down.astype(jnp.float32) - step_rate * summed_down).astype(jnp.bfloat16)
+    inputs_back, new_w_in, new_w_down = lax.optimization_barrier((inputs_back, new_w_in, new_w_down))
+
     combine = jnp.sum(jnp.where(match, gates[None, :, :], 0.0), axis=2)
     moe_out = jnp.einsum(
         "st,sd->td",
@@ -147,8 +151,6 @@
         preferred_element_type=jnp.float32,
     ).astype(jnp.bfloat16)
 
-    new_w_in = (w_in.astype(jnp.float32) - step_rate * summed_in).astype(jnp.bfloat16)
-    new_w_down = (w_down.astype(jnp.float32) - step_rate * summed_down).astype(jnp.bfloat16)
     return (moe_out, token_grad, new_w_in, new_w_down)
 
 

time: 267 us -> 254 us (0.951)
  waiting for transfers between devices: 160 us -> 148 us
    all_to_all x1, waiting for transfers between devices: 46.9 us -> 28.8 us  [body(): lax.all_to_all(results_here, 'expert', split_axis=0, concat_axis=0, tiled...]
    reduce_scatter x1, waiting for transfers between devices: 0.01 us -> 17.8 us  [body(): summed = lax.psum_scatter(packed_g, 'dp', scatter_dimension=0, tiled=True)]
    all_to_all x1, waiting for transfers between devices: 36.8 us -> 24.9 us  [body(): lax.all_to_all(grad_inputs, 'expert', split_axis=0, concat_axis=0, tiled=...]
    unnamed x33 -> x39, local copies, waits for them, and re-layouts: 10.1 us -> 11.7 us
  transfers between devices with their start and end apart: 6 -> 6, of which waited for: 4 -> 5; matrix products, arithmetic and copies ran while one was open for 15% -> 18% of each run, Pallas kernels for 0% -> 0%
where the time goes in v3:
time: 254 us; the launch traced here: 253 us
  waiting for transfers between devices  148 us (58%)
  starting transfers between devices  31.9 us (13%)
  matrix products  26.2 us (10%)
  local copies, waits for them, and re-layouts  23 us (9%)
  between operations  14.3 us (6%)
  other arithmetic  9.5 us (4%)
    all_to_all x1, waiting for transfers between devices, body(): lax.all_to_all(send_inputs.reshape(layout), 'expert', split_axis=0, conca...  45.6 us
    all_to_all x1, waiting for transfers between devices, body(): lax.all_to_all(send_grads.reshape(layout), 'expert', split_axis=0, concat...  31.2 us
    all_to_all x1, waiting for transfers between devices, body(): lax.all_to_all(results_here, 'expert', split_axis=0, concat_axis=0, tiled...  28.8 us
    all_to_all x1, waiting for transfers between devices, body(): lax.all_to_all(grad_inputs, 'expert', split_axis=0, concat_axis=0, tiled=...  24.9 us
    reduce_scatter x1, waiting for transfers between devices, body(): summed = lax.psum_scatter(packed_g, 'dp', scatter_dimension=0, tiled=True)  17.8 us
    all_to_all x1, starting transfers between devices, body(): lax.all_to_all(send_inputs.reshape(layout), 'expert', split_axis=0, conca...  13.3 us
    unnamed x39, local copies, waits for them, and re-layouts  11.7 us
    all_to_all x1, starting transfers between devices, body(): lax.all_to_all(results_here, 'expert', split_axis=0, concat_axis=0, tiled...  6.26 us
  transfers between devices with their start and end apart: 6, of which 5 were waited for; matrix products, arithmetic and copies ran while one was open for 18% of the time, Pallas kernels for 0%

profile of v3, /device:TPU:56, one launch (start us, length us, event | category | flops | bytes accessed | tf_op | source)
XLA Modules:
  0.0 253.5 jit_solution(5129634766031706128)
XLA Ops:
  11.0 2.0 convolution_convert_fusion
  13.1 13.3 %all-to-all-start = ((bf16[32,1,32,1024]{3,2,1,0:T(8,128)(2,1)}), bf16[32,1,32,1024]{3,2,1,0:T(8,128)(2,1)S(1)}, u32[]{:S(2)}, u32[]{:S(2)}) async-start(bf16[32,1,32,1024]{3,2,1,0:T(8,128)(2,1)} %bitcast.3), calls=%async_computation | async-start | bytes 4194304 | tf_op jit(solution)/shard_map/all_to_all | solution.py:104
  28.8 2.0 multiply_convert_fusion.1
  30.8 45.6 %all-to-all-done = bf16[32,1,32,1024]{3,2,1,0:T(8,128)(2,1)S(1)} async-done(((bf16[32,1,32,1024]{3,2,1,0:T(8,128)(2,1)}), bf16[32,1,32,1024]{3,2,1,0:T(8,128)(2,1)S(1)}, u32[]{:S(2)}, u32[]{:S(2)}) %all-to-all-start) | async-done | bytes 2097184 | tf_op jit(solution)/shard_map/all_to_all | solution.py:104
  77.8 6.1 %all-to-all-start.2 = ((bf16[32,1,32,1024]{3,2,1,0:T(8,128)(2,1)}), bf16[32,1,32,1024]{3,2,1,0:T(8,128)(2,1)S(1)}, u32[]{:S(2)}, u32[]{:S(2)}) async-start(bf16[32,1,32,1024]{3,2,1,0:T(8,128)(2,1)} %bitcast.119), calls=%async_computation.2 | async-start | bytes 4194304 | tf_op jit(solution)/shard_map/all_to_all | solution.py:107
  83.9 4.9 %copy.71 = bf16[16,1,73728]{2,0,1:T(8,128)(2,1)S(1)} copy(bf16[16,1,73728]{2,1,0:T(2,128)(2,1)} %all-gather.3.cloned.1.call-done) | data formatting | bytes 4718592
  90.2 2.8 %reshape.183 = bf16[1024,768,1]{1,0,2:T(8,128)(2,1)} reshape(bf16[16,49152]{1,0:T(8,128)(2,1)} %slice.41) | data formatting | bytes 3145728 | tf_op jit(solution)/shard_map/reshape.3
  94.2 4.0 %multiply_bitcast_fusion = f32[32,1,32,768]{3,2,0,1:T(8,128)S(1)} fusion(bf16[1024,768,1]{1,0,2:T(8,128)(2,1)} %reshape.183, bf16[32,1,32,1024]{3,2,1,0:T(8,128)(2,1)} %copy-done.2), kind=kOutput, calls=%fused_computation.5 | convolution fusion | flops 1611399168 | bytes 6815744 | tf_op jit(solution)/shard_map/sxcd,xdj->sxcj/dot_general | solution.py:22
  99.9 2.6 %fusion.1 = bf16[32,1,32,1024]{3,2,0,1:T(8,128)(2,1)} fusion(bf16[384,1024,1]{1,0,2:T(8,128)(2,1)S(1)} %copy-done.6, bf16[32,1,32,384]{3,2,0,1:T(8,128)(2,1)S(1)} %fusion.16), kind=kOutput, calls=%fused_computation.10 | convolution fusion | flops 807403520 | bytes 3670016 | tf_op jit(solution)/shard_map/sxcf,xfd->sxcd/dot_general | solution.py:29
  102.5 31.2 %all-to-all-done.2 = bf16[32,1,32,1024]{3,2,1,0:T(8,128)(2,1)S(1)} async-done(((bf16[32,1,32,1024]{3,2,1,0:T(8,128)(2,1)}), bf16[32,1,32,1024]{3,2,1,0:T(8,128)(2,1)S(1)}, u32[]{:S(2)}, u32[]{:S(2)}) %all-to-all-start.2) | async-done | bytes 2097184 | tf_op jit(solution)/shard_map/all_to_all | solution.py:107
  133.7 6.3 %all-to-all-start.1 = ((bf16[32,1,32,1024]{3,2,1,0:T(8,128)(2,1)}), bf16[32,1,32,1024]{3,2,1,0:T(8,128)(2,1)}, u32[]{:S(2)}, u32[]{:S(2)}) async-start(bf16[32,1,32,1024]{3,2,1,0:T(8,128)(2,1)} %bitcast.120), calls=%async_computation.1 | async-start | bytes 4194304 | tf_op jit(solution)/shard_map/all_to_all | solution.py:113
  140.0 1.9 fusion.17
  141.9 1.5 reshape_transpose_reshape.5
  143.4 4.1 %fusion.27 = (bf16[32,32,384]{2,1,0:T(8,128)(2,1)S(1)}, bf16[32,32,384]{2,1,0:T(8,128)(2,1)S(1)}) fusion(f32[32,1,32,768]{3,2,0,1:T(8,128)} %copy-done.1, bf16[384,1024,1]{1,0,2:T(8,128)(2,1)} %reshape.184, bf16[32,1,32,1024]{3,2,1,0:T(8,128)(2,1)S(1)} %all-to-all-done.2), kind=kOutput, calls=%fused_computation.40 | convolution fusion | flops 810811392 | bytes 7602176 | tf_op jit(solution)/shard_map/sxcd,xfd->sxcf/dot_general | solution.py:38
  148.7 1.9 fusion
  150.6 1.6 reshape_transpose_reshape.4
  152.2 1.6 pad_maximum_fusion
  153.8 2.2 reshape.178
  157.6 3.1 %fusion.2 = bf16[32,1,32,1024]{3,2,1,0:T(8,128)(2,1)} fusion(bf16[1024,768,1]{1,0,2:T(8,128)(2,1)S(1)} %copy-done.5, bf16[32,32,384]{2,1,0:T(8,128)(2,1)S(1)} %copy-done.16, bf16[32,32,384]{2,1,0:T(8,128)(2,1)S(1)} %copy-done.14), kind=kOutput, calls=%fused_computation.11 | convolution fusion | flops 1615855616 | bytes 5242880 | tf_op jit(solution)/shard_map/sxcj,xdj->sxcd/dot_general | solution.py:48
  160.8 28.8 %all-to-all-done.1 = bf16[32,1,32,1024]{3,2,1,0:T(8,128)(2,1)} async-done(((bf16[32,1,32,1024]{3,2,1,0:T(8,128)(2,1)}), bf16[32,1,32,1024]{3,2,1,0:T(8,128)(2,1)}, u32[]{:S(2)}, u32[]{:S(2)}) %all-to-all-start.1) | async-done | bytes 2097184 | tf_op jit(solution)/shard_map/all_to_all | solution.py:113
  189.6 6.1 %all-to-all-start.3 = ((bf16[32,1,32,1024]{3,2,1,0:T(8,128)(2,1)}), bf16[32,1,32,1024]{3,2,1,0:T(8,128)(2,1)S(1)}, u32[]{:S(2)}, u32[]{:S(2)}) async-start(bf16[32,1,32,1024]{3,2,1,0:T(8,128)(2,1)} %fusion.2), calls=%async_computation.3 | async-start | bytes 4194304 | tf_op jit(solution)/shard_map/all_to_all | solution.py:133
  195.7 3.4 %convolution_convert_fusion.2 = bf16[128,1024]{1,0:T(8,128)(2,1)} fusion(f32[1024,128]{1,0:T(8,128)S(1)} %copy-done.4, bf16[1024,1024]{1,0:T(8,128)(2,1)} %bitcast.12), kind=kOutput, calls=%fused_computation.36 | convolution fusion | flops 1610743808 | bytes 2883584 | tf_op jit(solution)/shard_map/st,sd->td/dot_general | solution.py:140
  199.2 17.8 %reduce-scatter.2.cloned.1.call-done = bf16[8,9216]{1,0:T(8,128)(2,1)} async-done(((bf16[128,9216]{1,0:T(8,128)(2,1)}), bf16[8,9216]{1,0:T(8,128)(2,1)}) %reduce-scatter.2.cloned.1.call-update) | async-done | bytes 147472 | tf_op jit(solution)/shard_map/reduce_scatter | solution.py:126
  220.5 24.9 %all-to-all-done.3 = bf16[32,1,32,1024]{3,2,1,0:T(8,128)(2,1)S(1)} async-done(((bf16[32,1,32,1024]{3,2,1,0:T(8,128)(2,1)}), bf16[32,1,32,1024]{3,2,1,0:T(8,128)(2,1)S(1)}, u32[]{:S(2)}, u32[]{:S(2)}) %all-to-all-start.3) | async-done | bytes 2097184 | tf_op jit(solution)/shard_map/all_to_all | solution.py:133
  (70 shorter events, 19.3 us)
Async XLA Ops:
  7.2 3.9 %copy-start = (bf16[128,1024]{1,0:T(8,128)(2,1)S(1)}, bf16[128,1024]{1,0:T(8,128)(2,1)}, u32[]{:S(2)}) copy-start(bf16[128,1024]{1,0:T(8,128)(2,1)} %param.6) | copy-start | bytes 786436
  13.1 13.4 %copy-start.10 = (bf16[1,24,1024]{2,1,0:T(8,128)(2,1)S(1)}, bf16[1,24,1024]{2,1,0:T(8,128)(2,1)}, u32[]{:S(2)}) copy-start(bf16[1,24,1024]{2,1,0:T(8,128)(2,1)} %param.10) | copy-start | bytes 147460
  13.1 13.5 %copy-start.7 = (bf16[1,64,768]{2,1,0:T(8,128)(2,1)S(1)}, bf16[1,64,768]{2,1,0:T(8,128)(2,1)}, u32[]{:S(2)}) copy-start(bf16[1,64,768]{2,1,0:T(8,128)(2,1)} %param.9) | copy-start | bytes 294916
  13.1 14.7 %copy-start.12 = (f32[128,4]{0,1:T(4,128)S(1)}, f32[128,4]{0,1:T(4,128)}, u32[]{:S(2)}) copy-start(f32[128,4]{0,1:T(4,128)} %param.8) | copy-start | bytes 6148
  13.1 15.7 %copy-start.9 = (bf16[128,1024]{1,0:T(8,128)(2,1)S(1)}, bf16[128,1024]{1,0:T(8,128)(2,1)}, u32[]{:S(2)}) copy-start(bf16[128,1024]{1,0:T(8,128)(2,1)} %param.11) | copy-start | bytes 786436
  13.1 63.4 %all-to-all-start = ((bf16[32,1,32,1024]{3,2,1,0:T(8,128)(2,1)}), bf16[32,1,32,1024]{3,2,1,0:T(8,128)(2,1)S(1)}, u32[]{:S(2)}, u32[]{:S(2)}) async-start(bf16[32,1,32,1024]{3,2,1,0:T(8,128)(2,1)} %bitcast.3), calls=%async_computation | async-start | bytes 4194304 | tf_op jit(solution)/shard_map/all_to_all | solution.py:104
  26.4 57.5 %all-gather.3.cloned.1.call-start = ((), (), s32[]{:S(2)}) async-start(), calls=%async_computation.6 | async-start | bytes 5013504 | tf_op jit(solution)/shard_map/all_gather | solution.py:89
  76.4 1.3 copy-start.2
  77.8 55.9 %all-to-all-start.2 = ((bf16[32,1,32,1024]{3,2,1,0:T(8,128)(2,1)}), bf16[32,1,32,1024]{3,2,1,0:T(8,128)(2,1)S(1)}, u32[]{:S(2)}, u32[]{:S(2)}) async-start(bf16[32,1,32,1024]{3,2,1,0:T(8,128)(2,1)} %bitcast.119), calls=%async_computation.2 | async-start | bytes 4194304 | tf_op jit(solution)/shard_map/all_to_all | solution.py:107
  98.2 1.7 copy-start.1
  98.2 1.7 copy-start.6
  133.7 55.9 %all-to-all-start.1 = ((bf16[32,1,32,1024]{3,2,1,0:T(8,128)(2,1)}), bf16[32,1,32,1024]{3,2,1,0:T(8,128)(2,1)}, u32[]{:S(2)}, u32[]{:S(2)}) async-start(bf16[32,1,32,1024]{3,2,1,0:T(8,128)(2,1)} %bitcast.120), calls=%async_computation.1 | async-start | bytes 4194304 | tf_op jit(solution)/shard_map/all_to_all | solution.py:113
  139.9 77.1 %reduce-scatter.2.cloned.1.call-start = ((), (), s32[]{:S(2)}) async-start(), calls=%async_computation.5 | async-start | bytes 2506752 | tf_op jit(solution)/shard_map/reduce_scatter | solution.py:126
  143.4 5.3 %copy-start.3 = (bf16[32,1,32,1024]{3,2,1,0:T(8,128)(2,1)S(1)}, bf16[32,1,32,1024]{3,2,1,0:T(8,128)(2,1)}, u32[]{:S(2)}) copy-start(bf16[32,1,32,1024]{3,2,1,0:T(8,128)(2,1)} %copy-done.2) | copy-start | bytes 6291460
  147.5 1.0 copy-start.13
  147.5 1.2 copy-start.15
  153.8 2.2 copy-start.16
  156.0 1.4 copy-start.5
  156.0 1.6 copy-start.14
  160.8 34.9 %copy-start.4 = (f32[1024,128]{1,0:T(8,128)S(1)}, f32[1024,128]{1,0:T(8,128)}, u32[]{:S(2)}) copy-start(f32[1024,128]{1,0:T(8,128)} %get-tuple-element.17) | copy-start | bytes 1572868
  189.6 55.8 %all-to-all-start.3 = ((bf16[32,1,32,1024]{3,2,1,0:T(8,128)(2,1)}), bf16[32,1,32,1024]{3,2,1,0:T(8,128)(2,1)S(1)}, u32[]{:S(2)}, u32[]{:S(2)}) async-start(bf16[32,1,32,1024]{3,2,1,0:T(8,128)(2,1)} %fusion.2), calls=%async_computation.3 | async-start | bytes 4194304 | tf_op jit(solution)/shard_map/all_to_all | solution.py:133
  195.7 23.5 %copy-start.11 = (bf16[1,24,1024]{2,1,0:T(8,128)(2,1)S(1)}, bf16[1,24,1024]{2,1,0:T(8,128)(2,1)}, u32[]{:S(2)}) copy-start(bf16[1,24,1024]{2,1,0:T(8,128)(2,1)} %param.10) | copy-start | bytes 147460
  195.7 24.1 %copy-start.8 = (bf16[1,64,768]{2,1,0:T(8,128)(2,1)S(1)}, bf16[1,64,768]{2,1,0:T(8,128)(2,1)}, u32[]{:S(2)}) copy-start(bf16[1,64,768]{2,1,0:T(8,128)(2,1)} %param.9) | copy-start | bytes 294916
Sparse Core Ops, SparseCore 0:
  29.3 45.2 all-gather.2
  156.2 60.7 reduce-scatter.1

commit v4 on v3

--- a/solution.py
+++ b/solution.py
@@ -69,6 +69,27 @@
     )
 
 
+def gather_by_permutes(piece, owners):
+    me = lax.axis_index("dp")
+    arrived = [piece]
+    for shift in range(1, owners):
+        pairs = [(i, (i + shift) % owners) for i in range(owners)]
+        arrived.append(lax.ppermute(piece, "dp", pairs))
+    stacked = jnp.stack(arrived)
+    order = (me - jnp.arange(owners, dtype=jnp.int32)) % owners
+    return jnp.take(stacked, order, axis=0)
+
+
+def reduce_scatter_by_permutes(parts, owners):
+    me = lax.axis_index("dp")
+    rotated = jnp.take(parts, (me + jnp.arange(owners, dtype=jnp.int32)) % owners, axis=0)
+    total = rotated[0].astype(jnp.float32)
+    for shift in range(1, owners):
+        pairs = [(i, (i + shift) % owners) for i in range(owners)]
+        total = total + lax.ppermute(rotated[shift], "dp", pairs).astype(jnp.float32)
+    return total
+
+
 def body(tokens, routes, gates, w_in, w_down, out_grad):
     tok_rows, model_width = tokens.shape
     top_count = routes.shape[1]
@@ -86,7 +107,7 @@
         [w_in.reshape(1, per_device * in_size), w_down.reshape(1, per_device * down_rows * down_cols)],
         axis=1,
     )
-    gathered = lax.all_gather(packed_w, "dp", axis=0, tiled=True)
+    gathered = gather_by_permutes(packed_w[0], owners)
     full_in = from_owner_rows(gathered[:, : per_device * in_size], owners, per_device, in_rows, in_cols)
     full_down = from_owner_rows(
         gathered[:, per_device * in_size :], owners, per_device, down_rows, down_cols
@@ -122,9 +143,7 @@
         * hidden_units ** (-0.5)
     ).astype(jnp.bfloat16)
     packed_g = jnp.concatenate([to_owner_rows(grad_in, owners), to_owner_rows(grad_down, owners)], axis=1)
-    packed_g = packed_g.reshape(owners * 8, -1)
-    summed = lax.psum_scatter(packed_g, "dp", scatter_dimension=0, tiled=True)
-    summed = summed.reshape(1, -1).astype(jnp.float32)
+    summed = reduce_scatter_by_permutes(packed_g, owners).reshape(1, -1)
     summed_in = from_owner_rows(summed[:, : per_device * in_size], 1, per_device, in_rows, in_cols)
     summed_down = from_owner_rows(
         summed[:, per_device * in_size :], 1, per_device, down_rows, down_cols

time: 254 us -> 356 us (1.40); the launches traced: 253 us -> 351 us
  starting transfers between devices: 31.9 us -> 152 us
  waiting for transfers between devices: 148 us -> 98.4 us
  local copies, waits for them, and re-layouts: 23 us -> 42.2 us
  other arithmetic: 9.5 us -> 26.3 us
  between operations: 14.3 us -> 1.38 us
  matrix products: 26.2 us -> 29.9 us
    ppermute x0 -> x30, starting transfers between devices: none -> 114 us  [the longest x15 60.5 us: gather_by_permutes(): arrived.append(lax.ppermute(piece, 'dp', pairs))]
    all_to_all x1, waiting for transfers between devices: 45.6 us -> 0.01 us  [body(): lax.all_to_all(send_inputs.reshape(layout), 'expert', split_axis=0, conca...]
    all_to_all x1, waiting for transfers between devices: 28.8 us -> 0.01 us  [body(): lax.all_to_all(results_here, 'expert', split_axis=0, concat_axis=0, tiled...]
    ppermute x0 -> x30, waiting for transfers between devices: none -> 26.2 us  [the longest x15 22.1 us: reduce_scatter_by_permutes(): lax.ppermute(rotated[shift], 'dp', pairs).astype(jnp.float32)]
    another operation x3 -> x19, local copies, waits for them, and re-layouts: 4.02 us -> 27.6 us  [the longest x16 24.7 us: gather_by_permutes(): stacked = jnp.stack(arrived)]
    reduce_scatter x1 -> x0, waiting for transfers between devices: 17.8 us -> none  [body(): summed = lax.psum_scatter(packed_g, 'dp', scatter_dimension=0, tiled=True)]
    slice x0 -> x1, other arithmetic: none -> 14.6 us  [reduce_scatter_by_permutes(): rotated[shift]]
    all_to_all x1, waiting for transfers between devices: 24.9 us -> 34.7 us  [body(): lax.all_to_all(grad_inputs, 'expert', split_axis=0, concat_axis=0, tiled=...]
  transfers between devices with their start and end apart: 6 -> 34, of which waited for: 5 -> 11; matrix products, arithmetic and copies ran while one was open for 18% -> 22% of each run, Pallas kernels for 0% -> 0%
where the time goes in v4:
time: 356 us; the launch traced here: 351 us
  starting transfers between devices  152 us (43%)
  waiting for transfers between devices  98.4 us (28%)
  local copies, waits for them, and re-layouts  42.2 us (12%)
  matrix products  29.9 us (8%)
  other arithmetic  26.3 us (7%)
    ppermute x15, starting transfers between devices, gather_by_permutes(): arrived.append(lax.ppermute(piece, 'dp', pairs))  60.5 us
    ppermute x15, starting transfers between devices, reduce_scatter_by_permutes(): lax.ppermute(rotated[shift], 'dp', pairs).astype(jnp.float32)  54 us
    all_to_all x1, waiting for transfers between devices, body(): lax.all_to_all(send_grads.reshape(layout), 'expert', split_axis=0, concat...  37.6 us
    all_to_all x1, waiting for transfers between devices, body(): lax.all_to_all(grad_inputs, 'expert', split_axis=0, concat_axis=0, tiled=...  34.7 us
    another operation x16, local copies, waits for them, and re-layouts, gather_by_permutes(): stacked = jnp.stack(arrived)  24.7 us
    ppermute x15, waiting for transfers between devices, reduce_scatter_by_permutes(): lax.ppermute(rotated[shift], 'dp', pairs).astype(jnp.float32)  22.1 us
    slice x1, other arithmetic, reduce_scatter_by_permutes(): rotated[shift]  14.6 us
    all_to_all x1, starting transfers between devices, body(): lax.all_to_all(send_inputs.reshape(layout), 'expert', split_axis=0, conca...  13.4 us
  transfers between devices with their start and end apart: 34, of which 11 were waited for; matrix products, arithmetic and copies ran while one was open for 22% of the time, Pallas kernels for 0%

profile of v4, /device:TPU:56, one launch (start us, length us, event | category | flops | bytes accessed | tf_op | source)
XLA Modules:
  0.0 350.6 jit_solution(7051629833574957335)
XLA Ops:
  6.6 13.4 %all-to-all-start = ((bf16[32,1,32,1024]{3,2,1,0:T(8,128)(2,1)}), bf16[32,1,32,1024]{3,2,1,0:T(8,128)(2,1)}, u32[]{:S(2)}, u32[]{:S(2)}) async-start(bf16[32,1,32,1024]{3,2,1,0:T(8,128)(2,1)} %bitcast.2), calls=%async_computation | async-start | bytes 4194304 | tf_op jit(solution)/shard_map/all_to_all | solution.py:125
  24.0 4.3 %collective-permute-start.2 = (bf16[73728]{0:T(1024)(128)(2,1)}, bf16[73728]{0:T(1024)(128)(2,1)S(1)}, u32[]{:S(2)}, u32[]{:S(2)}) collective-permute-start(bf16[73728]{0:T(1024)(128)(2,1)} %reduce.1), channel_id=1, source_target_pairs={{0,96},{32,128},{64,160},{96,192},{128,224},{160,256},{192,288},{2... | collective-permute-start | bytes 442376 | tf_op jit(solution)/shard_map/ppermute | solution.py:77
  28.3 5.7 %collective-permute-start.3 = (bf16[73728]{0:T(1024)(128)(2,1)}, bf16[73728]{0:T(1024)(128)(2,1)S(1)}, u32[]{:S(2)}, u32[]{:S(2)}) collective-permute-start(bf16[73728]{0:T(1024)(128)(2,1)} %reduce.1), channel_id=1, source_target_pairs={{0,128},{32,160},{64,192},{96,224},{128,256},{160,288},{192,320},{... | collective-permute-start | bytes 442376 | tf_op jit(solution)/shard_map/ppermute | solution.py:77
  42.1 6.8 %collective-permute-start.6 = (bf16[73728]{0:T(1024)(128)(2,1)}, bf16[73728]{0:T(1024)(128)(2,1)S(1)}, u32[]{:S(2)}, u32[]{:S(2)}) collective-permute-start(bf16[73728]{0:T(1024)(128)(2,1)} %reduce.1), channel_id=1, source_target_pairs={{0,224},{32,256},{64,288},{96,320},{128,352},{160,384},{192,416},{... | collective-permute-start | bytes 442376 | tf_op jit(solution)/shard_map/ppermute | solution.py:77
  51.9 6.3 %collective-permute-start.8 = (bf16[73728]{0:T(1024)(128)(2,1)}, bf16[73728]{0:T(1024)(128)(2,1)S(1)}, u32[]{:S(2)}, u32[]{:S(2)}) collective-permute-start(bf16[73728]{0:T(1024)(128)(2,1)} %reduce.1), channel_id=1, source_target_pairs={{0,288},{32,320},{64,352},{96,384},{128,416},{160,448},{192,480},{... | collective-permute-start | bytes 442376 | tf_op jit(solution)/shard_map/ppermute | solution.py:77
  60.2 6.2 %collective-permute-start.10 = (bf16[73728]{0:T(1024)(128)(2,1)}, bf16[73728]{0:T(1024)(128)(2,1)S(1)}, u32[]{:S(2)}, u32[]{:S(2)}) collective-permute-start(bf16[73728]{0:T(1024)(128)(2,1)} %reduce.1), channel_id=1, source_target_pairs={{0,352},{32,384},{64,416},{96,448},{128,480},{160,0},{192,32},{224... | collective-permute-start | bytes 442376 | tf_op jit(solution)/shard_map/ppermute | solution.py:77
  68.5 9.2 %collective-permute-start.12 = (bf16[73728]{0:T(1024)(128)(2,1)}, bf16[73728]{0:T(1024)(128)(2,1)S(1)}, u32[]{:S(2)}, u32[]{:S(2)}) collective-permute-start(bf16[73728]{0:T(1024)(128)(2,1)} %reduce.1), channel_id=1, source_target_pairs={{0,416},{32,448},{64,480},{96,0},{128,32},{160,64},{192,96},{224,1... | collective-permute-start | bytes 442376 | tf_op jit(solution)/shard_map/ppermute | solution.py:77
  77.7 5.4 %collective-permute-start.13 = (bf16[73728]{0:T(1024)(128)(2,1)}, bf16[73728]{0:T(1024)(128)(2,1)S(1)}, u32[]{:S(2)}, u32[]{:S(2)}) collective-permute-start(bf16[73728]{0:T(1024)(128)(2,1)} %reduce.1), channel_id=1, source_target_pairs={{0,448},{32,480},{64,0},{96,32},{128,64},{160,96},{192,128},{224,1... | collective-permute-start | bytes 442376 | tf_op jit(solution)/shard_map/ppermute | solution.py:77
  95.8 4.0 %collective-permute-done.12 = bf16[73728]{0:T(1024)(128)(2,1)S(1)} collective-permute-done((bf16[73728]{0:T(1024)(128)(2,1)}, bf16[73728]{0:T(1024)(128)(2,1)S(1)}, u32[]{:S(2)}, u32[]{:S(2)}) %collective-permute-start.12) | collective-permute-done | bytes 147488 | tf_op jit(solution)/shard_map/ppermute | solution.py:77
  102.3 12.3 %stack.63 = bf16[16,73728]{1,0:T(8,128)(2,1)S(1)} concatenate(bf16[1,73728]{1,0:T(2,128)(2,1)S(1)} %constant_dynamic-update-slice_fusion, bf16[1,73728]{1,0:T(2,128)(2,1)S(1)} %stack.48, bf16[1,73728]{1,0:T(2,128)(2,1)} %stack.49, bf16[1,73728]{1,0:T(2,128)(2,1)} %stack.50, bf16[1,73728]{1,0:T(2,128)(2,1)} %stack.51, bf16[1,73728]{1,0:T(2,128)(2,1)} %stack.52, ...), dimensions={0} | concatenate | bytes 4718592 | tf_op jit(solution)/shard_map/stack | solution.py:78
  118.2 10.1 %all-to-all-start.2 = ((bf16[32,1,32,1024]{3,2,1,0:T(8,128)(2,1)}), bf16[32,1,32,1024]{3,2,1,0:T(8,128)(2,1)}, u32[]{:S(2)}, u32[]{:S(2)}) async-start(bf16[32,1,32,1024]{3,2,1,0:T(8,128)(2,1)} %bitcast.109), calls=%async_computation.2 | async-start | bytes 4194304 | tf_op jit(solution)/shard_map/all_to_all | solution.py:128
  140.8 37.6 %all-to-all-done.2 = bf16[32,1,32,1024]{3,2,1,0:T(8,128)(2,1)} async-done(((bf16[32,1,32,1024]{3,2,1,0:T(8,128)(2,1)}), bf16[32,1,32,1024]{3,2,1,0:T(8,128)(2,1)}, u32[]{:S(2)}, u32[]{:S(2)}) %all-to-all-start.2) | async-done | bytes 2097184 | tf_op jit(solution)/shard_map/all_to_all | solution.py:128
  186.4 8.1 %all-to-all-start.3 = ((bf16[32,1,32,1024]{3,2,1,0:T(8,128)(2,1)}), bf16[32,1,32,1024]{3,2,1,0:T(8,128)(2,1)}, u32[]{:S(2)}, u32[]{:S(2)}) async-start(bf16[32,1,32,1024]{3,2,1,0:T(8,128)(2,1)} %fusion.2), calls=%async_computation.3 | async-start | bytes 4194304 | tf_op jit(solution)/shard_map/all_to_all | solution.py:152
  209.9 34.7 %all-to-all-done.3 = bf16[32,1,32,1024]{3,2,1,0:T(8,128)(2,1)} async-done(((bf16[32,1,32,1024]{3,2,1,0:T(8,128)(2,1)}), bf16[32,1,32,1024]{3,2,1,0:T(8,128)(2,1)}, u32[]{:S(2)}, u32[]{:S(2)}) %all-to-all-start.3) | async-done | bytes 2097184 | tf_op jit(solution)/shard_map/all_to_all | solution.py:152
  244.6 6.3 %all-to-all-start.1 = ((bf16[32,1,32,1024]{3,2,1,0:T(8,128)(2,1)}), bf16[32,1,32,1024]{3,2,1,0:T(8,128)(2,1)}, u32[]{:S(2)}, u32[]{:S(2)}) async-start(bf16[32,1,32,1024]{3,2,1,0:T(8,128)(2,1)} %bitcast.110), calls=%async_computation.1 | async-start | bytes 4194304 | tf_op jit(solution)/shard_map/all_to_all | solution.py:134
  250.9 14.6 %slice_reduce_fusion.14 = (bf16[73728]{0:T(1024)(128)(2,1)S(1)}, bf16[73728]{0:T(1024)(128)(2,1)S(1)}, bf16[73728]{0:T(1024)(128)(2,1)S(1)}, bf16[73728]{0:T(102...) fusion(bf16[16,73728]{1,0:T(8,128)(2,1)S(1)} %broadcast_select_, ...), kind=kLoop, calls=%fused_computation.58 | loop fusion | flops 73728 | bytes 4866048 | tf_op jit(solution)/shard_map/slice | solution.py:89
  271.7 4.4 %collective-permute-start.26 = (bf16[73728]{0:T(1024)(128)(2,1)S(1)}, bf16[73728]{0:T(1024)(128)(2,1)S(1)}, u32[]{:S(2)}, u32[]{:S(2)}) collective-permute-start(bf16[73728]{0:T(1024)(128)(2,1)S(1)} %get-tuple-element.21), channel_id=1, source_target_pairs={{0,384},{32,416},{64,448},{96,480},{128,0},{160,32},{192,64},{224,... | collective-permute-start | bytes 442376 | tf_op jit(solution)/shard_map/ppermute | solution.py:89
  279.3 4.0 %collective-permute-start.24 = (bf16[73728]{0:T(1024)(128)(2,1)S(1)}, bf16[73728]{0:T(1024)(128)(2,1)S(1)}, u32[]{:S(2)}, u32[]{:S(2)}) collective-permute-start(bf16[73728]{0:T(1024)(128)(2,1)S(1)} %get-tuple-element.23), channel_id=1, source_target_pairs={{0,320},{32,352},{64,384},{96,416},{128,448},{160,480},{192,0},{22... | collective-permute-start | bytes 442376 | tf_op jit(solution)/shard_map/ppermute | solution.py:89
  283.3 4.8 %collective-permute-start.23 = (bf16[73728]{0:T(1024)(128)(2,1)S(1)}, bf16[73728]{0:T(1024)(128)(2,1)S(1)}, u32[]{:S(2)}, u32[]{:S(2)}) collective-permute-start(bf16[73728]{0:T(1024)(128)(2,1)S(1)} %get-tuple-element.24), channel_id=1, source_target_pairs={{0,288},{32,320},{64,352},{96,384},{128,416},{160,448},{192,480},{... | collective-permute-start | bytes 442376 | tf_op jit(solution)/shard_map/ppermute | solution.py:89
  288.2 4.7 %collective-permute-start.22 = (bf16[73728]{0:T(1024)(128)(2,1)S(1)}, bf16[73728]{0:T(1024)(128)(2,1)S(1)}, u32[]{:S(2)}, u32[]{:S(2)}) collective-permute-start(bf16[73728]{0:T(1024)(128)(2,1)S(1)} %get-tuple-element.25), channel_id=1, source_target_pairs={{0,256},{32,288},{64,320},{96,352},{128,384},{160,416},{192,448},{... | collective-permute-start | bytes 442376 | tf_op jit(solution)/shard_map/ppermute | solution.py:89
  296.7 5.9 %collective-permute-start.20 = (bf16[73728]{0:T(1024)(128)(2,1)S(1)}, bf16[73728]{0:T(1024)(128)(2,1)S(1)}, u32[]{:S(2)}, u32[]{:S(2)}) collective-permute-start(bf16[73728]{0:T(1024)(128)(2,1)S(1)} %get-tuple-element.27), channel_id=1, source_target_pairs={{0,192},{32,224},{64,256},{96,288},{128,320},{160,352},{192,384},{... | collective-permute-start | bytes 442376 | tf_op jit(solution)/shard_map/ppermute | solution.py:89
  302.6 4.8 %collective-permute-done.24 = bf16[73728]{0:T(1024)(128)(2,1)S(1)} collective-permute-done((bf16[73728]{0:T(1024)(128)(2,1)S(1)}, bf16[73728]{0:T(1024)(128)(2,1)S(1)}, u32[]{:S(2)}, u32[]{:S(2)}) %collective-permute-start.24) | collective-permute-done | bytes 147488 | tf_op jit(solution)/shard_map/ppermute | solution.py:89
  317.5 10.0 %collective-permute-start.16 = (bf16[73728]{0:T(1024)(128)(2,1)S(1)}, bf16[73728]{0:T(1024)(128)(2,1)S(1)}, u32[]{:S(2)}, u32[]{:S(2)}) collective-permute-start(bf16[73728]{0:T(1024)(128)(2,1)S(1)} %get-tuple-element.31), channel_id=1, source_target_pairs={{0,64},{32,96},{64,128},{96,160},{128,192},{160,224},{192,256},{22... | collective-permute-start | bytes 442376 | tf_op jit(solution)/shard_map/ppermute | solution.py:89
  331.0 5.9 %collective-permute-done.18 = bf16[73728]{0:T(1024)(128)(2,1)S(1)} collective-permute-done((bf16[73728]{0:T(1024)(128)(2,1)S(1)}, bf16[73728]{0:T(1024)(128)(2,1)S(1)}, u32[]{:S(2)}, u32[]{:S(2)}) %collective-permute-start.18) | collective-permute-done | bytes 147488 | tf_op jit(solution)/shard_map/ppermute | solution.py:89
  (150 shorter events, 119.6 us)
Async XLA Ops:
  6.6 111.7 %all-to-all-start = ((bf16[32,1,32,1024]{3,2,1,0:T(8,128)(2,1)}), bf16[32,1,32,1024]{3,2,1,0:T(8,128)(2,1)}, u32[]{:S(2)}, u32[]{:S(2)}) async-start(bf16[32,1,32,1024]{3,2,1,0:T(8,128)(2,1)} %bitcast.2), calls=%async_computation | async-start | bytes 4194304 | tf_op jit(solution)/shard_map/all_to_all | solution.py:125
  24.0 24.9 %collective-permute-start.2 = (bf16[73728]{0:T(1024)(128)(2,1)}, bf16[73728]{0:T(1024)(128)(2,1)S(1)}, u32[]{:S(2)}, u32[]{:S(2)}) collective-permute-start(bf16[73728]{0:T(1024)(128)(2,1)} %reduce.1), channel_id=1, source_target_pairs={{0,96},{32,128},{64,160},{96,192},{128,224},{160,256},{192,288},{2... | collective-permute-start | bytes 442376 | tf_op jit(solution)/shard_map/ppermute | solution.py:77
  28.3 23.6 %collective-permute-start.3 = (bf16[73728]{0:T(1024)(128)(2,1)}, bf16[73728]{0:T(1024)(128)(2,1)S(1)}, u32[]{:S(2)}, u32[]{:S(2)}) collective-permute-start(bf16[73728]{0:T(1024)(128)(2,1)} %reduce.1), channel_id=1, source_target_pairs={{0,128},{32,160},{64,192},{96,224},{128,256},{160,288},{192,320},{... | collective-permute-start | bytes 442376 | tf_op jit(solution)/shard_map/ppermute | solution.py:77
  34.0 24.2 %collective-permute-start.4 = (bf16[73728]{0:T(1024)(128)(2,1)}, bf16[73728]{0:T(1024)(128)(2,1)S(1)}, u32[]{:S(2)}, u32[]{:S(2)}) collective-permute-start(bf16[73728]{0:T(1024)(128)(2,1)} %reduce.1), channel_id=1, source_target_pairs={{0,160},{32,192},{64,224},{96,256},{128,288},{160,320},{192,352},{... | collective-permute-start | bytes 442376 | tf_op jit(solution)/shard_map/ppermute | solution.py:77
  42.1 24.3 %collective-permute-start.6 = (bf16[73728]{0:T(1024)(128)(2,1)}, bf16[73728]{0:T(1024)(128)(2,1)S(1)}, u32[]{:S(2)}, u32[]{:S(2)}) collective-permute-start(bf16[73728]{0:T(1024)(128)(2,1)} %reduce.1), channel_id=1, source_target_pairs={{0,224},{32,256},{64,288},{96,320},{128,352},{160,384},{192,416},{... | collective-permute-start | bytes 442376 | tf_op jit(solution)/shard_map/ppermute | solution.py:77
  51.9 25.8 %collective-permute-start.8 = (bf16[73728]{0:T(1024)(128)(2,1)}, bf16[73728]{0:T(1024)(128)(2,1)S(1)}, u32[]{:S(2)}, u32[]{:S(2)}) collective-permute-start(bf16[73728]{0:T(1024)(128)(2,1)} %reduce.1), channel_id=1, source_target_pairs={{0,288},{32,320},{64,352},{96,384},{128,416},{160,448},{192,480},{... | collective-permute-start | bytes 442376 | tf_op jit(solution)/shard_map/ppermute | solution.py:77
  58.2 24.9 %collective-permute-start.9 = (bf16[73728]{0:T(1024)(128)(2,1)}, bf16[73728]{0:T(1024)(128)(2,1)S(1)}, u32[]{:S(2)}, u32[]{:S(2)}) collective-permute-start(bf16[73728]{0:T(1024)(128)(2,1)} %reduce.1), channel_id=1, source_target_pairs={{0,320},{32,352},{64,384},{96,416},{128,448},{160,480},{192,0},{22... | collective-permute-start | bytes 442376 | tf_op jit(solution)/shard_map/ppermute | solution.py:77
  60.2 33.8 %collective-permute-start.10 = (bf16[73728]{0:T(1024)(128)(2,1)}, bf16[73728]{0:T(1024)(128)(2,1)S(1)}, u32[]{:S(2)}, u32[]{:S(2)}) collective-permute-start(bf16[73728]{0:T(1024)(128)(2,1)} %reduce.1), channel_id=1, source_target_pairs={{0,352},{32,384},{64,416},{96,448},{128,480},{160,0},{192,32},{224... | collective-permute-start | bytes 442376 | tf_op jit(solution)/shard_map/ppermute | solution.py:77
  66.4 28.4 %collective-permute-start.11 = (bf16[73728]{0:T(1024)(128)(2,1)}, bf16[73728]{0:T(1024)(128)(2,1)S(1)}, u32[]{:S(2)}, u32[]{:S(2)}) collective-permute-start(bf16[73728]{0:T(1024)(128)(2,1)} %reduce.1), channel_id=1, source_target_pairs={{0,384},{32,416},{64,448},{96,480},{128,0},{160,32},{192,64},{224,... | collective-permute-start | bytes 442376 | tf_op jit(solution)/shard_map/ppermute | solution.py:77
  68.5 31.2 %collective-permute-start.12 = (bf16[73728]{0:T(1024)(128)(2,1)}, bf16[73728]{0:T(1024)(128)(2,1)S(1)}, u32[]{:S(2)}, u32[]{:S(2)}) collective-permute-start(bf16[73728]{0:T(1024)(128)(2,1)} %reduce.1), channel_id=1, source_target_pairs={{0,416},{32,448},{64,480},{96,0},{128,32},{160,64},{192,96},{224,1... | collective-permute-start | bytes 442376 | tf_op jit(solution)/shard_map/ppermute | solution.py:77
  77.7 22.9 %collective-permute-start.13 = (bf16[73728]{0:T(1024)(128)(2,1)}, bf16[73728]{0:T(1024)(128)(2,1)S(1)}, u32[]{:S(2)}, u32[]{:S(2)}) collective-permute-start(bf16[73728]{0:T(1024)(128)(2,1)} %reduce.1), channel_id=1, source_target_pairs={{0,448},{32,480},{64,0},{96,32},{128,64},{160,96},{192,128},{224,1... | collective-permute-start | bytes 442376 | tf_op jit(solution)/shard_map/ppermute | solution.py:77
  118.2 60.1 %all-to-all-start.2 = ((bf16[32,1,32,1024]{3,2,1,0:T(8,128)(2,1)}), bf16[32,1,32,1024]{3,2,1,0:T(8,128)(2,1)}, u32[]{:S(2)}, u32[]{:S(2)}) async-start(bf16[32,1,32,1024]{3,2,1,0:T(8,128)(2,1)} %bitcast.109), calls=%async_computation.2 | async-start | bytes 4194304 | tf_op jit(solution)/shard_map/all_to_all | solution.py:128
  186.4 58.2 %all-to-all-start.3 = ((bf16[32,1,32,1024]{3,2,1,0:T(8,128)(2,1)}), bf16[32,1,32,1024]{3,2,1,0:T(8,128)(2,1)}, u32[]{:S(2)}, u32[]{:S(2)}) async-start(bf16[32,1,32,1024]{3,2,1,0:T(8,128)(2,1)} %fusion.2), calls=%async_computation.3 | async-start | bytes 4194304 | tf_op jit(solution)/shard_map/all_to_all | solution.py:152
  244.6 102.6 %all-to-all-start.1 = ((bf16[32,1,32,1024]{3,2,1,0:T(8,128)(2,1)}), bf16[32,1,32,1024]{3,2,1,0:T(8,128)(2,1)}, u32[]{:S(2)}, u32[]{:S(2)}) async-start(bf16[32,1,32,1024]{3,2,1,0:T(8,128)(2,1)} %bitcast.110), calls=%async_computation.1 | async-start | bytes 4194304 | tf_op jit(solution)/shard_map/all_to_all | solution.py:134
  271.7 21.2 %collective-permute-start.26 = (bf16[73728]{0:T(1024)(128)(2,1)S(1)}, bf16[73728]{0:T(1024)(128)(2,1)S(1)}, u32[]{:S(2)}, u32[]{:S(2)}) collective-permute-start(bf16[73728]{0:T(1024)(128)(2,1)S(1)} %get-tuple-element.21), channel_id=1, source_target_pairs={{0,384},{32,416},{64,448},{96,480},{128,0},{160,32},{192,64},{224,... | collective-permute-start | bytes 442376 | tf_op jit(solution)/shard_map/ppermute | solution.py:89
  279.3 28.1 %collective-permute-start.24 = (bf16[73728]{0:T(1024)(128)(2,1)S(1)}, bf16[73728]{0:T(1024)(128)(2,1)S(1)}, u32[]{:S(2)}, u32[]{:S(2)}) collective-permute-start(bf16[73728]{0:T(1024)(128)(2,1)S(1)} %get-tuple-element.23), channel_id=1, source_target_pairs={{0,320},{32,352},{64,384},{96,416},{128,448},{160,480},{192,0},{22... | collective-permute-start | bytes 442376 | tf_op jit(solution)/shard_map/ppermute | solution.py:89
  283.3 28.5 %collective-permute-start.23 = (bf16[73728]{0:T(1024)(128)(2,1)S(1)}, bf16[73728]{0:T(1024)(128)(2,1)S(1)}, u32[]{:S(2)}, u32[]{:S(2)}) collective-permute-start(bf16[73728]{0:T(1024)(128)(2,1)S(1)} %get-tuple-element.24), channel_id=1, source_target_pairs={{0,288},{32,320},{64,352},{96,384},{128,416},{160,448},{192,480},{... | collective-permute-start | bytes 442376 | tf_op jit(solution)/shard_map/ppermute | solution.py:89
  288.2 27.4 %collective-permute-start.22 = (bf16[73728]{0:T(1024)(128)(2,1)S(1)}, bf16[73728]{0:T(1024)(128)(2,1)S(1)}, u32[]{:S(2)}, u32[]{:S(2)}) collective-permute-start(bf16[73728]{0:T(1024)(128)(2,1)S(1)} %get-tuple-element.25), channel_id=1, source_target_pairs={{0,256},{32,288},{64,320},{96,352},{128,384},{160,416},{192,448},{... | collective-permute-start | bytes 442376 | tf_op jit(solution)/shard_map/ppermute | solution.py:89
  292.9 24.6 %collective-permute-start.21 = (bf16[73728]{0:T(1024)(128)(2,1)S(1)}, bf16[73728]{0:T(1024)(128)(2,1)S(1)}, u32[]{:S(2)}, u32[]{:S(2)}) collective-permute-start(bf16[73728]{0:T(1024)(128)(2,1)S(1)} %get-tuple-element.26), channel_id=1, source_target_pairs={{0,224},{32,256},{64,288},{96,320},{128,352},{160,384},{192,416},{... | collective-permute-start | bytes 442376 | tf_op jit(solution)/shard_map/ppermute | solution.py:89
  296.7 30.9 %collective-permute-start.20 = (bf16[73728]{0:T(1024)(128)(2,1)S(1)}, bf16[73728]{0:T(1024)(128)(2,1)S(1)}, u32[]{:S(2)}, u32[]{:S(2)}) collective-permute-start(bf16[73728]{0:T(1024)(128)(2,1)S(1)} %get-tuple-element.27), channel_id=1, source_target_pairs={{0,192},{32,224},{64,256},{96,288},{128,320},{160,352},{192,384},{... | collective-permute-start | bytes 442376 | tf_op jit(solution)/shard_map/ppermute | solution.py:89
  307.4 23.6 %collective-permute-start.19 = (bf16[73728]{0:T(1024)(128)(2,1)S(1)}, bf16[73728]{0:T(1024)(128)(2,1)S(1)}, u32[]{:S(2)}, u32[]{:S(2)}) collective-permute-start(bf16[73728]{0:T(1024)(128)(2,1)S(1)} %get-tuple-element.28), channel_id=1, source_target_pairs={{0,160},{32,192},{64,224},{96,256},{128,288},{160,320},{192,352},{... | collective-permute-start | bytes 442376 | tf_op jit(solution)/shard_map/ppermute | solution.py:89
  311.8 25.0 %collective-permute-start.18 = (bf16[73728]{0:T(1024)(128)(2,1)S(1)}, bf16[73728]{0:T(1024)(128)(2,1)S(1)}, u32[]{:S(2)}, u32[]{:S(2)}) collective-permute-start(bf16[73728]{0:T(1024)(128)(2,1)S(1)} %get-tuple-element.29), channel_id=1, source_target_pairs={{0,128},{32,160},{64,192},{96,224},{128,256},{160,288},{192,320},{... | collective-permute-start | bytes 442376 | tf_op jit(solution)/shard_map/ppermute | solution.py:89
  315.6 22.2 %collective-permute-start.17 = (bf16[73728]{0:T(1024)(128)(2,1)S(1)}, bf16[73728]{0:T(1024)(128)(2,1)S(1)}, u32[]{:S(2)}, u32[]{:S(2)}) collective-permute-start(bf16[73728]{0:T(1024)(128)(2,1)S(1)} %get-tuple-element.30), channel_id=1, source_target_pairs={{0,96},{32,128},{64,160},{96,192},{128,224},{160,256},{192,288},{2... | collective-permute-start | bytes 442376 | tf_op jit(solution)/shard_map/ppermute | solution.py:89
  317.5 23.1 %collective-permute-start.16 = (bf16[73728]{0:T(1024)(128)(2,1)S(1)}, bf16[73728]{0:T(1024)(128)(2,1)S(1)}, u32[]{:S(2)}, u32[]{:S(2)}) collective-permute-start(bf16[73728]{0:T(1024)(128)(2,1)S(1)} %get-tuple-element.31), channel_id=1, source_target_pairs={{0,64},{32,96},{64,128},{96,160},{128,192},{160,224},{192,256},{22... | collective-permute-start | bytes 442376 | tf_op jit(solution)/shard_map/ppermute | solution.py:89
  (28 other events, 436.3 us)

commit v5 on v3

--- a/solution.py
+++ b/solution.py
@@ -4,16 +4,6 @@
 from jax.sharding import PartitionSpec as P
 
 step_rate = 0.5
-
-
-def slot_numbers(route_rows, experts, capacity):
-    flat_routes = route_rows.reshape(-1)
-    one_hot = (flat_routes[:, None] == jnp.arange(experts, dtype=jnp.int32)[None, :]).astype(
-        jnp.int32
-    )
-    running = jnp.cumsum(one_hot, axis=0)
-    position = jnp.sum(one_hot * running, axis=1) - 1
-    return flat_routes * capacity + position
 
 
 def expert_forward(inputs, full_in, full_down):
@@ -92,10 +82,19 @@
         gathered[:, per_device * in_size :], owners, per_device, down_rows, down_cols
     )
 
-    slot_index = slot_numbers(routes, experts, capacity).reshape(tok_rows, top_count)
-    match = slot_index[None, :, :] == jnp.arange(total, dtype=jnp.int32)[:, None, None]
-    pick = jnp.any(match, axis=2).astype(jnp.bfloat16)
-    gate_of_slot = jnp.sum(jnp.where(match, gates[None, :, :], 0.0), axis=(1, 2))
+    named = routes[:, :, None] == jnp.arange(experts, dtype=jnp.int32)[None, None, :]
+    routed = jnp.any(named, axis=1)
+    gate_of = jnp.sum(jnp.where(named, gates[:, :, None], 0.0), axis=1)
+    earlier = (
+        jnp.arange(tok_rows, dtype=jnp.int32)[:, None] > jnp.arange(tok_rows, dtype=jnp.int32)[None, :]
+    ).astype(jnp.bfloat16)
+    rank = jnp.dot(earlier, routed.astype(jnp.bfloat16), preferred_element_type=jnp.float32)
+    in_slot = routed.T[:, None, :] & (
+        rank.T[:, None, :] == jnp.arange(capacity, dtype=jnp.float32)[None, :, None]
+    )
+    slot_gate = jnp.where(in_slot, gate_of.T[:, None, :], 0.0).reshape(total, tok_rows)
+    pick = in_slot.reshape(total, tok_rows).astype(jnp.bfloat16)
+    gate_of_slot = jnp.sum(slot_gate, axis=1)
     layout = (sources, per_device, capacity, model_width)
     send_inputs = jnp.dot(pick, tokens, preferred_element_type=jnp.float32).astype(jnp.bfloat16)
     grad_of_slot = jnp.dot(pick, out_grad, preferred_element_type=jnp.float32)
@@ -136,10 +135,9 @@
     new_w_down = (w_down.astype(jnp.float32) - step_rate * summed_down).astype(jnp.bfloat16)
     inputs_back, new_w_in, new_w_down = lax.optimization_barrier((inputs_back, new_w_in, new_w_down))
 
-    combine = jnp.sum(jnp.where(match, gates[None, :, :], 0.0), axis=2)
     moe_out = jnp.einsum(
         "st,sd->td",
-        combine,
+        slot_gate,
         results_home.reshape(total, model_width).astype(jnp.float32),
         precision=lax.Precision.HIGHEST,
         preferred_element_type=jnp.float32,

time: 254 us -> 252 us (level)
    another operation x3 -> x1, local copies, waits for them, and re-layouts: 4.02 us -> 1.25 us
    reshape x0 -> x1, local copies, waits for them, and re-layouts: none -> 2.76 us
    unnamed x39 -> x44, local copies, waits for them, and re-layouts: 11.7 us -> 10.8 us
  transfers between devices with their start and end apart: 6 -> 6, of which waited for: 5 -> 5; matrix products, arithmetic and copies ran while one was open for 18% -> 19% of each run, Pallas kernels for 0% -> 0%
where the time goes in v5:
time: 252 us; the launch traced here: 251 us
  waiting for transfers between devices  148 us (59%)
  starting transfers between devices  32.1 us (13%)
  matrix products  26.5 us (11%)
  local copies, waits for them, and re-layouts  21.8 us (9%)
  between operations  14.4 us (6%)
  other arithmetic  8.09 us (3%)
    all_to_all x1, waiting for transfers between devices, body(): lax.all_to_all(send_inputs.reshape(layout), 'expert', split_axis=0, conca...  45.6 us
    all_to_all x1, waiting for transfers between devices, body(): lax.all_to_all(send_grads.reshape(layout), 'expert', split_axis=0, concat...  31.1 us
    all_to_all x1, waiting for transfers between devices, body(): lax.all_to_all(results_here, 'expert', split_axis=0, concat_axis=0, tiled...  28.6 us
    all_to_all x1, waiting for transfers between devices, body(): lax.all_to_all(grad_inputs, 'expert', split_axis=0, concat_axis=0, tiled=...  24.7 us
    reduce_scatter x1, waiting for transfers between devices, body(): summed = lax.psum_scatter(packed_g, 'dp', scatter_dimension=0, tiled=True)  18 us
    all_to_all x1, starting transfers between devices, body(): lax.all_to_all(send_inputs.reshape(layout), 'expert', split_axis=0, conca...  13.3 us
    unnamed x44, local copies, waits for them, and re-layouts  10.8 us
    all_to_all x1, starting transfers between devices, body(): lax.all_to_all(results_here, 'expert', split_axis=0, concat_axis=0, tiled...  6.26 us
  transfers between devices with their start and end apart: 6, of which 5 were waited for; matrix products, arithmetic and copies ran while one was open for 19% of the time, Pallas kernels for 0%

profile of v5, /device:TPU:56, one launch (start us, length us, event | category | flops | bytes accessed | tf_op | source)
XLA Modules:
  0.0 250.9 jit_solution(6241190906361734122)
XLA Ops:
  8.4 2.1 convolution_convert_fusion
  10.5 13.3 %all-to-all-start = ((bf16[32,1,32,1024]{3,2,1,0:T(8,128)(2,1)}), bf16[32,1,32,1024]{3,2,1,0:T(8,128)(2,1)S(1)}, u32[]{:S(2)}, u32[]{:S(2)}) async-start(bf16[32,1,32,1024]{3,2,1,0:T(8,128)(2,1)} %bitcast.7), calls=%async_computation | async-start | bytes 4194304 | tf_op jit(solution)/shard_map/all_to_all | solution.py:103
  26.2 2.0 multiply_convert_fusion.1
  28.2 45.6 %all-to-all-done = bf16[32,1,32,1024]{3,2,1,0:T(8,128)(2,1)S(1)} async-done(((bf16[32,1,32,1024]{3,2,1,0:T(8,128)(2,1)}), bf16[32,1,32,1024]{3,2,1,0:T(8,128)(2,1)S(1)}, u32[]{:S(2)}, u32[]{:S(2)}) %all-to-all-start) | async-done | bytes 2097184 | tf_op jit(solution)/shard_map/all_to_all | solution.py:103
  75.2 6.1 %all-to-all-start.2 = ((bf16[32,1,32,1024]{3,2,1,0:T(8,128)(2,1)}), bf16[32,1,32,1024]{3,2,1,0:T(8,128)(2,1)S(1)}, u32[]{:S(2)}, u32[]{:S(2)}) async-start(bf16[32,1,32,1024]{3,2,1,0:T(8,128)(2,1)} %bitcast.115), calls=%async_computation.2 | async-start | bytes 4194304 | tf_op jit(solution)/shard_map/all_to_all | solution.py:106
  81.4 4.9 %copy.44 = bf16[16,1,73728]{2,0,1:T(8,128)(2,1)S(1)} copy(bf16[16,1,73728]{2,1,0:T(2,128)(2,1)} %all-gather.3.cloned.1.call-done) | data formatting | bytes 4718592
  87.6 2.8 %reshape.244 = bf16[1024,768,1]{1,0,2:T(8,128)(2,1)} reshape(bf16[16,49152]{1,0:T(8,128)(2,1)} %slice.32) | data formatting | bytes 3145728 | tf_op jit(solution)/shard_map/reshape
  91.6 4.0 %multiply_bitcast_fusion = f32[32,1,32,768]{3,2,0,1:T(8,128)S(1)} fusion(bf16[1024,768,1]{1,0,2:T(8,128)(2,1)} %reshape.244, bf16[32,1,32,1024]{3,2,1,0:T(8,128)(2,1)} %copy-done.2), kind=kOutput, calls=%fused_computation.5 | convolution fusion | flops 1611399168 | bytes 6815744 | tf_op jit(solution)/shard_map/sxcd,xdj->sxcj/dot_general | solution.py:12
  97.4 2.6 %fusion.1 = bf16[32,1,32,1024]{3,2,0,1:T(8,128)(2,1)} fusion(bf16[384,1024,1]{1,0,2:T(8,128)(2,1)S(1)} %copy-done.6, bf16[32,1,32,384]{3,2,0,1:T(8,128)(2,1)S(1)} %fusion.15), kind=kOutput, calls=%fused_computation.8 | convolution fusion | flops 807403520 | bytes 3670016 | tf_op jit(solution)/shard_map/sxcf,xfd->sxcd/dot_general | solution.py:19
  100.0 31.1 %all-to-all-done.2 = bf16[32,1,32,1024]{3,2,1,0:T(8,128)(2,1)S(1)} async-done(((bf16[32,1,32,1024]{3,2,1,0:T(8,128)(2,1)}), bf16[32,1,32,1024]{3,2,1,0:T(8,128)(2,1)S(1)}, u32[]{:S(2)}, u32[]{:S(2)}) %all-to-all-start.2) | async-done | bytes 2097184 | tf_op jit(solution)/shard_map/all_to_all | solution.py:106
  131.1 6.3 %all-to-all-start.1 = ((bf16[32,1,32,1024]{3,2,1,0:T(8,128)(2,1)}), bf16[32,1,32,1024]{3,2,1,0:T(8,128)(2,1)}, u32[]{:S(2)}, u32[]{:S(2)}) async-start(bf16[32,1,32,1024]{3,2,1,0:T(8,128)(2,1)} %bitcast.116), calls=%async_computation.1 | async-start | bytes 4194304 | tf_op jit(solution)/shard_map/all_to_all | solution.py:112
  137.6 1.9 fusion.16
  139.5 1.5 reshape_transpose_reshape.5
  141.0 4.1 %fusion.26 = (bf16[32,32,384]{2,1,0:T(8,128)(2,1)S(1)}, bf16[32,32,384]{2,1,0:T(8,128)(2,1)S(1)}) fusion(f32[32,1,32,768]{3,2,0,1:T(8,128)} %copy-done.1, bf16[384,1024,1]{1,0,2:T(8,128)(2,1)} %reshape.245, bf16[32,1,32,1024]{3,2,1,0:T(8,128)(2,1)S(1)} %all-to-all-done.2), kind=kOutput, calls=%fused_computation.36 | convolution fusion | flops 810811392 | bytes 7602176 | tf_op jit(solution)/shard_map/sxcd,xfd->sxcf/dot_general | solution.py:28
  146.3 1.9 fusion
  148.2 1.6 reshape_transpose_reshape.4
  149.9 1.6 pad_maximum_fusion
  151.4 2.2 reshape.239
  155.3 3.1 %fusion.2 = bf16[32,1,32,1024]{3,2,1,0:T(8,128)(2,1)} fusion(bf16[1024,768,1]{1,0,2:T(8,128)(2,1)S(1)} %copy-done.5, bf16[32,32,384]{2,1,0:T(8,128)(2,1)S(1)} %copy-done.19, bf16[32,32,384]{2,1,0:T(8,128)(2,1)S(1)} %copy-done.17), kind=kOutput, calls=%fused_computation.9 | convolution fusion | flops 1615855616 | bytes 5242880 | tf_op jit(solution)/shard_map/sxcj,xdj->sxcd/dot_general | solution.py:38
  158.4 28.6 %all-to-all-done.1 = bf16[32,1,32,1024]{3,2,1,0:T(8,128)(2,1)} async-done(((bf16[32,1,32,1024]{3,2,1,0:T(8,128)(2,1)}), bf16[32,1,32,1024]{3,2,1,0:T(8,128)(2,1)}, u32[]{:S(2)}, u32[]{:S(2)}) %all-to-all-start.1) | async-done | bytes 2097184 | tf_op jit(solution)/shard_map/all_to_all | solution.py:112
  187.0 6.1 %all-to-all-start.3 = ((bf16[32,1,32,1024]{3,2,1,0:T(8,128)(2,1)}), bf16[32,1,32,1024]{3,2,1,0:T(8,128)(2,1)S(1)}, u32[]{:S(2)}, u32[]{:S(2)}) async-start(bf16[32,1,32,1024]{3,2,1,0:T(8,128)(2,1)} %fusion.2), calls=%async_computation.3 | async-start | bytes 4194304 | tf_op jit(solution)/shard_map/all_to_all | solution.py:132
  193.3 3.4 %convolution_convert_fusion.2 = bf16[128,1024]{1,0:T(8,128)(2,1)} fusion(f32[1024,128]{1,0:T(8,128)S(1)} %bitcast.117, bf16[1024,1024]{1,0:T(8,128)(2,1)} %bitcast.16), kind=kOutput, calls=%fused_computation.32 | convolution fusion | flops 1610743808 | bytes 2883584 | tf_op jit(solution)/shard_map/st,sd->td/dot_general | solution.py:138
  196.7 18.0 %reduce-scatter.2.cloned.1.call-done = bf16[8,9216]{1,0:T(8,128)(2,1)} async-done(((bf16[128,9216]{1,0:T(8,128)(2,1)}), bf16[8,9216]{1,0:T(8,128)(2,1)}) %reduce-scatter.2.cloned.1.call-update) | async-done | bytes 147472 | tf_op jit(solution)/shard_map/reduce_scatter | solution.py:125
  218.1 24.7 %all-to-all-done.3 = bf16[32,1,32,1024]{3,2,1,0:T(8,128)(2,1)S(1)} async-done(((bf16[32,1,32,1024]{3,2,1,0:T(8,128)(2,1)}), bf16[32,1,32,1024]{3,2,1,0:T(8,128)(2,1)S(1)}, u32[]{:S(2)}, u32[]{:S(2)}) %all-to-all-start.3) | async-done | bytes 2097184 | tf_op jit(solution)/shard_map/all_to_all | solution.py:132
  (70 shorter events, 16.9 us)
Async XLA Ops:
  7.2 1.2 copy-start
  7.9 17.3 %copy-start.12 = (pred[128,32]{0,1:T(8,128)(4,1)}, pred[128,32]{0,1:T(8,128)(4,1)S(1)}, u32[]{:S(2)}) copy-start(pred[128,32]{0,1:T(8,128)(4,1)S(1)} %fusion.32) | copy-start | bytes 12292
  8.1 17.1 %copy-start.10 = (f32[32,128]{1,0:T(8,128)}, f32[32,128]{1,0:T(8,128)S(1)}, u32[]{:S(2)}) copy-start(f32[32,128]{1,0:T(8,128)S(1)} %fusion.33) | copy-start | bytes 49156
  10.5 13.4 %copy-start.9 = (bf16[1,24,1024]{2,1,0:T(8,128)(2,1)S(1)}, bf16[1,24,1024]{2,1,0:T(8,128)(2,1)}, u32[]{:S(2)}) copy-start(bf16[1,24,1024]{2,1,0:T(8,128)(2,1)} %param.10) | copy-start | bytes 147460
  10.5 13.5 %copy-start.7 = (bf16[1,64,768]{2,1,0:T(8,128)(2,1)S(1)}, bf16[1,64,768]{2,1,0:T(8,128)(2,1)}, u32[]{:S(2)}) copy-start(bf16[1,64,768]{2,1,0:T(8,128)(2,1)} %param.9) | copy-start | bytes 294916
  10.5 14.7 %copy-start.14 = (s32[128,4]{0,1:T(4,128)S(1)}, s32[128,4]{0,1:T(4,128)}, u32[]{:S(2)}) copy-start(s32[128,4]{0,1:T(4,128)} %param.7) | copy-start | bytes 6148
  10.5 14.7 %copy-start.15 = (f32[128,4]{0,1:T(4,128)S(1)}, f32[128,4]{0,1:T(4,128)}, u32[]{:S(2)}) copy-start(f32[128,4]{0,1:T(4,128)} %param.8) | copy-start | bytes 6148
  10.5 15.7 %copy-start.8 = (bf16[128,1024]{1,0:T(8,128)(2,1)S(1)}, bf16[128,1024]{1,0:T(8,128)(2,1)}, u32[]{:S(2)}) copy-start(bf16[128,1024]{1,0:T(8,128)(2,1)} %param.11) | copy-start | bytes 786436
  10.5 63.4 %all-to-all-start = ((bf16[32,1,32,1024]{3,2,1,0:T(8,128)(2,1)}), bf16[32,1,32,1024]{3,2,1,0:T(8,128)(2,1)S(1)}, u32[]{:S(2)}, u32[]{:S(2)}) async-start(bf16[32,1,32,1024]{3,2,1,0:T(8,128)(2,1)} %bitcast.7), calls=%async_computation | async-start | bytes 4194304 | tf_op jit(solution)/shard_map/all_to_all | solution.py:103
  23.8 57.6 %all-gather.3.cloned.1.call-start = ((), (), s32[]{:S(2)}) async-start(), calls=%async_computation.6 | async-start | bytes 5013504 | tf_op jit(solution)/shard_map/all_gather | solution.py:79
  73.8 1.4 copy-start.2
  75.2 55.9 %all-to-all-start.2 = ((bf16[32,1,32,1024]{3,2,1,0:T(8,128)(2,1)}), bf16[32,1,32,1024]{3,2,1,0:T(8,128)(2,1)S(1)}, u32[]{:S(2)}, u32[]{:S(2)}) async-start(bf16[32,1,32,1024]{3,2,1,0:T(8,128)(2,1)} %bitcast.115), calls=%async_computation.2 | async-start | bytes 4194304 | tf_op jit(solution)/shard_map/all_to_all | solution.py:106
  95.6 1.7 copy-start.1
  95.6 1.7 copy-start.6
  131.1 55.9 %all-to-all-start.1 = ((bf16[32,1,32,1024]{3,2,1,0:T(8,128)(2,1)}), bf16[32,1,32,1024]{3,2,1,0:T(8,128)(2,1)}, u32[]{:S(2)}, u32[]{:S(2)}) async-start(bf16[32,1,32,1024]{3,2,1,0:T(8,128)(2,1)} %bitcast.116), calls=%async_computation.1 | async-start | bytes 4194304 | tf_op jit(solution)/shard_map/all_to_all | solution.py:112
  137.4 77.3 %reduce-scatter.2.cloned.1.call-start = ((), (), s32[]{:S(2)}) async-start(), calls=%async_computation.5 | async-start | bytes 2506752 | tf_op jit(solution)/shard_map/reduce_scatter | solution.py:125
  141.0 5.3 %copy-start.3 = (bf16[32,1,32,1024]{3,2,1,0:T(8,128)(2,1)S(1)}, bf16[32,1,32,1024]{3,2,1,0:T(8,128)(2,1)}, u32[]{:S(2)}) copy-start(bf16[32,1,32,1024]{3,2,1,0:T(8,128)(2,1)} %copy-done.2) | copy-start | bytes 6291460
  151.4 2.3 copy-start.19
  153.7 1.4 copy-start.5
  153.7 1.6 copy-start.17
  158.4 34.7 %copy-start.11 = (f32[32,128]{1,0:T(8,128)S(1)}, f32[32,128]{1,0:T(8,128)}, u32[]{:S(2)}) copy-start(f32[32,128]{1,0:T(8,128)} %copy-done.10) | copy-start | bytes 49156
  158.4 34.7 %copy-start.13 = (pred[128,32]{0,1:T(8,128)(4,1)S(1)}, pred[128,32]{0,1:T(8,128)(4,1)}, u32[]{:S(2)}) copy-start(pred[128,32]{0,1:T(8,128)(4,1)} %copy-done.12) | copy-start | bytes 12292
  158.4 34.9 %copy-start.4 = (f32[32,32,128]{2,1,0:T(8,128)S(1)}, f32[32,32,128]{2,1,0:T(8,128)}, u32[]{:S(2)}) copy-start(f32[32,32,128]{2,1,0:T(8,128)} %get-tuple-element.19) | copy-start | bytes 1572868
  187.0 55.8 %all-to-all-start.3 = ((bf16[32,1,32,1024]{3,2,1,0:T(8,128)(2,1)}), bf16[32,1,32,1024]{3,2,1,0:T(8,128)(2,1)S(1)}, u32[]{:S(2)}, u32[]{:S(2)}) async-start(bf16[32,1,32,1024]{3,2,1,0:T(8,128)(2,1)} %fusion.2), calls=%async_computation.3 | async-start | bytes 4194304 | tf_op jit(solution)/shard_map/all_to_all | solution.py:132
  (2 other events, 2.1 us)
Sparse Core Ops, SparseCore 0:
  26.8 45.2 all-gather.2
  153.8 60.8 reduce-scatter.1

commit v6 on v5

--- a/solution.py
+++ b/solution.py
@@ -93,7 +93,7 @@
         rank.T[:, None, :] == jnp.arange(capacity, dtype=jnp.float32)[None, :, None]
     )
     slot_gate = jnp.where(in_slot, gate_of.T[:, None, :], 0.0).reshape(total, tok_rows)
-    pick = in_slot.reshape(total, tok_rows).astype(jnp.bfloat16)
+    pick = lax.optimization_barrier(in_slot.reshape(total, tok_rows).astype(jnp.bfloat16))
     gate_of_slot = jnp.sum(slot_gate, axis=1)
     layout = (sources, per_device, capacity, model_width)
     send_inputs = jnp.dot(pick, tokens, preferred_element_type=jnp.float32).astype(jnp.bfloat16)

time: 252 us -> 252 us (level)
  waiting for transfers between devices: 148 us -> 142 us
  local copies, waits for them, and re-layouts: 21.8 us -> 25.3 us
  matrix products: 26.5 us -> 29.8 us
    all_to_all x1, waiting for transfers between devices: 28.6 us -> 25.3 us  [body(): lax.all_to_all(results_here, 'expert', split_axis=0, concat_axis=0, tiled...]
    all_to_all x1, waiting for transfers between devices: 31.1 us -> 28.3 us  [body(): lax.all_to_all(send_grads.reshape(layout), 'expert', split_axis=0, concat...]
    unnamed x44 -> x32, local copies, waits for them, and re-layouts: 10.8 us -> 11.6 us
  transfers between devices with their start and end apart: 6 -> 6, of which waited for: 5 -> 5; matrix products, arithmetic and copies ran while one was open for 19% -> 21% of each run, Pallas kernels for 0% -> 0%
where the time goes in v6:
time: 252 us; the launch traced here: 251 us
  waiting for transfers between devices  142 us (56%)
  starting transfers between devices  32.1 us (13%)
  matrix products  29.8 us (12%)
  local copies, waits for them, and re-layouts  25.3 us (10%)
  between operations  14.3 us (6%)
  other arithmetic  7.56 us (3%)
    all_to_all x1, waiting for transfers between devices, body(): lax.all_to_all(send_inputs.reshape(layout), 'expert', split_axis=0, conca...  45.3 us
    all_to_all x1, waiting for transfers between devices, body(): lax.all_to_all(send_grads.reshape(layout), 'expert', split_axis=0, concat...  28.3 us
    all_to_all x1, waiting for transfers between devices, body(): lax.all_to_all(results_here, 'expert', split_axis=0, concat_axis=0, tiled...  25.3 us
    all_to_all x1, waiting for transfers between devices, body(): lax.all_to_all(grad_inputs, 'expert', split_axis=0, concat_axis=0, tiled=...  22.9 us
    reduce_scatter x1, waiting for transfers between devices, body(): summed = lax.psum_scatter(packed_g, 'dp', scatter_dimension=0, tiled=True)  19.9 us
    all_to_all x1, starting transfers between devices, body(): lax.all_to_all(send_inputs.reshape(layout), 'expert', split_axis=0, conca...  13.3 us
    unnamed x32, local copies, waits for them, and re-layouts  11.6 us
    all_to_all x1, starting transfers between devices, body(): lax.all_to_all(results_here, 'expert', split_axis=0, concat_axis=0, tiled...  6.26 us
  transfers between devices with their start and end apart: 6, of which 5 were waited for; matrix products, arithmetic and copies ran while one was open for 21% of the time, Pallas kernels for 0%

profile of v6, /device:TPU:56, one launch (start us, length us, event | category | flops | bytes accessed | tf_op | source)
XLA Modules:
  0.0 250.9 jit_solution(5327136570781952103)
XLA Ops:
  8.4 2.1 convolution_convert_fusion
  10.5 13.3 %all-to-all-start = ((bf16[32,1,32,1024]{3,2,1,0:T(8,128)(2,1)}), bf16[32,1,32,1024]{3,2,1,0:T(8,128)(2,1)S(1)}, u32[]{:S(2)}, u32[]{:S(2)}) async-start(bf16[32,1,32,1024]{3,2,1,0:T(8,128)(2,1)} %bitcast.7), calls=%async_computation | async-start | bytes 4194304 | tf_op jit(solution)/shard_map/all_to_all | solution.py:103
  25.5 3.0 %multiply_convert_fusion.1 = bf16[1024,1024]{1,0:T(8,128)(2,1)} fusion(bf16[1024,128]{1,0:T(8,128)(2,1)S(1)} %fusion.30, bf16[128,1024]{1,0:T(8,128)(2,1)} %param.11, f32[1024]{0:T(1024)S(1)} %mul.131), kind=kOutput, calls=%fused_computation.1 | convolution fusion | flops 270532608 | bytes 2625536 | tf_op jit(solution)/shard_map/dot_general | solution.py:100
  28.5 45.3 %all-to-all-done = bf16[32,1,32,1024]{3,2,1,0:T(8,128)(2,1)S(1)} async-done(((bf16[32,1,32,1024]{3,2,1,0:T(8,128)(2,1)}), bf16[32,1,32,1024]{3,2,1,0:T(8,128)(2,1)S(1)}, u32[]{:S(2)}, u32[]{:S(2)}) %all-to-all-start) | async-done | bytes 2097184 | tf_op jit(solution)/shard_map/all_to_all | solution.py:103
  75.2 6.1 %all-to-all-start.2 = ((bf16[32,1,32,1024]{3,2,1,0:T(8,128)(2,1)}), bf16[32,1,32,1024]{3,2,1,0:T(8,128)(2,1)S(1)}, u32[]{:S(2)}, u32[]{:S(2)}) async-start(bf16[32,1,32,1024]{3,2,1,0:T(8,128)(2,1)} %bitcast.116), calls=%async_computation.2 | async-start | bytes 4194304 | tf_op jit(solution)/shard_map/all_to_all | solution.py:106
  81.4 4.9 %copy.44 = bf16[16,1,73728]{2,0,1:T(8,128)(2,1)S(1)} copy(bf16[16,1,73728]{2,1,0:T(2,128)(2,1)} %all-gather.3.cloned.1.call-done) | data formatting | bytes 4718592
  88.5 2.7 %reshape.211 = bf16[1024,768,1]{1,0,2:T(8,128)(2,1)} reshape(bf16[16,49152]{1,0:T(8,128)(2,1)} %slice.32) | data formatting | bytes 3145728 | tf_op jit(solution)/shard_map/reshape
  91.3 2.4 reshape.212
  93.6 4.0 %multiply_bitcast_fusion = f32[32,1,32,768]{3,2,0,1:T(8,128)S(1)} fusion(bf16[1024,768,1]{1,0,2:T(8,128)(2,1)} %reshape.211, bf16[32,1,32,1024]{3,2,1,0:T(8,128)(2,1)} %copy-done.3), kind=kOutput, calls=%fused_computation.5 | convolution fusion | flops 1611399168 | bytes 6815744 | tf_op jit(solution)/shard_map/sxcd,xdj->sxcj/dot_general | solution.py:12
  100.1 2.7 %fusion.1 = bf16[32,1,32,1024]{3,2,0,1:T(8,128)(2,1)} fusion(bf16[384,1024,1]{1,0,2:T(8,128)(2,1)S(1)} %copy-done.6, bf16[32,1,32,384]{3,2,0,1:T(8,128)(2,1)S(1)} %fusion.15), kind=kOutput, calls=%fused_computation.8 | convolution fusion | flops 807403520 | bytes 3670016 | tf_op jit(solution)/shard_map/sxcf,xfd->sxcd/dot_general | solution.py:19
  102.8 28.3 %all-to-all-done.2 = bf16[32,1,32,1024]{3,2,1,0:T(8,128)(2,1)S(1)} async-done(((bf16[32,1,32,1024]{3,2,1,0:T(8,128)(2,1)}), bf16[32,1,32,1024]{3,2,1,0:T(8,128)(2,1)S(1)}, u32[]{:S(2)}, u32[]{:S(2)}) %all-to-all-start.2) | async-done | bytes 2097184 | tf_op jit(solution)/shard_map/all_to_all | solution.py:106
  131.1 6.3 %all-to-all-start.1 = ((bf16[32,1,32,1024]{3,2,1,0:T(8,128)(2,1)}), bf16[32,1,32,1024]{3,2,1,0:T(8,128)(2,1)}, u32[]{:S(2)}, u32[]{:S(2)}) async-start(bf16[32,1,32,1024]{3,2,1,0:T(8,128)(2,1)} %bitcast.117), calls=%async_computation.1 | async-start | bytes 4194304 | tf_op jit(solution)/shard_map/all_to_all | solution.py:112
  137.6 3.1 %fusion.16 = bf16[384,1024]{1,0:T(8,128)(2,1)} fusion(bf16[32,1,32,1024]{3,2,1,0:T(8,128)(2,1)S(1)} %all-to-all-done.2, bf16[32,1,32,384]{3,2,0,1:T(8,128)(2,1)} %copy-done.2), kind=kOutput, calls=%fused_computation.23 | convolution fusion | flops 806092800 | bytes 3670016 | tf_op jit(solution)/shard_map/sxcf,sxcd->xfd/dot_general | solution.py:120
  140.7 2.4 reshape_transpose_reshape.5
  143.1 4.1 %fusion.26 = (bf16[32,32,384]{2,1,0:T(8,128)(2,1)S(1)}, bf16[32,32,384]{2,1,0:T(8,128)(2,1)S(1)}) fusion(f32[32,1,32,768]{3,2,0,1:T(8,128)} %copy-done.1, bf16[384,1024,1]{1,0,2:T(8,128)(2,1)} %reshape.212, bf16[32,1,32,1024]{3,2,1,0:T(8,128)(2,1)S(1)} %all-to-all-done.2), kind=kOutput, calls=%fused_computation.36 | convolution fusion | flops 810811392 | bytes 7602176 | tf_op jit(solution)/shard_map/sxcd,xfd->sxcf/dot_general | solution.py:28
  148.3 1.9 fusion
  151.9 1.8 pad_maximum_fusion
  153.7 2.1 reshape.206
  157.4 4.3 %fusion.2 = bf16[32,1,32,1024]{3,2,1,0:T(8,128)(2,1)} fusion(bf16[1024,768,1]{1,0,2:T(8,128)(2,1)S(1)} %copy-done.5, bf16[32,32,384]{2,1,0:T(8,128)(2,1)} %copy-done.13, bf16[32,32,384]{2,1,0:T(8,128)(2,1)S(1)} %copy-done.12), kind=kOutput, calls=%fused_computation.9 | convolution fusion | flops 1615855616 | bytes 5242880 | tf_op jit(solution)/shard_map/sxcj,xdj->sxcd/dot_general | solution.py:38
  161.7 25.3 %all-to-all-done.1 = bf16[32,1,32,1024]{3,2,1,0:T(8,128)(2,1)} async-done(((bf16[32,1,32,1024]{3,2,1,0:T(8,128)(2,1)}), bf16[32,1,32,1024]{3,2,1,0:T(8,128)(2,1)}, u32[]{:S(2)}, u32[]{:S(2)}) %all-to-all-start.1) | async-done | bytes 2097184 | tf_op jit(solution)/shard_map/all_to_all | solution.py:112
  187.0 6.1 %all-to-all-start.3 = ((bf16[32,1,32,1024]{3,2,1,0:T(8,128)(2,1)}), bf16[32,1,32,1024]{3,2,1,0:T(8,128)(2,1)S(1)}, u32[]{:S(2)}, u32[]{:S(2)}) async-start(bf16[32,1,32,1024]{3,2,1,0:T(8,128)(2,1)} %fusion.2), calls=%async_computation.3 | async-start | bytes 4194304 | tf_op jit(solution)/shard_map/all_to_all | solution.py:132
  193.1 3.4 %convolution_convert_fusion.2 = bf16[128,1024]{1,0:T(8,128)(2,1)} fusion(f32[1024,128]{1,0:T(8,128)S(1)} %bitcast.118, bf16[1024,1024]{1,0:T(8,128)(2,1)} %bitcast.16), kind=kOutput, calls=%fused_computation.32 | convolution fusion | flops 1610743808 | bytes 2883584 | tf_op jit(solution)/shard_map/st,sd->td/dot_general | solution.py:138
  196.6 19.9 %reduce-scatter.2.cloned.1.call-done = bf16[8,9216]{1,0:T(8,128)(2,1)} async-done(((bf16[128,9216]{1,0:T(8,128)(2,1)}), bf16[8,9216]{1,0:T(8,128)(2,1)}) %reduce-scatter.2.cloned.1.call-update) | async-done | bytes 147472 | tf_op jit(solution)/shard_map/reduce_scatter | solution.py:125
  219.9 22.9 %all-to-all-done.3 = bf16[32,1,32,1024]{3,2,1,0:T(8,128)(2,1)S(1)} async-done(((bf16[32,1,32,1024]{3,2,1,0:T(8,128)(2,1)}), bf16[32,1,32,1024]{3,2,1,0:T(8,128)(2,1)S(1)}, u32[]{:S(2)}, u32[]{:S(2)}) %all-to-all-start.3) | async-done | bytes 2097184 | tf_op jit(solution)/shard_map/all_to_all | solution.py:132
  (57 shorter events, 18.1 us)
Async XLA Ops:
  7.2 1.2 copy-start
  10.5 13.4 %copy-start.8 = (bf16[1,24,1024]{2,1,0:T(8,128)(2,1)S(1)}, bf16[1,24,1024]{2,1,0:T(8,128)(2,1)}, u32[]{:S(2)}) copy-start(bf16[1,24,1024]{2,1,0:T(8,128)(2,1)} %param.10) | copy-start | bytes 147460
  10.5 13.5 %copy-start.7 = (bf16[1,64,768]{2,1,0:T(8,128)(2,1)S(1)}, bf16[1,64,768]{2,1,0:T(8,128)(2,1)}, u32[]{:S(2)}) copy-start(bf16[1,64,768]{2,1,0:T(8,128)(2,1)} %param.9) | copy-start | bytes 294916
  10.5 14.7 %copy-start.9 = (s32[128,4]{0,1:T(4,128)S(1)}, s32[128,4]{0,1:T(4,128)}, u32[]{:S(2)}) copy-start(s32[128,4]{0,1:T(4,128)} %param.7) | copy-start | bytes 6148
  10.5 14.7 %copy-start.10 = (f32[128,4]{0,1:T(4,128)S(1)}, f32[128,4]{0,1:T(4,128)}, u32[]{:S(2)}) copy-start(f32[128,4]{0,1:T(4,128)} %param.8) | copy-start | bytes 6148
  10.5 63.4 %all-to-all-start = ((bf16[32,1,32,1024]{3,2,1,0:T(8,128)(2,1)}), bf16[32,1,32,1024]{3,2,1,0:T(8,128)(2,1)S(1)}, u32[]{:S(2)}, u32[]{:S(2)}) async-start(bf16[32,1,32,1024]{3,2,1,0:T(8,128)(2,1)} %bitcast.7), calls=%async_computation | async-start | bytes 4194304 | tf_op jit(solution)/shard_map/all_to_all | solution.py:103
  23.8 57.6 %all-gather.3.cloned.1.call-start = ((), (), s32[]{:S(2)}) async-start(), calls=%async_computation.6 | async-start | bytes 5013504 | tf_op jit(solution)/shard_map/all_gather | solution.py:79
  73.8 1.4 copy-start.3
  75.2 55.9 %all-to-all-start.2 = ((bf16[32,1,32,1024]{3,2,1,0:T(8,128)(2,1)}), bf16[32,1,32,1024]{3,2,1,0:T(8,128)(2,1)S(1)}, u32[]{:S(2)}, u32[]{:S(2)}) async-start(bf16[32,1,32,1024]{3,2,1,0:T(8,128)(2,1)} %bitcast.116), calls=%async_computation.2 | async-start | bytes 4194304 | tf_op jit(solution)/shard_map/all_to_all | solution.py:106
  97.6 1.6 copy-start.1
  97.6 2.5 %copy-start.6 = (bf16[384,1024,1]{1,0,2:T(8,128)(2,1)S(1)}, bf16[384,1024,1]{1,0,2:T(8,128)(2,1)}, u32[]{:S(2)}) copy-start(bf16[384,1024,1]{1,0,2:T(8,128)(2,1)} %reshape.212) | copy-start | bytes 2359300
  99.2 0.9 copy-start.2
  131.1 55.9 %all-to-all-start.1 = ((bf16[32,1,32,1024]{3,2,1,0:T(8,128)(2,1)}), bf16[32,1,32,1024]{3,2,1,0:T(8,128)(2,1)}, u32[]{:S(2)}, u32[]{:S(2)}) async-start(bf16[32,1,32,1024]{3,2,1,0:T(8,128)(2,1)} %bitcast.117), calls=%async_computation.1 | async-start | bytes 4194304 | tf_op jit(solution)/shard_map/all_to_all | solution.py:112
  137.4 79.1 %reduce-scatter.2.cloned.1.call-start = ((), (), s32[]{:S(2)}) async-start(), calls=%async_computation.5 | async-start | bytes 2506752 | tf_op jit(solution)/shard_map/reduce_scatter | solution.py:125
  143.1 5.2 %copy-start.4 = (bf16[32,1,32,1024]{3,2,1,0:T(8,128)(2,1)S(1)}, bf16[32,1,32,1024]{3,2,1,0:T(8,128)(2,1)}, u32[]{:S(2)}) copy-start(bf16[32,1,32,1024]{3,2,1,0:T(8,128)(2,1)} %copy-done.3) | copy-start | bytes 6291460
  147.2 0.9 copy-start.11
  147.2 1.1 copy-start.13
  155.8 1.4 copy-start.5
  155.8 1.6 copy-start.12
  187.0 55.8 %all-to-all-start.3 = ((bf16[32,1,32,1024]{3,2,1,0:T(8,128)(2,1)}), bf16[32,1,32,1024]{3,2,1,0:T(8,128)(2,1)S(1)}, u32[]{:S(2)}, u32[]{:S(2)}) async-start(bf16[32,1,32,1024]{3,2,1,0:T(8,128)(2,1)} %fusion.2), calls=%async_computation.3 | async-start | bytes 4194304 | tf_op jit(solution)/shard_map/all_to_all | solution.py:132
Sparse Core Ops, SparseCore 0:
  26.7 45.2 all-gather.2
  156.0 60.4 reduce-scatter.1

commit v7 on v5

--- a/solution.py
+++ b/solution.py
@@ -96,7 +96,7 @@
     pick = in_slot.reshape(total, tok_rows).astype(jnp.bfloat16)
     gate_of_slot = jnp.sum(slot_gate, axis=1)
     layout = (sources, per_device, capacity, model_width)
-    send_inputs = jnp.dot(pick, tokens, preferred_element_type=jnp.float32).astype(jnp.bfloat16)
+    send_inputs = jnp.dot(pick, tokens, preferred_element_type=jnp.bfloat16)
     grad_of_slot = jnp.dot(pick, out_grad, preferred_element_type=jnp.float32)
     send_grads = (gate_of_slot[:, None] * grad_of_slot).astype(jnp.bfloat16)
 

time: 252 us -> 251 us (level)
    unnamed x44 -> x38, local copies, waits for them, and re-layouts: 10.8 us -> 10.9 us
where the time goes in v7:
time: 251 us
  waiting for transfers between devices  148 us (59%)
  starting transfers between devices  32.1 us (13%)
  matrix products  26.4 us (11%)
  local copies, waits for them, and re-layouts  21.8 us (9%)
  between operations  14.3 us (6%)
  other arithmetic  8.06 us (3%)
    all_to_all x1, waiting for transfers between devices, body(): lax.all_to_all(send_inputs.reshape(layout), 'expert', split_axis=0, conca...  45.3 us
    all_to_all x1, waiting for transfers between devices, body(): lax.all_to_all(send_grads.reshape(layout), 'expert', split_axis=0, concat...  31.2 us
    all_to_all x1, waiting for transfers between devices, body(): lax.all_to_all(results_here, 'expert', split_axis=0, concat_axis=0, tiled...  28.6 us
    all_to_all x1, waiting for transfers between devices, body(): lax.all_to_all(grad_inputs, 'expert', split_axis=0, concat_axis=0, tiled=...  24.7 us
    reduce_scatter x1, waiting for transfers between devices, body(): summed = lax.psum_scatter(packed_g, 'dp', scatter_dimension=0, tiled=True)  18 us
    all_to_all x1, starting transfers between devices, body(): lax.all_to_all(send_inputs.reshape(layout), 'expert', split_axis=0, conca...  13.3 us
    unnamed x38, local copies, waits for them, and re-layouts  10.9 us
    all_to_all x1, starting transfers between devices, body(): lax.all_to_all(results_here, 'expert', split_axis=0, concat_axis=0, tiled...  6.26 us
  transfers between devices with their start and end apart: 6, of which 5 were waited for; matrix products, arithmetic and copies ran while one was open for 19% of the time, Pallas kernels for 0%

profile of v7, /device:TPU:56, one launch (start us, length us, event | category | flops | bytes accessed | tf_op | source)
XLA Modules:
  0.0 250.6 jit_solution(18303902534726242330)
XLA Ops:
  8.1 2.0 convolution_bitcast_fusion
  10.2 13.3 %all-to-all-start = ((bf16[32,1,32,1024]{3,2,1,0:T(8,128)(2,1)}), bf16[32,1,32,1024]{3,2,1,0:T(8,128)(2,1)S(1)}, u32[]{:S(2)}, u32[]{:S(2)}) async-start(bf16[32,1,32,1024]{3,2,1,0:T(8,128)(2,1)} %convolution_bitcast_fusion), calls=%async_computation | async-start | bytes 4194304 | tf_op jit(solution)/shard_map/all_to_all | solution.py:103
  26.2 2.0 multiply_convert_fusion.1
  28.2 45.3 %all-to-all-done = bf16[32,1,32,1024]{3,2,1,0:T(8,128)(2,1)S(1)} async-done(((bf16[32,1,32,1024]{3,2,1,0:T(8,128)(2,1)}), bf16[32,1,32,1024]{3,2,1,0:T(8,128)(2,1)S(1)}, u32[]{:S(2)}, u32[]{:S(2)}) %all-to-all-start) | async-done | bytes 2097184 | tf_op jit(solution)/shard_map/all_to_all | solution.py:103
  74.9 6.1 %all-to-all-start.2 = ((bf16[32,1,32,1024]{3,2,1,0:T(8,128)(2,1)}), bf16[32,1,32,1024]{3,2,1,0:T(8,128)(2,1)S(1)}, u32[]{:S(2)}, u32[]{:S(2)}) async-start(bf16[32,1,32,1024]{3,2,1,0:T(8,128)(2,1)} %bitcast.117), calls=%async_computation.2 | async-start | bytes 4194304 | tf_op jit(solution)/shard_map/all_to_all | solution.py:106
  81.1 4.9 %copy.41 = bf16[16,1,73728]{2,0,1:T(8,128)(2,1)S(1)} copy(bf16[16,1,73728]{2,1,0:T(2,128)(2,1)} %all-gather.3.cloned.1.call-done) | data formatting | bytes 4718592
  87.3 2.8 %reshape.258 = bf16[1024,768,1]{1,0,2:T(8,128)(2,1)} reshape(bf16[16,49152]{1,0:T(8,128)(2,1)} %slice.32) | data formatting | bytes 3145728 | tf_op jit(solution)/shard_map/reshape
  91.3 4.0 %multiply_bitcast_fusion = f32[32,1,32,768]{3,2,0,1:T(8,128)S(1)} fusion(bf16[1024,768,1]{1,0,2:T(8,128)(2,1)} %reshape.258, bf16[32,1,32,1024]{3,2,1,0:T(8,128)(2,1)} %copy-done.2), kind=kOutput, calls=%fused_computation.5 | convolution fusion | flops 1611399168 | bytes 6815744 | tf_op jit(solution)/shard_map/sxcd,xdj->sxcj/dot_general | solution.py:12
  97.0 2.6 %fusion.1 = bf16[32,1,32,1024]{3,2,0,1:T(8,128)(2,1)} fusion(bf16[384,1024,1]{1,0,2:T(8,128)(2,1)S(1)} %copy-done.6, bf16[32,1,32,384]{3,2,0,1:T(8,128)(2,1)S(1)} %fusion.15), kind=kOutput, calls=%fused_computation.8 | convolution fusion | flops 807403520 | bytes 3670016 | tf_op jit(solution)/shard_map/sxcf,xfd->sxcd/dot_general | solution.py:19
  99.6 31.2 %all-to-all-done.2 = bf16[32,1,32,1024]{3,2,1,0:T(8,128)(2,1)S(1)} async-done(((bf16[32,1,32,1024]{3,2,1,0:T(8,128)(2,1)}), bf16[32,1,32,1024]{3,2,1,0:T(8,128)(2,1)S(1)}, u32[]{:S(2)}, u32[]{:S(2)}) %all-to-all-start.2) | async-done | bytes 2097184 | tf_op jit(solution)/shard_map/all_to_all | solution.py:106
  130.8 6.3 %all-to-all-start.1 = ((bf16[32,1,32,1024]{3,2,1,0:T(8,128)(2,1)}), bf16[32,1,32,1024]{3,2,1,0:T(8,128)(2,1)}, u32[]{:S(2)}, u32[]{:S(2)}) async-start(bf16[32,1,32,1024]{3,2,1,0:T(8,128)(2,1)} %bitcast.118), calls=%async_computation.1 | async-start | bytes 4194304 | tf_op jit(solution)/shard_map/all_to_all | solution.py:112
  137.3 1.9 fusion.16
  139.2 1.5 reshape_transpose_reshape.5
  140.7 4.1 %fusion.26 = (bf16[32,32,384]{2,1,0:T(8,128)(2,1)S(1)}, bf16[32,32,384]{2,1,0:T(8,128)(2,1)S(1)}) fusion(f32[32,1,32,768]{3,2,0,1:T(8,128)} %copy-done.1, bf16[384,1024,1]{1,0,2:T(8,128)(2,1)} %reshape.259, bf16[32,1,32,1024]{3,2,1,0:T(8,128)(2,1)S(1)} %all-to-all-done.2), kind=kOutput, calls=%fused_computation.36 | convolution fusion | flops 810811392 | bytes 7602176 | tf_op jit(solution)/shard_map/sxcd,xfd->sxcf/dot_general | solution.py:28
  146.0 1.9 fusion
  147.9 1.6 reshape_transpose_reshape.4
  149.5 1.6 pad_maximum_fusion
  151.1 2.2 reshape.252
  154.9 3.1 %fusion.2 = bf16[32,1,32,1024]{3,2,1,0:T(8,128)(2,1)} fusion(bf16[1024,768,1]{1,0,2:T(8,128)(2,1)S(1)} %copy-done.5, bf16[32,32,384]{2,1,0:T(8,128)(2,1)S(1)} %copy-done.16, bf16[32,32,384]{2,1,0:T(8,128)(2,1)S(1)} %copy-done.14), kind=kOutput, calls=%fused_computation.9 | convolution fusion | flops 1615855616 | bytes 5242880 | tf_op jit(solution)/shard_map/sxcj,xdj->sxcd/dot_general | solution.py:38
  158.1 28.6 %all-to-all-done.1 = bf16[32,1,32,1024]{3,2,1,0:T(8,128)(2,1)} async-done(((bf16[32,1,32,1024]{3,2,1,0:T(8,128)(2,1)}), bf16[32,1,32,1024]{3,2,1,0:T(8,128)(2,1)}, u32[]{:S(2)}, u32[]{:S(2)}) %all-to-all-start.1) | async-done | bytes 2097184 | tf_op jit(solution)/shard_map/all_to_all | solution.py:112
  186.7 6.1 %all-to-all-start.3 = ((bf16[32,1,32,1024]{3,2,1,0:T(8,128)(2,1)}), bf16[32,1,32,1024]{3,2,1,0:T(8,128)(2,1)S(1)}, u32[]{:S(2)}, u32[]{:S(2)}) async-start(bf16[32,1,32,1024]{3,2,1,0:T(8,128)(2,1)} %fusion.2), calls=%async_computation.3 | async-start | bytes 4194304 | tf_op jit(solution)/shard_map/all_to_all | solution.py:132
  193.0 3.4 %convolution_convert_fusion.1 = bf16[128,1024]{1,0:T(8,128)(2,1)} fusion(f32[1024,128]{1,0:T(8,128)S(1)} %bitcast.119, bf16[1024,1024]{1,0:T(8,128)(2,1)} %bitcast.15), kind=kOutput, calls=%fused_computation.32 | convolution fusion | flops 1610743808 | bytes 2883584 | tf_op jit(solution)/shard_map/st,sd->td/dot_general | solution.py:138
  196.4 18.0 %reduce-scatter.2.cloned.1.call-done = bf16[8,9216]{1,0:T(8,128)(2,1)} async-done(((bf16[128,9216]{1,0:T(8,128)(2,1)}), bf16[8,9216]{1,0:T(8,128)(2,1)}) %reduce-scatter.2.cloned.1.call-update) | async-done | bytes 147472 | tf_op jit(solution)/shard_map/reduce_scatter | solution.py:125
  217.8 24.7 %all-to-all-done.3 = bf16[32,1,32,1024]{3,2,1,0:T(8,128)(2,1)S(1)} async-done(((bf16[32,1,32,1024]{3,2,1,0:T(8,128)(2,1)}), bf16[32,1,32,1024]{3,2,1,0:T(8,128)(2,1)S(1)}, u32[]{:S(2)}, u32[]{:S(2)}) %all-to-all-start.3) | async-done | bytes 2097184 | tf_op jit(solution)/shard_map/all_to_all | solution.py:132
  (64 shorter events, 16.9 us)
Async XLA Ops:
  7.2 1.0 copy-start
  10.2 13.4 %copy-start.9 = (bf16[1,24,1024]{2,1,0:T(8,128)(2,1)S(1)}, bf16[1,24,1024]{2,1,0:T(8,128)(2,1)}, u32[]{:S(2)}) copy-start(bf16[1,24,1024]{2,1,0:T(8,128)(2,1)} %param.10) | copy-start | bytes 147460
  10.2 13.5 %copy-start.7 = (bf16[1,64,768]{2,1,0:T(8,128)(2,1)S(1)}, bf16[1,64,768]{2,1,0:T(8,128)(2,1)}, u32[]{:S(2)}) copy-start(bf16[1,64,768]{2,1,0:T(8,128)(2,1)} %param.9) | copy-start | bytes 294916
  10.2 15.0 %copy-start.11 = (s32[128,4]{0,1:T(4,128)S(1)}, s32[128,4]{0,1:T(4,128)}, u32[]{:S(2)}) copy-start(s32[128,4]{0,1:T(4,128)} %param.7) | copy-start | bytes 6148
  10.2 15.0 %copy-start.12 = (f32[128,4]{0,1:T(4,128)S(1)}, f32[128,4]{0,1:T(4,128)}, u32[]{:S(2)}) copy-start(f32[128,4]{0,1:T(4,128)} %param.8) | copy-start | bytes 6148
  10.2 63.4 %all-to-all-start = ((bf16[32,1,32,1024]{3,2,1,0:T(8,128)(2,1)}), bf16[32,1,32,1024]{3,2,1,0:T(8,128)(2,1)S(1)}, u32[]{:S(2)}, u32[]{:S(2)}) async-start(bf16[32,1,32,1024]{3,2,1,0:T(8,128)(2,1)} %convolution_bitcast_fusion), calls=%async_computation | async-start | bytes 4194304 | tf_op jit(solution)/shard_map/all_to_all | solution.py:103
  23.5 2.7 %copy-start.8 = (bf16[128,1024]{1,0:T(8,128)(2,1)S(1)}, bf16[128,1024]{1,0:T(8,128)(2,1)}, u32[]{:S(2)}) copy-start(bf16[128,1024]{1,0:T(8,128)(2,1)} %param.11) | copy-start | bytes 786436
  23.5 57.5 %all-gather.3.cloned.1.call-start = ((), (), s32[]{:S(2)}) async-start(), calls=%async_computation.6 | async-start | bytes 5013504 | tf_op jit(solution)/shard_map/all_gather | solution.py:79
  73.6 1.3 copy-start.2
  74.9 55.9 %all-to-all-start.2 = ((bf16[32,1,32,1024]{3,2,1,0:T(8,128)(2,1)}), bf16[32,1,32,1024]{3,2,1,0:T(8,128)(2,1)S(1)}, u32[]{:S(2)}, u32[]{:S(2)}) async-start(bf16[32,1,32,1024]{3,2,1,0:T(8,128)(2,1)} %bitcast.117), calls=%async_computation.2 | async-start | bytes 4194304 | tf_op jit(solution)/shard_map/all_to_all | solution.py:106
  95.3 1.7 copy-start.1
  95.3 1.7 copy-start.6
  130.8 55.9 %all-to-all-start.1 = ((bf16[32,1,32,1024]{3,2,1,0:T(8,128)(2,1)}), bf16[32,1,32,1024]{3,2,1,0:T(8,128)(2,1)}, u32[]{:S(2)}, u32[]{:S(2)}) async-start(bf16[32,1,32,1024]{3,2,1,0:T(8,128)(2,1)} %bitcast.118), calls=%async_computation.1 | async-start | bytes 4194304 | tf_op jit(solution)/shard_map/all_to_all | solution.py:112
  137.1 77.3 %reduce-scatter.2.cloned.1.call-start = ((), (), s32[]{:S(2)}) async-start(), calls=%async_computation.5 | async-start | bytes 2506752 | tf_op jit(solution)/shard_map/reduce_scatter | solution.py:125
  140.7 5.3 %copy-start.3 = (bf16[32,1,32,1024]{3,2,1,0:T(8,128)(2,1)S(1)}, bf16[32,1,32,1024]{3,2,1,0:T(8,128)(2,1)}, u32[]{:S(2)}) copy-start(bf16[32,1,32,1024]{3,2,1,0:T(8,128)(2,1)} %copy-done.2) | copy-start | bytes 6291460
  144.8 1.0 copy-start.13
  144.8 1.2 copy-start.15
  151.1 2.3 copy-start.16
  153.3 1.4 copy-start.5
  153.3 1.6 copy-start.14
  158.1 34.9 %copy-start.4 = (f32[32,32,128]{2,1,0:T(8,128)S(1)}, f32[32,32,128]{2,1,0:T(8,128)}, u32[]{:S(2)}) copy-start(f32[32,32,128]{2,1,0:T(8,128)} %get-tuple-element.19) | copy-start | bytes 1572868
  186.7 55.8 %all-to-all-start.3 = ((bf16[32,1,32,1024]{3,2,1,0:T(8,128)(2,1)}), bf16[32,1,32,1024]{3,2,1,0:T(8,128)(2,1)S(1)}, u32[]{:S(2)}, u32[]{:S(2)}) async-start(bf16[32,1,32,1024]{3,2,1,0:T(8,128)(2,1)} %fusion.2), calls=%async_computation.3 | async-start | bytes 4194304 | tf_op jit(solution)/shard_map/all_to_all | solution.py:132
  192.9 23.6 %copy-start.10 = (bf16[1,24,1024]{2,1,0:T(8,128)(2,1)S(1)}, bf16[1,24,1024]{2,1,0:T(8,128)(2,1)}, u32[]{:S(2)}) copy-start(bf16[1,24,1024]{2,1,0:T(8,128)(2,1)} %param.10) | copy-start | bytes 147460
Sparse Core Ops, SparseCore 0:
  26.5 45.2 all-gather.2
  153.5 60.8 reduce-scatter.1

commit v8 on v7

--- a/solution.py
+++ b/solution.py
@@ -1,9 +1,39 @@
 import jax
 import jax.numpy as jnp
 from jax import lax
+from jax.experimental import pallas as pl
+from jax.experimental.pallas import tpu as pltpu
 from jax.sharding import PartitionSpec as P
 
 step_rate = 0.5
+
+
+def dispatch_kernel(pick_ref, rows_ref, out_ref):
+    out_ref[...] = jnp.dot(
+        pick_ref[...], rows_ref[...], preferred_element_type=jnp.float32
+    ).astype(out_ref.dtype)
+
+
+def dispatch_rows(pick, rows):
+    slots, count = pick.shape
+    width = rows.shape[1]
+    block = 256
+    return pl.pallas_call(
+        dispatch_kernel,
+        out_shape=jax.ShapeDtypeStruct((slots, width), jnp.bfloat16),
+        grid=(slots // block,),
+        in_specs=[
+            pl.BlockSpec((block, count), lambda i: (i, 0)),
+            pl.BlockSpec((count, width), lambda i: (0, 0)),
+        ],
+        out_specs=pl.BlockSpec((block, width), lambda i: (i, 0)),
+        cost_estimate=pl.CostEstimate(
+            flops=2 * slots * count * width,
+            bytes_accessed=2 * (slots * count + count * width + slots * width),
+            transcendentals=0,
+        ),
+        name="dispatch_rows",
+    )(pick, rows)
 
 
 def expert_forward(inputs, full_in, full_down):
@@ -96,7 +126,7 @@
     pick = in_slot.reshape(total, tok_rows).astype(jnp.bfloat16)
     gate_of_slot = jnp.sum(slot_gate, axis=1)
     layout = (sources, per_device, capacity, model_width)
-    send_inputs = jnp.dot(pick, tokens, preferred_element_type=jnp.bfloat16)
+    send_inputs = dispatch_rows(pick, tokens)
     grad_of_slot = jnp.dot(pick, out_grad, preferred_element_type=jnp.float32)
     send_grads = (gate_of_slot[:, None] * grad_of_slot).astype(jnp.bfloat16)
 

time: 251 us -> 254 us (1.012)
  Pallas kernels: 0 us -> 4.01 us
    pallas_call x0 -> x1, Pallas kernels: none -> 4.01 us  [dispatch_rows(): pl.pallas_call(dispatch_kernel, out_shape=jax.ShapeDtypeStruct((slots, wi...]
    unnamed x38 -> x42, local copies, waits for them, and re-layouts: 10.9 us -> 10.8 us
  transfers between devices with their start and end apart: 6 -> 6, of which waited for: 5 -> 5; matrix products, arithmetic and copies ran while one was open for 19% -> 18% of each run, Pallas kernels for 0% -> 0%
where the time goes in v8:
time: 254 us
  waiting for transfers between devices  148 us (58%)
  starting transfers between devices  32.1 us (13%)
  matrix products  24.4 us (10%)
  local copies, waits for them, and re-layouts  21.8 us (9%)
  between operations  14.4 us (6%)
  other arithmetic  8.79 us (3%)
  Pallas kernels  4.01 us (2%)
    all_to_all x1, waiting for transfers between devices, body(): lax.all_to_all(send_inputs.reshape(layout), 'expert', split_axis=0, conca...  45.6 us
    all_to_all x1, waiting for transfers between devices, body(): lax.all_to_all(send_grads.reshape(layout), 'expert', split_axis=0, concat...  31.1 us
    all_to_all x1, waiting for transfers between devices, body(): lax.all_to_all(results_here, 'expert', split_axis=0, concat_axis=0, tiled...  28.6 us
    all_to_all x1, waiting for transfers between devices, body(): lax.all_to_all(grad_inputs, 'expert', split_axis=0, concat_axis=0, tiled=...  24.8 us
    reduce_scatter x1, waiting for transfers between devices, body(): summed = lax.psum_scatter(packed_g, 'dp', scatter_dimension=0, tiled=True)  17.9 us
    all_to_all x1, starting transfers between devices, body(): lax.all_to_all(send_inputs.reshape(layout), 'expert', split_axis=0, conca...  13.3 us
    unnamed x42, local copies, waits for them, and re-layouts  10.8 us
    all_to_all x1, starting transfers between devices, body(): lax.all_to_all(results_here, 'expert', split_axis=0, concat_axis=0, tiled...  6.26 us
  transfers between devices with their start and end apart: 6, of which 5 were waited for; matrix products, arithmetic and copies ran while one was open for 18% of the time, Pallas kernels for 0%

profile of v8, /device:TPU:56, one launch (start us, length us, event | category | flops | bytes accessed | tf_op | source)
XLA Modules:
  0.0 253.5 jit_solution(445908097091922786)
XLA Ops:
  9.1 4.0 %dispatch_rows.1 = bf16[1024,1024]{1,0:T(8,128)(2,1)} custom-call(bf16[1024,128]{1,0:T(8,128)(2,1)} %get-tuple-element.21.pick_ref, bf16[128,1024]{1,0:T(8,128)(2,1)} %rows_ref.1), custom_call_target="tpu_custom_call" | custom-call | flops 268435456 | bytes 2621440 | tf_op jit(solution)/shard_map/dispatch_rows/pallas_call | solution.py:21
  13.1 13.3 %all-to-all-start = ((bf16[32,1,32,1024]{3,2,1,0:T(8,128)(2,1)}), bf16[32,1,32,1024]{3,2,1,0:T(8,128)(2,1)S(1)}, u32[]{:S(2)}, u32[]{:S(2)}) async-start(bf16[32,1,32,1024]{3,2,1,0:T(8,128)(2,1)} %bitcast.116), calls=%async_computation | async-start | bytes 4194304 | tf_op jit(solution)/shard_map/all_to_all | solution.py:133
  28.8 2.0 multiply_convert_fusion.1
  30.9 45.6 %all-to-all-done = bf16[32,1,32,1024]{3,2,1,0:T(8,128)(2,1)S(1)} async-done(((bf16[32,1,32,1024]{3,2,1,0:T(8,128)(2,1)}), bf16[32,1,32,1024]{3,2,1,0:T(8,128)(2,1)S(1)}, u32[]{:S(2)}, u32[]{:S(2)}) %all-to-all-start) | async-done | bytes 2097184 | tf_op jit(solution)/shard_map/all_to_all | solution.py:133
  77.8 6.1 %all-to-all-start.2 = ((bf16[32,1,32,1024]{3,2,1,0:T(8,128)(2,1)}), bf16[32,1,32,1024]{3,2,1,0:T(8,128)(2,1)S(1)}, u32[]{:S(2)}, u32[]{:S(2)}) async-start(bf16[32,1,32,1024]{3,2,1,0:T(8,128)(2,1)} %bitcast.118), calls=%async_computation.2 | async-start | bytes 4194304 | tf_op jit(solution)/shard_map/all_to_all | solution.py:136
  84.0 4.9 %copy.41 = bf16[16,1,73728]{2,0,1:T(8,128)(2,1)S(1)} copy(bf16[16,1,73728]{2,1,0:T(2,128)(2,1)} %all-gather.3.cloned.1.call-done) | data formatting | bytes 4718592
  90.3 2.8 %reshape.244 = bf16[1024,768,1]{1,0,2:T(8,128)(2,1)} reshape(bf16[16,49152]{1,0:T(8,128)(2,1)} %slice.32) | data formatting | bytes 3145728 | tf_op jit(solution)/shard_map/reshape
  94.3 4.0 %multiply_bitcast_fusion = f32[32,1,32,768]{3,2,0,1:T(8,128)S(1)} fusion(bf16[1024,768,1]{1,0,2:T(8,128)(2,1)} %reshape.244, bf16[32,1,32,1024]{3,2,1,0:T(8,128)(2,1)} %copy-done.2), kind=kOutput, calls=%fused_computation.5 | convolution fusion | flops 1611399168 | bytes 6815744 | tf_op jit(solution)/shard_map/sxcd,xdj->sxcj/dot_general | solution.py:42
  100.0 2.6 %fusion.1 = bf16[32,1,32,1024]{3,2,0,1:T(8,128)(2,1)} fusion(bf16[384,1024,1]{1,0,2:T(8,128)(2,1)S(1)} %copy-done.6, bf16[32,1,32,384]{3,2,0,1:T(8,128)(2,1)S(1)} %fusion.15), kind=kOutput, calls=%fused_computation.8 | convolution fusion | flops 807403520 | bytes 3670016 | tf_op jit(solution)/shard_map/sxcf,xfd->sxcd/dot_general | solution.py:49
  102.6 31.1 %all-to-all-done.2 = bf16[32,1,32,1024]{3,2,1,0:T(8,128)(2,1)S(1)} async-done(((bf16[32,1,32,1024]{3,2,1,0:T(8,128)(2,1)}), bf16[32,1,32,1024]{3,2,1,0:T(8,128)(2,1)S(1)}, u32[]{:S(2)}, u32[]{:S(2)}) %all-to-all-start.2) | async-done | bytes 2097184 | tf_op jit(solution)/shard_map/all_to_all | solution.py:136
  133.7 6.3 %all-to-all-start.1 = ((bf16[32,1,32,1024]{3,2,1,0:T(8,128)(2,1)}), bf16[32,1,32,1024]{3,2,1,0:T(8,128)(2,1)}, u32[]{:S(2)}, u32[]{:S(2)}) async-start(bf16[32,1,32,1024]{3,2,1,0:T(8,128)(2,1)} %bitcast.119), calls=%async_computation.1 | async-start | bytes 4194304 | tf_op jit(solution)/shard_map/all_to_all | solution.py:142
  140.2 1.9 fusion.16
  142.2 1.5 reshape_transpose_reshape.5
  143.7 4.1 %fusion.26 = (bf16[32,32,384]{2,1,0:T(8,128)(2,1)S(1)}, bf16[32,32,384]{2,1,0:T(8,128)(2,1)S(1)}) fusion(f32[32,1,32,768]{3,2,0,1:T(8,128)} %copy-done.1, bf16[384,1024,1]{1,0,2:T(8,128)(2,1)} %reshape.245, bf16[32,1,32,1024]{3,2,1,0:T(8,128)(2,1)S(1)} %all-to-all-done.2), kind=kOutput, calls=%fused_computation.35 | convolution fusion | flops 810811392 | bytes 7602176 | tf_op jit(solution)/shard_map/sxcd,xfd->sxcf/dot_general | solution.py:58
  148.9 1.9 fusion
  150.8 1.6 reshape_transpose_reshape.4
  152.5 1.6 pad_maximum_fusion
  154.1 2.2 reshape.239
  157.9 3.1 %fusion.2 = bf16[32,1,32,1024]{3,2,1,0:T(8,128)(2,1)} fusion(bf16[1024,768,1]{1,0,2:T(8,128)(2,1)S(1)} %copy-done.5, bf16[32,32,384]{2,1,0:T(8,128)(2,1)S(1)} %copy-done.18, bf16[32,32,384]{2,1,0:T(8,128)(2,1)S(1)} %copy-done.16), kind=kOutput, calls=%fused_computation.9 | convolution fusion | flops 1615855616 | bytes 5242880 | tf_op jit(solution)/shard_map/sxcj,xdj->sxcd/dot_general | solution.py:68
  161.0 28.6 %all-to-all-done.1 = bf16[32,1,32,1024]{3,2,1,0:T(8,128)(2,1)} async-done(((bf16[32,1,32,1024]{3,2,1,0:T(8,128)(2,1)}), bf16[32,1,32,1024]{3,2,1,0:T(8,128)(2,1)}, u32[]{:S(2)}, u32[]{:S(2)}) %all-to-all-start.1) | async-done | bytes 2097184 | tf_op jit(solution)/shard_map/all_to_all | solution.py:142
  189.6 6.1 %all-to-all-start.3 = ((bf16[32,1,32,1024]{3,2,1,0:T(8,128)(2,1)}), bf16[32,1,32,1024]{3,2,1,0:T(8,128)(2,1)S(1)}, u32[]{:S(2)}, u32[]{:S(2)}) async-start(bf16[32,1,32,1024]{3,2,1,0:T(8,128)(2,1)} %fusion.2), calls=%async_computation.3 | async-start | bytes 4194304 | tf_op jit(solution)/shard_map/all_to_all | solution.py:162
  195.9 3.4 %convolution_convert_fusion.1 = bf16[128,1024]{1,0:T(8,128)(2,1)} fusion(f32[1024,128]{1,0:T(8,128)S(1)} %bitcast.120, bf16[1024,1024]{1,0:T(8,128)(2,1)} %bitcast.16), kind=kOutput, calls=%fused_computation.31 | convolution fusion | flops 1610743808 | bytes 2883584 | tf_op jit(solution)/shard_map/st,sd->td/dot_general | solution.py:168
  199.3 17.9 %reduce-scatter.2.cloned.1.call-done = bf16[8,9216]{1,0:T(8,128)(2,1)} async-done(((bf16[128,9216]{1,0:T(8,128)(2,1)}), bf16[8,9216]{1,0:T(8,128)(2,1)}) %reduce-scatter.2.cloned.1.call-update) | async-done | bytes 147472 | tf_op jit(solution)/shard_map/reduce_scatter | solution.py:155
  220.7 24.8 %all-to-all-done.3 = bf16[32,1,32,1024]{3,2,1,0:T(8,128)(2,1)S(1)} async-done(((bf16[32,1,32,1024]{3,2,1,0:T(8,128)(2,1)}), bf16[32,1,32,1024]{3,2,1,0:T(8,128)(2,1)S(1)}, u32[]{:S(2)}, u32[]{:S(2)}) %all-to-all-start.3) | async-done | bytes 2097184 | tf_op jit(solution)/shard_map/all_to_all | solution.py:162
  (68 shorter events, 17.6 us)
Async XLA Ops:
  7.2 21.7 %copy-start = (bf16[128,1024]{1,0:T(8,128)(2,1)S(1)}, bf16[128,1024]{1,0:T(8,128)(2,1)}, u32[]{:S(2)}) copy-start(bf16[128,1024]{1,0:T(8,128)(2,1)} %param.11) | copy-start | bytes 786436
  7.9 19.9 %copy-start.11 = (pred[128,32]{0,1:T(8,128)(4,1)}, pred[128,32]{0,1:T(8,128)(4,1)S(1)}, u32[]{:S(2)}) copy-start(pred[128,32]{0,1:T(8,128)(4,1)S(1)} %fusion.32) | copy-start | bytes 12292
  8.1 19.8 %copy-start.9 = (f32[32,128]{1,0:T(8,128)}, f32[32,128]{1,0:T(8,128)S(1)}, u32[]{:S(2)}) copy-start(f32[32,128]{1,0:T(8,128)S(1)} %fusion.33) | copy-start | bytes 49156
  13.1 13.4 %copy-start.8 = (bf16[1,24,1024]{2,1,0:T(8,128)(2,1)S(1)}, bf16[1,24,1024]{2,1,0:T(8,128)(2,1)}, u32[]{:S(2)}) copy-start(bf16[1,24,1024]{2,1,0:T(8,128)(2,1)} %param.10) | copy-start | bytes 147460
  13.1 13.5 %copy-start.7 = (bf16[1,64,768]{2,1,0:T(8,128)(2,1)S(1)}, bf16[1,64,768]{2,1,0:T(8,128)(2,1)}, u32[]{:S(2)}) copy-start(bf16[1,64,768]{2,1,0:T(8,128)(2,1)} %param.9) | copy-start | bytes 294916
  13.1 14.7 %copy-start.13 = (s32[128,4]{0,1:T(4,128)S(1)}, s32[128,4]{0,1:T(4,128)}, u32[]{:S(2)}) copy-start(s32[128,4]{0,1:T(4,128)} %param.7) | copy-start | bytes 6148
  13.1 14.7 %copy-start.14 = (f32[128,4]{0,1:T(4,128)S(1)}, f32[128,4]{0,1:T(4,128)}, u32[]{:S(2)}) copy-start(f32[128,4]{0,1:T(4,128)} %param.8) | copy-start | bytes 6148
  13.1 63.4 %all-to-all-start = ((bf16[32,1,32,1024]{3,2,1,0:T(8,128)(2,1)}), bf16[32,1,32,1024]{3,2,1,0:T(8,128)(2,1)S(1)}, u32[]{:S(2)}, u32[]{:S(2)}) async-start(bf16[32,1,32,1024]{3,2,1,0:T(8,128)(2,1)} %bitcast.116), calls=%async_computation | async-start | bytes 4194304 | tf_op jit(solution)/shard_map/all_to_all | solution.py:133
  26.4 57.6 %all-gather.3.cloned.1.call-start = ((), (), s32[]{:S(2)}) async-start(), calls=%async_computation.6 | async-start | bytes 5013504 | tf_op jit(solution)/shard_map/all_gather | solution.py:109
  76.5 1.4 copy-start.2
  77.8 55.9 %all-to-all-start.2 = ((bf16[32,1,32,1024]{3,2,1,0:T(8,128)(2,1)}), bf16[32,1,32,1024]{3,2,1,0:T(8,128)(2,1)S(1)}, u32[]{:S(2)}, u32[]{:S(2)}) async-start(bf16[32,1,32,1024]{3,2,1,0:T(8,128)(2,1)} %bitcast.118), calls=%async_computation.2 | async-start | bytes 4194304 | tf_op jit(solution)/shard_map/all_to_all | solution.py:136
  98.3 1.7 copy-start.1
  98.3 1.7 copy-start.6
  133.7 55.9 %all-to-all-start.1 = ((bf16[32,1,32,1024]{3,2,1,0:T(8,128)(2,1)}), bf16[32,1,32,1024]{3,2,1,0:T(8,128)(2,1)}, u32[]{:S(2)}, u32[]{:S(2)}) async-start(bf16[32,1,32,1024]{3,2,1,0:T(8,128)(2,1)} %bitcast.119), calls=%async_computation.1 | async-start | bytes 4194304 | tf_op jit(solution)/shard_map/all_to_all | solution.py:142
  140.0 77.2 %reduce-scatter.2.cloned.1.call-start = ((), (), s32[]{:S(2)}) async-start(), calls=%async_computation.5 | async-start | bytes 2506752 | tf_op jit(solution)/shard_map/reduce_scatter | solution.py:155
  143.7 5.3 %copy-start.3 = (bf16[32,1,32,1024]{3,2,1,0:T(8,128)(2,1)S(1)}, bf16[32,1,32,1024]{3,2,1,0:T(8,128)(2,1)}, u32[]{:S(2)}) copy-start(bf16[32,1,32,1024]{3,2,1,0:T(8,128)(2,1)} %copy-done.2) | copy-start | bytes 6291460
  147.8 1.2 copy-start.17
  154.0 2.3 copy-start.18
  156.3 1.4 copy-start.5
  156.3 1.6 copy-start.16
  161.0 34.7 %copy-start.10 = (f32[32,128]{1,0:T(8,128)S(1)}, f32[32,128]{1,0:T(8,128)}, u32[]{:S(2)}) copy-start(f32[32,128]{1,0:T(8,128)} %copy-done.9) | copy-start | bytes 49156
  161.0 34.8 %copy-start.12 = (pred[128,32]{0,1:T(8,128)(4,1)S(1)}, pred[128,32]{0,1:T(8,128)(4,1)}, u32[]{:S(2)}) copy-start(pred[128,32]{0,1:T(8,128)(4,1)} %copy-done.11) | copy-start | bytes 12292
  161.0 34.9 %copy-start.4 = (f32[32,32,128]{2,1,0:T(8,128)S(1)}, f32[32,32,128]{2,1,0:T(8,128)}, u32[]{:S(2)}) copy-start(f32[32,32,128]{2,1,0:T(8,128)} %get-tuple-element.19) | copy-start | bytes 1572868
  189.6 55.8 %all-to-all-start.3 = ((bf16[32,1,32,1024]{3,2,1,0:T(8,128)(2,1)}), bf16[32,1,32,1024]{3,2,1,0:T(8,128)(2,1)S(1)}, u32[]{:S(2)}, u32[]{:S(2)}) async-start(bf16[32,1,32,1024]{3,2,1,0:T(8,128)(2,1)} %fusion.2), calls=%async_computation.3 | async-start | bytes 4194304 | tf_op jit(solution)/shard_map/all_to_all | solution.py:162
  (1 other events, 0.9 us)
Sparse Core Ops, SparseCore 0:
  29.4 45.2 all-gather.2
  156.4 60.7 reduce-scatter.1

commit v9 on v7

--- a/solution.py
+++ b/solution.py
@@ -82,17 +82,17 @@
         gathered[:, per_device * in_size :], owners, per_device, down_rows, down_cols
     )
 
-    named = routes[:, :, None] == jnp.arange(experts, dtype=jnp.int32)[None, None, :]
+    named = routes.T[None, :, :] == jnp.arange(experts, dtype=jnp.int32)[:, None, None]
     routed = jnp.any(named, axis=1)
-    gate_of = jnp.sum(jnp.where(named, gates[:, :, None], 0.0), axis=1)
-    earlier = (
-        jnp.arange(tok_rows, dtype=jnp.int32)[:, None] > jnp.arange(tok_rows, dtype=jnp.int32)[None, :]
+    gate_of = jnp.sum(jnp.where(named, gates.T[None, :, :], 0.0), axis=1)
+    later = (
+        jnp.arange(tok_rows, dtype=jnp.int32)[:, None] < jnp.arange(tok_rows, dtype=jnp.int32)[None, :]
     ).astype(jnp.bfloat16)
-    rank = jnp.dot(earlier, routed.astype(jnp.bfloat16), preferred_element_type=jnp.float32)
-    in_slot = routed.T[:, None, :] & (
-        rank.T[:, None, :] == jnp.arange(capacity, dtype=jnp.float32)[None, :, None]
+    rank = jnp.dot(routed.astype(jnp.bfloat16), later, preferred_element_type=jnp.float32)
+    in_slot = routed[:, None, :] & (
+        rank[:, None, :] == jnp.arange(capacity, dtype=jnp.float32)[None, :, None]
     )
-    slot_gate = jnp.where(in_slot, gate_of.T[:, None, :], 0.0).reshape(total, tok_rows)
+    slot_gate = jnp.where(in_slot, gate_of[:, None, :], 0.0).reshape(total, tok_rows)
     pick = in_slot.reshape(total, tok_rows).astype(jnp.bfloat16)
     gate_of_slot = jnp.sum(slot_gate, axis=1)
     layout = (sources, per_device, capacity, model_width)

time: 251 us -> 251 us (level)
  no operation moved by 1% of the time
where the time goes in v9:
time: 251 us
  waiting for transfers between devices  148 us (59%)
  starting transfers between devices  32.1 us (13%)
  matrix products  26.4 us (11%)
  local copies, waits for them, and re-layouts  21.8 us (9%)
  between operations  14.3 us (6%)
  other arithmetic  8.06 us (3%)
    all_to_all x1, waiting for transfers between devices, body(): lax.all_to_all(send_inputs.reshape(layout), 'expert', split_axis=0, conca...  45.3 us
    all_to_all x1, waiting for transfers between devices, body(): lax.all_to_all(send_grads.reshape(layout), 'expert', split_axis=0, concat...  31.2 us
    all_to_all x1, waiting for transfers between devices, body(): lax.all_to_all(results_here, 'expert', split_axis=0, concat_axis=0, tiled...  28.6 us
    all_to_all x1, waiting for transfers between devices, body(): lax.all_to_all(grad_inputs, 'expert', split_axis=0, concat_axis=0, tiled=...  24.7 us
    reduce_scatter x1, waiting for transfers between devices, body(): summed = lax.psum_scatter(packed_g, 'dp', scatter_dimension=0, tiled=True)  18 us
    all_to_all x1, starting transfers between devices, body(): lax.all_to_all(send_inputs.reshape(layout), 'expert', split_axis=0, conca...  13.3 us
    unnamed x38, local copies, waits for them, and re-layouts  10.9 us
    all_to_all x1, starting transfers between devices, body(): lax.all_to_all(results_here, 'expert', split_axis=0, concat_axis=0, tiled...  6.26 us
  transfers between devices with their start and end apart: 6, of which 5 were waited for; matrix products, arithmetic and copies ran while one was open for 19% of the time, Pallas kernels for 0%

profile of v9, /device:TPU:56, one launch (start us, length us, event | category | flops | bytes accessed | tf_op | source)
XLA Modules:
  0.0 250.6 jit_solution(1697671866470254714)
XLA Ops:
  8.1 2.0 convolution_bitcast_fusion
  10.2 13.3 %all-to-all-start = ((bf16[32,1,32,1024]{3,2,1,0:T(8,128)(2,1)}), bf16[32,1,32,1024]{3,2,1,0:T(8,128)(2,1)S(1)}, u32[]{:S(2)}, u32[]{:S(2)}) async-start(bf16[32,1,32,1024]{3,2,1,0:T(8,128)(2,1)} %convolution_bitcast_fusion), calls=%async_computation | async-start | bytes 4194304 | tf_op jit(solution)/shard_map/all_to_all | solution.py:103
  26.2 2.0 multiply_convert_fusion.1
  28.2 45.3 %all-to-all-done = bf16[32,1,32,1024]{3,2,1,0:T(8,128)(2,1)S(1)} async-done(((bf16[32,1,32,1024]{3,2,1,0:T(8,128)(2,1)}), bf16[32,1,32,1024]{3,2,1,0:T(8,128)(2,1)S(1)}, u32[]{:S(2)}, u32[]{:S(2)}) %all-to-all-start) | async-done | bytes 2097184 | tf_op jit(solution)/shard_map/all_to_all | solution.py:103
  74.9 6.1 %all-to-all-start.2 = ((bf16[32,1,32,1024]{3,2,1,0:T(8,128)(2,1)}), bf16[32,1,32,1024]{3,2,1,0:T(8,128)(2,1)S(1)}, u32[]{:S(2)}, u32[]{:S(2)}) async-start(bf16[32,1,32,1024]{3,2,1,0:T(8,128)(2,1)} %bitcast.117), calls=%async_computation.2 | async-start | bytes 4194304 | tf_op jit(solution)/shard_map/all_to_all | solution.py:106
  81.1 4.9 %copy.35 = bf16[16,1,73728]{2,0,1:T(8,128)(2,1)S(1)} copy(bf16[16,1,73728]{2,1,0:T(2,128)(2,1)} %all-gather.3.cloned.1.call-done) | data formatting | bytes 4718592
  87.3 2.8 %reshape.256 = bf16[1024,768,1]{1,0,2:T(8,128)(2,1)} reshape(bf16[16,49152]{1,0:T(8,128)(2,1)} %slice.32) | data formatting | bytes 3145728 | tf_op jit(solution)/shard_map/reshape
  91.3 4.0 %multiply_bitcast_fusion = f32[32,1,32,768]{3,2,0,1:T(8,128)S(1)} fusion(bf16[1024,768,1]{1,0,2:T(8,128)(2,1)} %reshape.256, bf16[32,1,32,1024]{3,2,1,0:T(8,128)(2,1)} %copy-done.2), kind=kOutput, calls=%fused_computation.5 | convolution fusion | flops 1611399168 | bytes 6815744 | tf_op jit(solution)/shard_map/sxcd,xdj->sxcj/dot_general | solution.py:12
  97.0 2.6 %fusion.1 = bf16[32,1,32,1024]{3,2,0,1:T(8,128)(2,1)} fusion(bf16[384,1024,1]{1,0,2:T(8,128)(2,1)S(1)} %copy-done.6, bf16[32,1,32,384]{3,2,0,1:T(8,128)(2,1)S(1)} %fusion.15), kind=kOutput, calls=%fused_computation.8 | convolution fusion | flops 807403520 | bytes 3670016 | tf_op jit(solution)/shard_map/sxcf,xfd->sxcd/dot_general | solution.py:19
  99.6 31.2 %all-to-all-done.2 = bf16[32,1,32,1024]{3,2,1,0:T(8,128)(2,1)S(1)} async-done(((bf16[32,1,32,1024]{3,2,1,0:T(8,128)(2,1)}), bf16[32,1,32,1024]{3,2,1,0:T(8,128)(2,1)S(1)}, u32[]{:S(2)}, u32[]{:S(2)}) %all-to-all-start.2) | async-done | bytes 2097184 | tf_op jit(solution)/shard_map/all_to_all | solution.py:106
  130.8 6.3 %all-to-all-start.1 = ((bf16[32,1,32,1024]{3,2,1,0:T(8,128)(2,1)}), bf16[32,1,32,1024]{3,2,1,0:T(8,128)(2,1)}, u32[]{:S(2)}, u32[]{:S(2)}) async-start(bf16[32,1,32,1024]{3,2,1,0:T(8,128)(2,1)} %bitcast.118), calls=%async_computation.1 | async-start | bytes 4194304 | tf_op jit(solution)/shard_map/all_to_all | solution.py:112
  137.3 1.9 fusion.16
  139.2 1.5 reshape_transpose_reshape.5
  140.7 4.1 %fusion.26 = (bf16[32,32,384]{2,1,0:T(8,128)(2,1)S(1)}, bf16[32,32,384]{2,1,0:T(8,128)(2,1)S(1)}) fusion(f32[32,1,32,768]{3,2,0,1:T(8,128)} %copy-done.1, bf16[384,1024,1]{1,0,2:T(8,128)(2,1)} %reshape.257, bf16[32,1,32,1024]{3,2,1,0:T(8,128)(2,1)S(1)} %all-to-all-done.2), kind=kOutput, calls=%fused_computation.36 | convolution fusion | flops 810811392 | bytes 7602176 | tf_op jit(solution)/shard_map/sxcd,xfd->sxcf/dot_general | solution.py:28
  146.0 1.9 fusion
  147.9 1.6 reshape_transpose_reshape.4
  149.5 1.6 pad_maximum_fusion
  151.1 2.2 reshape.250
  154.9 3.1 %fusion.2 = bf16[32,1,32,1024]{3,2,1,0:T(8,128)(2,1)} fusion(bf16[1024,768,1]{1,0,2:T(8,128)(2,1)S(1)} %copy-done.5, bf16[32,32,384]{2,1,0:T(8,128)(2,1)S(1)} %copy-done.16, bf16[32,32,384]{2,1,0:T(8,128)(2,1)S(1)} %copy-done.14), kind=kOutput, calls=%fused_computation.9 | convolution fusion | flops 1615855616 | bytes 5242880 | tf_op jit(solution)/shard_map/sxcj,xdj->sxcd/dot_general | solution.py:38
  158.1 28.6 %all-to-all-done.1 = bf16[32,1,32,1024]{3,2,1,0:T(8,128)(2,1)} async-done(((bf16[32,1,32,1024]{3,2,1,0:T(8,128)(2,1)}), bf16[32,1,32,1024]{3,2,1,0:T(8,128)(2,1)}, u32[]{:S(2)}, u32[]{:S(2)}) %all-to-all-start.1) | async-done | bytes 2097184 | tf_op jit(solution)/shard_map/all_to_all | solution.py:112
  186.7 6.1 %all-to-all-start.3 = ((bf16[32,1,32,1024]{3,2,1,0:T(8,128)(2,1)}), bf16[32,1,32,1024]{3,2,1,0:T(8,128)(2,1)S(1)}, u32[]{:S(2)}, u32[]{:S(2)}) async-start(bf16[32,1,32,1024]{3,2,1,0:T(8,128)(2,1)} %fusion.2), calls=%async_computation.3 | async-start | bytes 4194304 | tf_op jit(solution)/shard_map/all_to_all | solution.py:132
  193.0 3.4 %convolution_convert_fusion.1 = bf16[128,1024]{1,0:T(8,128)(2,1)} fusion(f32[1024,128]{1,0:T(8,128)S(1)} %bitcast.119, bf16[1024,1024]{1,0:T(8,128)(2,1)} %bitcast.15), kind=kOutput, calls=%fused_computation.32 | convolution fusion | flops 1610743808 | bytes 2883584 | tf_op jit(solution)/shard_map/st,sd->td/dot_general | solution.py:138
  196.4 18.0 %reduce-scatter.2.cloned.1.call-done = bf16[8,9216]{1,0:T(8,128)(2,1)} async-done(((bf16[128,9216]{1,0:T(8,128)(2,1)}), bf16[8,9216]{1,0:T(8,128)(2,1)}) %reduce-scatter.2.cloned.1.call-update) | async-done | bytes 147472 | tf_op jit(solution)/shard_map/reduce_scatter | solution.py:125
  217.8 24.7 %all-to-all-done.3 = bf16[32,1,32,1024]{3,2,1,0:T(8,128)(2,1)S(1)} async-done(((bf16[32,1,32,1024]{3,2,1,0:T(8,128)(2,1)}), bf16[32,1,32,1024]{3,2,1,0:T(8,128)(2,1)S(1)}, u32[]{:S(2)}, u32[]{:S(2)}) %all-to-all-start.3) | async-done | bytes 2097184 | tf_op jit(solution)/shard_map/all_to_all | solution.py:132
  (64 shorter events, 16.9 us)
Async XLA Ops:
  7.2 1.0 copy-start
  10.2 13.4 %copy-start.9 = (bf16[1,24,1024]{2,1,0:T(8,128)(2,1)S(1)}, bf16[1,24,1024]{2,1,0:T(8,128)(2,1)}, u32[]{:S(2)}) copy-start(bf16[1,24,1024]{2,1,0:T(8,128)(2,1)} %param.10) | copy-start | bytes 147460
  10.2 13.5 %copy-start.7 = (bf16[1,64,768]{2,1,0:T(8,128)(2,1)S(1)}, bf16[1,64,768]{2,1,0:T(8,128)(2,1)}, u32[]{:S(2)}) copy-start(bf16[1,64,768]{2,1,0:T(8,128)(2,1)} %param.9) | copy-start | bytes 294916
  10.2 15.0 %copy-start.11 = (s32[128,4]{0,1:T(4,128)S(1)}, s32[128,4]{0,1:T(4,128)}, u32[]{:S(2)}) copy-start(s32[128,4]{0,1:T(4,128)} %param.7) | copy-start | bytes 6148
  10.2 15.0 %copy-start.12 = (f32[128,4]{0,1:T(4,128)S(1)}, f32[128,4]{0,1:T(4,128)}, u32[]{:S(2)}) copy-start(f32[128,4]{0,1:T(4,128)} %param.8) | copy-start | bytes 6148
  10.2 63.4 %all-to-all-start = ((bf16[32,1,32,1024]{3,2,1,0:T(8,128)(2,1)}), bf16[32,1,32,1024]{3,2,1,0:T(8,128)(2,1)S(1)}, u32[]{:S(2)}, u32[]{:S(2)}) async-start(bf16[32,1,32,1024]{3,2,1,0:T(8,128)(2,1)} %convolution_bitcast_fusion), calls=%async_computation | async-start | bytes 4194304 | tf_op jit(solution)/shard_map/all_to_all | solution.py:103
  23.5 2.7 %copy-start.8 = (bf16[128,1024]{1,0:T(8,128)(2,1)S(1)}, bf16[128,1024]{1,0:T(8,128)(2,1)}, u32[]{:S(2)}) copy-start(bf16[128,1024]{1,0:T(8,128)(2,1)} %param.11) | copy-start | bytes 786436
  23.5 57.5 %all-gather.3.cloned.1.call-start = ((), (), s32[]{:S(2)}) async-start(), calls=%async_computation.6 | async-start | bytes 5013504 | tf_op jit(solution)/shard_map/all_gather | solution.py:79
  73.6 1.3 copy-start.2
  74.9 55.9 %all-to-all-start.2 = ((bf16[32,1,32,1024]{3,2,1,0:T(8,128)(2,1)}), bf16[32,1,32,1024]{3,2,1,0:T(8,128)(2,1)S(1)}, u32[]{:S(2)}, u32[]{:S(2)}) async-start(bf16[32,1,32,1024]{3,2,1,0:T(8,128)(2,1)} %bitcast.117), calls=%async_computation.2 | async-start | bytes 4194304 | tf_op jit(solution)/shard_map/all_to_all | solution.py:106
  95.3 1.7 copy-start.1
  95.3 1.7 copy-start.6
  130.8 55.9 %all-to-all-start.1 = ((bf16[32,1,32,1024]{3,2,1,0:T(8,128)(2,1)}), bf16[32,1,32,1024]{3,2,1,0:T(8,128)(2,1)}, u32[]{:S(2)}, u32[]{:S(2)}) async-start(bf16[32,1,32,1024]{3,2,1,0:T(8,128)(2,1)} %bitcast.118), calls=%async_computation.1 | async-start | bytes 4194304 | tf_op jit(solution)/shard_map/all_to_all | solution.py:112
  137.1 77.3 %reduce-scatter.2.cloned.1.call-start = ((), (), s32[]{:S(2)}) async-start(), calls=%async_computation.5 | async-start | bytes 2506752 | tf_op jit(solution)/shard_map/reduce_scatter | solution.py:125
  140.7 5.3 %copy-start.3 = (bf16[32,1,32,1024]{3,2,1,0:T(8,128)(2,1)S(1)}, bf16[32,1,32,1024]{3,2,1,0:T(8,128)(2,1)}, u32[]{:S(2)}) copy-start(bf16[32,1,32,1024]{3,2,1,0:T(8,128)(2,1)} %copy-done.2) | copy-start | bytes 6291460
  144.8 1.0 copy-start.13
  144.8 1.2 copy-start.15
  151.1 2.3 copy-start.16
  153.3 1.4 copy-start.5
  153.3 1.6 copy-start.14
  158.1 34.9 %copy-start.4 = (f32[32,32,128]{2,1,0:T(8,128)S(1)}, f32[32,32,128]{2,1,0:T(8,128)}, u32[]{:S(2)}) copy-start(f32[32,32,128]{2,1,0:T(8,128)} %get-tuple-element.19) | copy-start | bytes 1572868
  186.7 55.8 %all-to-all-start.3 = ((bf16[32,1,32,1024]{3,2,1,0:T(8,128)(2,1)}), bf16[32,1,32,1024]{3,2,1,0:T(8,128)(2,1)S(1)}, u32[]{:S(2)}, u32[]{:S(2)}) async-start(bf16[32,1,32,1024]{3,2,1,0:T(8,128)(2,1)} %fusion.2), calls=%async_computation.3 | async-start | bytes 4194304 | tf_op jit(solution)/shard_map/all_to_all | solution.py:132
  192.9 23.6 %copy-start.10 = (bf16[1,24,1024]{2,1,0:T(8,128)(2,1)S(1)}, bf16[1,24,1024]{2,1,0:T(8,128)(2,1)}, u32[]{:S(2)}) copy-start(bf16[1,24,1024]{2,1,0:T(8,128)(2,1)} %param.10) | copy-start | bytes 147460
Sparse Core Ops, SparseCore 0:
  26.5 45.2 all-gather.2
  153.5 60.8 reduce-scatter.1
